TPU v7x, 512 devices: a whole 4x8x8 slice. The times are simulated.
512 devices in a mesh: wide: 32 (over z, x), tensor: 16 (over y, core).
Axes of the slice: x: 4, y: 8, z: 8, core: 2. Of those that a mesh axis runs over, the one named last changes fastest.
Arguments:
- tokens: bfloat16 [16384, 8192], P('wide', 'tensor'), may hold values from -6 to 6
- key_value_weight: bfloat16 [8192, 2048], P(None, 'tensor'), may hold values from -0.0625 to 0.0625
- adapter_down_maps: bfloat16 [8192, 512, 64], P('tensor', 'wide'), may hold values from -0.0625 to 0.0625
- adapter_up_maps: bfloat16 [512, 64, 2048], P('wide', None, 'tensor'), may hold values from -0.75 to 0.75
- adapter_per_row: int32 [16384], P('wide'), may hold values from 0 to 511, as said below
- adapter_storage_slot: int32 [512], replicated, may hold values from 0 to 511, as said below
Outputs:
- kv_out: bfloat16 [16384, 2048], P('wide', 'tensor')
Inputs may be any that keep to these rules, and one draw needn't show every extreme that they name: `adapter_per_row`: the adapter stored at position p belongs to owner p // 16 of wide. Among the 512 rows of one index of wide, at most 32 name adapters of one owner; in every draw one owner gets exactly 32 rows from every index of wide. `adapter_storage_slot`: each position is taken by exactly one adapter.
All inputs are finite; a program needn't handle non-finite values.
Results may differ from a plain program's by a relative error of at most 0.0049.
Values may be sent and summed in bfloat16 or wider, within the bound.
No kernel may reach another device: no remote copies, remote signals or barrier semaphores. Data moves between devices by JAX's collectives and lax.ppermute only.
A program may use at most 64 MiB of HBM per device.

v0:
```python
import jax
import jax.numpy as jnp
from jax import lax
from jax.sharding import PartitionSpec as P


def body(
    tokens,
    key_value_weight,
    adapter_down_maps,
    adapter_up_maps,
    adapter_per_row,
    adapter_storage_slot,
):
    row_count = tokens.shape[0]
    feature_portion = tokens.shape[1]
    wide_count = lax.axis_size("wide")
    capacity = 2 * row_count // wide_count
    present_adapters = adapter_down_maps.shape[1]
    rank_dimension = adapter_down_maps.shape[2]
    column_portion = key_value_weight.shape[1]
    gathered = lax.all_gather(tokens, "tensor", axis=1, tiled=True)
    base_projection_output = jnp.dot(gathered, key_value_weight, preferred_element_type=jnp.float32)
    total_adapters = adapter_storage_slot.shape[0]
    adapter_match = adapter_per_row[:, None] == jnp.arange(total_adapters, dtype=jnp.int32)[None, :]
    storage_position = jnp.sum(jnp.where(adapter_match, adapter_storage_slot[None, :], 0), axis=1)
    owner_index = storage_position // present_adapters
    local_index = storage_position % present_adapters
    owner_onehot = (
        owner_index[:, None] == jnp.arange(wide_count, dtype=jnp.int32)[None, :]
    ).astype(jnp.int32)
    earlier = jnp.cumsum(owner_onehot, axis=0) - owner_onehot
    rank_in_owner = jnp.sum(earlier * owner_onehot, axis=1)
    storage_slot_index = owner_index * capacity + rank_in_owner
    send_rows = (
        jnp.zeros((wide_count * capacity, feature_portion), jnp.bfloat16)
        .at[storage_slot_index]
        .set(tokens)
    )
    send_slots = (
        jnp.full((wide_count * capacity,), -1, jnp.int32).at[storage_slot_index].set(local_index)
    )
    send_rows = send_rows.reshape(wide_count, capacity, feature_portion)
    send_slots = send_slots.reshape(wide_count, capacity)
    down_matrix = adapter_down_maps.reshape(feature_portion, present_adapters * rank_dimension)
    up_matrix = adapter_up_maps.reshape(present_adapters * rank_dimension, column_portion)
    column_adapter = (
        jnp.arange(present_adapters * rank_dimension, dtype=jnp.int32) // rank_dimension
    )
    got_rows = lax.all_to_all(send_rows, "wide", split_axis=0, concat_axis=0, tiled=True)
    got_slots = lax.all_to_all(send_slots, "wide", split_axis=0, concat_axis=0, tiled=True)
    source_rows, entry_list = got_slots.shape
    flat_rows = got_rows.reshape(source_rows * entry_list, feature_portion)
    slot_adapter = got_slots.reshape(source_rows * entry_list)
    all_ranks = jnp.dot(flat_rows, down_matrix, preferred_element_type=jnp.float32)
    selected = slot_adapter[:, None] == column_adapter[None, :]
    partial_value = jnp.sum(
        jnp.where(selected, all_ranks, 0.0).reshape(
            source_rows * entry_list, present_adapters, rank_dimension
        ),
        axis=1,
    )
    summed = lax.psum(partial_value, "tensor")
    reduced_rows = summed.astype(jnp.bfloat16)
    expanded_rows = jnp.where(
        selected, jnp.tile(reduced_rows, (1, present_adapters)), jnp.zeros((), jnp.bfloat16)
    )
    adapter_correction = jnp.dot(
        expanded_rows, up_matrix, preferred_element_type=jnp.float32
    ).astype(jnp.bfloat16)
    adapter_correction = adapter_correction.reshape(source_rows, entry_list, column_portion)
    returned_rows = lax.all_to_all(
        adapter_correction, "wide", split_axis=0, concat_axis=0, tiled=True
    )
    returned_rows = returned_rows.reshape(wide_count * capacity, column_portion)
    adapter_row_output = returned_rows[storage_slot_index]
    return (base_projection_output + adapter_row_output.astype(jnp.float32)).astype(jnp.bfloat16)


def solution(mesh):
    in_specs = (
        P("wide", "tensor"),
        P(None, "tensor"),
        P("tensor", "wide", None),
        P("wide", None, "tensor"),
        P("wide"),
        P(),
    )
    out_specs = P("wide", "tensor")
    return jax.shard_map(body, mesh=mesh, in_specs=in_specs, out_specs=out_specs, check_vma=False)
```

profile of v0, /device:TPU:24, one launch (start us, length us, event | category | flops | bytes accessed | tf_op | source)
XLA Modules:
  0.0 157.6 jit_solution(14151198750834206589)
XLA Ops:
  6.5 0.0 copy-start
  6.5 0.0 all-gather.2.cloned.1.call-start
  6.5 0.7 all-gather.2.cloned.1.call-update
  7.3 0.9 select_reduce_fusion
  8.2 1.2 reduce-window.6
  9.4 0.2 slice_reduce_fusion
  9.7 0.1 fusion.12
  9.8 2.4 %scatter_custom_fusion = s32[1024]{0:T(1024)S(1)} fusion(s32[512]{0:T(512)S(1)} %bitcast.57, s32[512]{0:T(512)S(1)} %get-tuple-element.5, s32[]{:T(128)} %constant.50.clone.1), kind=kCustom, calls=%fused_computation.59 | custom fusion | bytes 4100 | tf_op jit(solution)/shard_map/scatter | solution.py:41
  12.3 0.7 all_to_all.12
  13.0 13.2 %all-to-all-start = ((s32[32,1,32]{2,1,0:T(1,128)}), s32[32,1,32]{2,1,0:T(1,128)S(1)}, u32[]{:S(2)}, u32[]{:S(2)}) async-start(s32[32,1,32]{2,1,0:T(1,128)} %all_to_all.12), calls=%async_computation | async-start | bytes 32768 | tf_op jit(solution)/shard_map/all_to_all | solution.py:51
  26.1 4.1 %scatter_custom_fusion.1 = bf16[1024,512]{1,0:T(8,128)(2,1)} fusion(s32[512]{0:T(512)S(1)} %bitcast.58, bf16[512,512]{1,0:T(8,128)(2,1)} %param.6, bf16[]{:T(256)} %constant.61.clone.1), kind=kCustom, calls=%fused_computation.16 | custom fusion | bytes 1049088 | tf_op jit(solution)/shard_map/scatter | solution.py:38
  30.2 5.6 %all-to-all-done = s32[32,1,32]{2,1,0:T(1,128)S(1)} async-done(((s32[32,1,32]{2,1,0:T(1,128)}), s32[32,1,32]{2,1,0:T(1,128)S(1)}, u32[]{:S(2)}, u32[]{:S(2)}) %all-to-all-start) | async-done | bytes 4128 | tf_op jit(solution)/shard_map/all_to_all | solution.py:51
  35.8 4.2 %all-to-all-start.1 = ((bf16[32,32,512]{2,1,0:T(8,128)(2,1)}), bf16[32,32,512]{2,1,0:T(8,128)(2,1)S(1)}, u32[]{:S(2)}, u32[]{:S(2)}) async-start(bf16[32,32,512]{2,1,0:T(8,128)(2,1)} %bitcast.5), calls=%async_computation.1 | async-start | bytes 2097152 | tf_op jit(solution)/shard_map/all_to_all | solution.py:50
  40.0 0.5 broadcast.228
  40.5 0.7 reduce.5
  41.2 0.1 eq.71
  41.3 26.2 %all-to-all-done.1 = bf16[32,32,512]{2,1,0:T(8,128)(2,1)S(1)} async-done(((bf16[32,32,512]{2,1,0:T(8,128)(2,1)}), bf16[32,32,512]{2,1,0:T(8,128)(2,1)S(1)}, u32[]{:S(2)}, u32[]{:S(2)}) %all-to-all-start.1) | async-done | bytes 1048608 | tf_op jit(solution)/shard_map/all_to_all | solution.py:50
  67.5 4.5 %compare_select_fusion = f32[1024,1024]{0,1:T(8,128)} fusion(bf16[1024,512]{1,0:T(8,128)(2,1)S(1)} %bitcast.55, bf16[512,1024]{0,1:T(8,128)(2,1)} %bitcast.61, s32[1024]{0:T(1024)S(1)} %eq.71, s32[1024]{0:T(1024)S(1)} %add_select_fusion.1), kind=kOutput, calls=%fused_computation.3 | convolution fusion | flops 1075838976 | bytes 6299648 | tf_op jit(solution)/shard_map/dot_general | solution.py:55
  71.9 0.0 copy-start.1
  72.0 2.5 %reduce_sum.38 = f32[1024,64]{0,1:T(8,128)S(1)} reduce(f32[1024,16,64]{0,2,1:T(8,128)} %bitcast.54, f32[]{:T(128)} %constant.62.clone.1), dimensions={1}, to_apply=%region_6.7 | reduce | flops 983040 | bytes 4456452 | tf_op jit(solution)/shard_map/reduce_sum | solution.py:57
  74.5 47.2 %all-reduce.1 = bf16[1024,64]{0,1:T(8,128)(2,1)S(1)} all-reduce(f32[1024,64]{0,1:T(8,128)S(1)} %reduce_sum.38), channel_id=1, replica_groups=mesh['wide'=32,'tensor'=16] {'tensor'}, use_global_device_ids=true, to_apply=%region_7.8 | all-reduce | flops 65536 | bytes 393216 | tf_op jit(solution)/shard_map/psum | solution.py:63
  121.7 0.0 copy-done.1
  121.7 1.7 %fusion.4 = bf16[1024,128]{1,0:T(8,128)(2,1)} fusion(bf16[16,64,128]{2,1,0:T(8,128)(2,1)S(1)} %copy-done.1, s32[16,64]{1,0:T(8,128)S(1)} %add_select_fusion, s32[1024]{0:T(1024)S(1)} %eq.71, bf16[1024,64]{0,1:T(8,128)(2,1)S(1)} %all-reduce.1), kind=kOutput, calls=%fused_computation.9 | convolution fusion | flops 270663680 | bytes 663552 | tf_op jit(solution)/shard_map/dot_general | solution.py:68
  123.4 5.7 %all-to-all-start.2 = ((bf16[32,32,128]{2,1,0:T(8,128)(2,1)}), bf16[32,32,128]{2,1,0:T(8,128)(2,1)S(1)}, u32[]{:S(2)}, u32[]{:S(2)}) async-start(bf16[32,32,128]{2,1,0:T(8,128)(2,1)} %bitcast.10), calls=%async_computation.2 | async-start | bytes 524288 | tf_op jit(solution)/shard_map/all_to_all | solution.py:72
  129.1 13.9 %all-to-all-done.2 = bf16[32,32,128]{2,1,0:T(8,128)(2,1)S(1)} async-done(((bf16[32,32,128]{2,1,0:T(8,128)(2,1)}), bf16[32,32,128]{2,1,0:T(8,128)(2,1)S(1)}, u32[]{:S(2)}, u32[]{:S(2)}) %all-to-all-start.2) | async-done | bytes 262176 | tf_op jit(solution)/shard_map/all_to_all | solution.py:72
  143.0 1.3 gather_fusion
  144.3 0.0 all-gather.2.cloned.1.call-done
  144.4 0.0 copy-done
  144.4 6.4 %fusion.5 = bf16[512,128]{1,0:T(8,128)(2,1)} fusion(bf16[512,8192]{1,0:T(8,128)(2,1)} %all-gather.2.cloned.1.call-done, bf16[8192,128]{1,0:T(8,128)(2,1)S(1)} %copy-done, bf16[512,128]{1,0:T(8,128)(2,1)S(1)} %gather_fusion), kind=kOutput, calls=%fused_computation.11 | convolution fusion | flops 1073938432 | bytes 10747904 | tf_op jit(solution)/shard_map/dot_general | solution.py:23
  (9 shorter events, 0.1 us)
Async XLA Ops:
  6.5 137.8 %copy-start = (bf16[8192,128]{1,0:T(8,128)(2,1)S(1)}, bf16[8192,128]{1,0:T(8,128)(2,1)}, u32[]{:S(2)}) copy-start(bf16[8192,128]{1,0:T(8,128)(2,1)} %param.7) | copy-start | bytes 6291460
  6.5 137.8 %all-gather.2.cloned.1.call-start = ((), (), s32[]{:S(2)}) async-start(), calls=%async_computation.3 | async-start | bytes 8912896 | tf_op jit(solution)/shard_map/all_gather | solution.py:22
  13.0 22.8 %all-to-all-start = ((s32[32,1,32]{2,1,0:T(1,128)}), s32[32,1,32]{2,1,0:T(1,128)S(1)}, u32[]{:S(2)}, u32[]{:S(2)}) async-start(s32[32,1,32]{2,1,0:T(1,128)} %all_to_all.12), calls=%async_computation | async-start | bytes 32768 | tf_op jit(solution)/shard_map/all_to_all | solution.py:51
  35.8 31.7 %all-to-all-start.1 = ((bf16[32,32,512]{2,1,0:T(8,128)(2,1)}), bf16[32,32,512]{2,1,0:T(8,128)(2,1)S(1)}, u32[]{:S(2)}, u32[]{:S(2)}) async-start(bf16[32,32,512]{2,1,0:T(8,128)(2,1)} %bitcast.5), calls=%async_computation.1 | async-start | bytes 2097152 | tf_op jit(solution)/shard_map/all_to_all | solution.py:50
  71.9 49.7 %copy-start.1 = (bf16[16,64,128]{2,1,0:T(8,128)(2,1)S(1)}, bf16[16,64,128]{2,1,0:T(8,128)(2,1)}, u32[]{:S(2)}) copy-start(bf16[16,64,128]{2,1,0:T(8,128)(2,1)} %param.9) | copy-start | bytes 786436
  123.4 19.6 %all-to-all-start.2 = ((bf16[32,32,128]{2,1,0:T(8,128)(2,1)}), bf16[32,32,128]{2,1,0:T(8,128)(2,1)S(1)}, u32[]{:S(2)}, u32[]{:S(2)}) async-start(bf16[32,32,128]{2,1,0:T(8,128)(2,1)} %bitcast.10), calls=%async_computation.2 | async-start | bytes 524288 | tf_op jit(solution)/shard_map/all_to_all | solution.py:72
Sparse Core Ops, SparseCore 0:
  9.5 62.3 all-gather.1
where the time goes:
time: 158 us
  blocking collectives  47.2 us (30%)
  waiting for transfers between devices  46.4 us (29%)
  starting transfers between devices  23 us (15%)
  between operations  13.5 us (9%)
  matrix products  12.6 us (8%)
  local copies, waits for them, and re-layouts  9.34 us (6%)
  other arithmetic  5.53 us (4%)
    psum x1, blocking collectives, body(): summed = lax.psum(partial_value, 'tensor')  47.2 us
    all_to_all x1, waiting for transfers between devices, body(): lax.all_to_all(send_rows, 'wide', split_axis=0, concat_axis=0, tiled=True)  26.2 us
    all_to_all x1, waiting for transfers between devices, body(): lax.all_to_all(adapter_correction, 'wide', split_axis=0, concat_axis=0, t...  13.9 us
    all_to_all x1, starting transfers between devices, body(): lax.all_to_all(send_slots, 'wide', split_axis=0, concat_axis=0, tiled=True)  13.2 us
    dot_general x1, matrix products, body(): jnp.dot(gathered, key_value_weight, preferred_element_type=jnp.float32)  6.39 us
    all_to_all x1, starting transfers between devices, body(): lax.all_to_all(adapter_correction, 'wide', split_axis=0, concat_axis=0, t...  5.67 us
    all_to_all x1, waiting for transfers between devices, body(): lax.all_to_all(send_slots, 'wide', split_axis=0, concat_axis=0, tiled=True)  5.61 us
    dot_general x1, matrix products, body(): jnp.dot(flat_rows, down_matrix, preferred_element_type=jnp.float32)  4.49 us
  transfers between devices with their start and end apart: 4, of which 3 were waited for; matrix products, arithmetic and copies ran while one was open for 13% of the time, Pallas kernels for 0%

commit v1 on v0

v1 whole, which is shorter than its diff:
```python
import jax
import jax.numpy as jnp
from jax import lax
from jax.sharding import PartitionSpec as P


def body(
    tokens,
    key_value_weight,
    adapter_down_maps,
    adapter_up_maps,
    adapter_per_row,
    adapter_storage_slot,
):
    row_count, feature_portion = tokens.shape
    wide_count = lax.axis_size("wide")
    capacity = 2 * row_count // wide_count
    present_adapters = adapter_down_maps.shape[1]
    rank_dimension = adapter_down_maps.shape[2]
    column_portion = key_value_weight.shape[1]
    total_adapters = adapter_storage_slot.shape[0]
    slot_count = wide_count * capacity
    lane = 128

    gathered = lax.all_gather(tokens, "tensor", axis=1, tiled=True)
    base_projection_output = jnp.dot(
        gathered, key_value_weight, preferred_element_type=jnp.float32
    )

    storage_position = jnp.take(adapter_storage_slot, adapter_per_row, axis=0)
    owner_index = storage_position // present_adapters
    local_index = storage_position % present_adapters

    owner_onehot = (
        owner_index[:, None] == jnp.arange(wide_count, dtype=jnp.int32)[None, :]
    ).astype(jnp.float32)
    row_iota = jnp.arange(row_count, dtype=jnp.int32)
    strictly_before = (row_iota[:, None] > row_iota[None, :]).astype(jnp.float32)
    earlier = jnp.dot(strictly_before, owner_onehot, preferred_element_type=jnp.float32)
    rank_in_owner = jnp.sum(earlier * owner_onehot, axis=1).astype(jnp.int32)
    destination = owner_index * capacity + rank_in_owner

    placement = (
        jnp.arange(slot_count, dtype=jnp.int32)[:, None] == destination[None, :]
    ).astype(jnp.bfloat16)

    local_onehot = (
        local_index[:, None] == jnp.arange(lane, dtype=jnp.int32)[None, :]
    ).astype(jnp.bfloat16)
    extended = jnp.concatenate([tokens, local_onehot], axis=1)
    send_rows = jnp.dot(placement, extended, preferred_element_type=jnp.float32).astype(
        jnp.bfloat16
    )
    send_rows = send_rows.reshape(wide_count, capacity, feature_portion + lane)

    got_rows = lax.all_to_all(send_rows, "wide", split_axis=0, concat_axis=0, tiled=True)
    got_rows = got_rows.reshape(slot_count, feature_portion + lane)
    flat_rows = got_rows[:, :feature_portion]
    got_onehot = got_rows[:, feature_portion : feature_portion + present_adapters]

    down_matrix = adapter_down_maps.reshape(feature_portion, present_adapters * rank_dimension)
    all_ranks = jnp.dot(flat_rows, down_matrix, preferred_element_type=jnp.float32)
    all_ranks = all_ranks.reshape(slot_count, present_adapters, rank_dimension)
    selected = got_onehot[:, :, None] > 0
    partial_value = jnp.sum(jnp.where(selected, all_ranks, 0.0), axis=1)
    summed = partial_value
    tensor_count = lax.axis_size("tensor")
    step = 1
    while step < tensor_count:
        exchange = [(i, i ^ step) for i in range(tensor_count)]
        summed = summed + lax.ppermute(summed, "tensor", exchange)
        step *= 2
    reduced_rows = summed.astype(jnp.bfloat16)

    expanded_rows = jnp.where(
        selected, reduced_rows[:, None, :], jnp.zeros((), jnp.bfloat16)
    ).reshape(slot_count, present_adapters * rank_dimension)
    up_matrix = adapter_up_maps.reshape(present_adapters * rank_dimension, column_portion)
    adapter_correction = jnp.dot(
        expanded_rows, up_matrix, preferred_element_type=jnp.float32
    ).astype(jnp.bfloat16)
    adapter_correction = adapter_correction.reshape(wide_count, capacity, column_portion)
    returned_rows = lax.all_to_all(
        adapter_correction, "wide", split_axis=0, concat_axis=0, tiled=True
    )
    returned_rows = returned_rows.reshape(slot_count, column_portion)
    adapter_row_output = jnp.dot(
        placement.T, returned_rows, preferred_element_type=jnp.float32
    )
    return (base_projection_output + adapter_row_output).astype(jnp.bfloat16)


def solution(mesh):
    in_specs = (
        P("wide", "tensor"),
        P(None, "tensor"),
        P("tensor", "wide", None),
        P("wide", None, "tensor"),
        P("wide"),
        P(),
    )
    out_specs = P("wide", "tensor")
    return jax.shard_map(body, mesh=mesh, in_specs=in_specs, out_specs=out_specs, check_vma=False)
```

time: 158 us -> 144 us (0.911)
  the two profiles are of different devices: /device:TPU:24 before, /device:TPU:1 now
where the time goes in v1:
time: 144 us; the launch traced here: 143 us
  blocking collectives  47.3 us (33%)
  waiting for transfers between devices  37 us (26%)
  starting transfers between devices  26.3 us (18%)
  between operations  13.5 us (9%)
  matrix products  12.5 us (9%)
  local copies, waits for them, and re-layouts  5.43 us (4%)
    all_to_all x1, blocking collectives, body(): lax.all_to_all(send_rows, 'wide', split_axis=0, concat_axis=0, tiled=True)  47.3 us
    ppermute x4, waiting for transfers between devices, body(): summed = summed + lax.ppermute(summed, 'tensor', exchange)  30.6 us
    ppermute x4, starting transfers between devices, body(): summed = summed + lax.ppermute(summed, 'tensor', exchange)  20.3 us
    all_to_all x1, starting transfers between devices, body(): lax.all_to_all(adapter_correction, 'wide', split_axis=0, concat_axis=0, t...  5.99 us
    all_to_all x1, waiting for transfers between devices, body(): lax.all_to_all(adapter_correction, 'wide', split_axis=0, concat_axis=0, t...  5.74 us
    dot_general x1, matrix products, body(): jnp.dot(gathered, key_value_weight, preferred_element_type=jnp.float32)  5.7 us
    gather x1, local copies, waits for them, and re-layouts, body(): storage_position = jnp.take(adapter_storage_slot, adapter_per_row, axis=0)  3.62 us
  transfers between devices with their start and end apart: 6, of which 5 were waited for; matrix products, arithmetic and copies ran while one was open for 12% of the time, Pallas kernels for 0%

profile of v1, /device:TPU:1, one launch (start us, length us, event | category | flops | bytes accessed | tf_op | source)
XLA Modules:
  0.0 143.1 jit_solution(4312614742262830336)
XLA Ops:
  6.5 0.0 copy-start
  6.5 0.0 copy-start.1
  6.5 0.0 all-gather.2.cloned.1.call-start
  6.5 0.7 all-gather.2.cloned.1.call-update
  7.3 0.7 compare_select_fusion
  8.0 3.6 %gather_fusion = s32[512]{0:T(512)S(1)} fusion(s32[512]{0:T(512)} %param.11, s32[1024]{0:T(1024)S(1)} %pad_clamp_fusion), kind=kCustom, calls=%fused_computation | custom fusion | bytes 6144 | tf_op jit(solution)/shard_map/jit(_take)/gather | solution.py:30
  11.6 0.0 copy-done.2
  11.6 0.3 fusion.14
  11.9 0.1 fusion.23
  12.1 0.0 copy-done.1
  12.1 1.0 fusion.5
  13.1 47.3 %all_to_all.10 = bf16[32,32,640]{2,1,0:T(8,128)(2,1)S(1)} all-to-all(bf16[32,32,640]{2,1,0:T(8,128)(2,1)S(1)} %bitcast.24), channel_id=1, replica_groups=mesh['wide'=32,'tensor'=16] {'wide'}, dimensions={0} | all-to-all | bytes 2621440 | tf_op jit(solution)/shard_map/all_to_all | solution.py:56
  60.4 0.7 slice.10
  61.2 1.1 copy.12
  62.3 2.6 %select_reduce_fusion = f32[1024,64]{0,1:T(8,128)S(1)} fusion(pred[1024,16]{0,1:T(8,128)(4,1)S(1)} %broadcast_compare_fusion, bf16[1024,640]{1,0:T(8,128)(2,1)S(1)} %bitcast.23, bf16[512,16,64]{0,2,1:T(8,128)(2,1)} %param.8), kind=kOutput, calls=%fused_computation.1 | convolution fusion | flops 1075773440 | bytes 2375680 | tf_op jit(solution)/shard_map/dot_general | solution.py:62
  64.8 0.0 copy-start.3
  64.8 4.4 %collective-permute-start = (f32[1024,64]{0,1:T(8,128)S(1)}, f32[1024,64]{0,1:T(8,128)S(1)}, u32[]{:S(2)}, u32[]{:S(2)}) collective-permute-start(f32[1024,64]{0,1:T(8,128)S(1)} %select_reduce_fusion), channel_id=1, source_target_pairs={{0,1},{1,0},{2,3},{3,2},{4,5},{5,4},{6,7},{7,6},{8,9},{9,8},{10,11... | collective-permute-start | bytes 786440 | tf_op jit(solution)/shard_map/ppermute | solution.py:71
  69.3 1.2 collective-permute-done
  70.5 3.2 %collective-permute-start.1 = (f32[1024,64]{0,1:T(8,128)S(1)}, f32[1024,64]{0,1:T(8,128)S(1)}, u32[]{:S(2)}, u32[]{:S(2)}) collective-permute-start(f32[1024,64]{0,1:T(8,128)S(1)} %add.45), channel_id=1, source_target_pairs={{0,2},{1,3},{2,0},{3,1},{4,6},{5,7},{6,4},{7,5},{8,10},{9,11},{10,... | collective-permute-start | bytes 786440 | tf_op jit(solution)/shard_map/ppermute | solution.py:71
  73.7 6.2 %collective-permute-done.1 = f32[1024,64]{0,1:T(8,128)S(1)} collective-permute-done((f32[1024,64]{0,1:T(8,128)S(1)}, f32[1024,64]{0,1:T(8,128)S(1)}, u32[]{:S(2)}, u32[]{:S(2)}) %collective-permute-start.1) | collective-permute-done | bytes 262176 | tf_op jit(solution)/shard_map/ppermute | solution.py:71
  80.0 4.2 %collective-permute-start.2 = (f32[1024,64]{0,1:T(8,128)S(1)}, f32[1024,64]{0,1:T(8,128)S(1)}, u32[]{:S(2)}, u32[]{:S(2)}) collective-permute-start(f32[1024,64]{0,1:T(8,128)S(1)} %add.46), channel_id=1, source_target_pairs={{0,4},{1,5},{2,6},{3,7},{4,0},{5,1},{6,2},{7,3},{8,12},{9,13},{10,... | collective-permute-start | bytes 786440 | tf_op jit(solution)/shard_map/ppermute | solution.py:71
  84.2 11.4 %collective-permute-done.2 = f32[1024,64]{0,1:T(8,128)S(1)} collective-permute-done((f32[1024,64]{0,1:T(8,128)S(1)}, f32[1024,64]{0,1:T(8,128)S(1)}, u32[]{:S(2)}, u32[]{:S(2)}) %collective-permute-start.2) | collective-permute-done | bytes 262176 | tf_op jit(solution)/shard_map/ppermute | solution.py:71
  95.6 8.5 %collective-permute-start.3 = (f32[1024,64]{0,1:T(8,128)S(1)}, f32[1024,64]{0,1:T(8,128)S(1)}, u32[]{:S(2)}, u32[]{:S(2)}) collective-permute-start(f32[1024,64]{0,1:T(8,128)S(1)} %add.47), channel_id=1, source_target_pairs={{0,8},{1,9},{2,10},{3,11},{4,12},{5,13},{6,14},{7,15},{8,0},{9,1},... | collective-permute-start | bytes 786440 | tf_op jit(solution)/shard_map/ppermute | solution.py:71
  104.1 11.7 %collective-permute-done.3 = f32[1024,64]{0,1:T(8,128)S(1)} collective-permute-done((f32[1024,64]{0,1:T(8,128)S(1)}, f32[1024,64]{0,1:T(8,128)S(1)}, u32[]{:S(2)}, u32[]{:S(2)}) %collective-permute-start.3) | collective-permute-done | bytes 262176 | tf_op jit(solution)/shard_map/ppermute | solution.py:71
  115.9 0.0 copy-done.3
  115.9 1.5 %fusion.9 = bf16[1024,128]{1,0:T(8,128)(2,1)} fusion(bf16[16,64,128]{2,1,0:T(8,128)(2,1)S(1)} %copy-done.3, pred[1024,16]{0,1:T(8,128)(4,1)S(1)} %broadcast_compare_fusion, bf16[1024,64]{0,1:T(8,128)(2,1)S(1)} %add_convert_fusion), kind=kOutput, calls=%fused_computation.10 | convolution fusion | flops 269615104 | bytes 671744 | tf_op jit(solution)/shard_map/dot_general | solution.py:79
  117.4 6.0 %all-to-all-start.1 = ((bf16[32,32,128]{2,1,0:T(8,128)(2,1)}), bf16[32,32,128]{2,1,0:T(8,128)(2,1)S(1)}, u32[]{:S(2)}, u32[]{:S(2)}) async-start(bf16[32,32,128]{2,1,0:T(8,128)(2,1)} %bitcast.7), calls=%async_computation.1 | async-start | bytes 524288 | tf_op jit(solution)/shard_map/all_to_all | solution.py:83
  123.4 0.0 all-gather.2.cloned.1.call-done
  123.4 0.0 copy-done
  123.5 5.7 %fusion.28 = f32[512,128]{1,0:T(8,128)S(1)} fusion(bf16[512,8192]{1,0:T(8,128)(2,1)} %all-gather.2.cloned.1.call-done, bf16[8192,128]{1,0:T(8,128)(2,1)S(1)} %copy-done), kind=kOutput, calls=%fused_computation.45 | convolution fusion | flops 1073741824 | bytes 10747904 | tf_op jit(solution)/shard_map/dot_general | solution.py:26
  129.2 5.7 %all-to-all-done.1 = bf16[32,32,128]{2,1,0:T(8,128)(2,1)S(1)} async-done(((bf16[32,32,128]{2,1,0:T(8,128)(2,1)}), bf16[32,32,128]{2,1,0:T(8,128)(2,1)S(1)}, u32[]{:S(2)}, u32[]{:S(2)}) %all-to-all-start.1) | async-done | bytes 262176 | tf_op jit(solution)/shard_map/all_to_all | solution.py:83
  134.9 1.4 fusion.13
  (9 shorter events, 0.2 us)
Async XLA Ops:
  6.5 116.9 %copy-start = (bf16[8192,128]{1,0:T(8,128)(2,1)S(1)}, bf16[8192,128]{1,0:T(8,128)(2,1)}, u32[]{:S(2)}) copy-start(bf16[8192,128]{1,0:T(8,128)(2,1)} %param.7) | copy-start | bytes 6291460
  6.5 5.5 %copy-start.1 = (bf16[512,512]{1,0:T(8,128)(2,1)S(1)}, bf16[512,512]{1,0:T(8,128)(2,1)}, u32[]{:S(2)}) copy-start(bf16[512,512]{1,0:T(8,128)(2,1)} %param.6) | copy-start | bytes 1572868
  6.5 5.1 %copy-start.2 = (s32[512]{0:T(512)S(1)}, s32[512]{0:T(512)}, u32[]{:S(2)}) copy-start(s32[512]{0:T(512)} %param.10) | copy-start | bytes 6148
  6.5 116.9 %all-gather.2.cloned.1.call-start = ((), (), s32[]{:S(2)}) async-start(), calls=%async_computation.2 | async-start | bytes 8912896 | tf_op jit(solution)/shard_map/all_gather | solution.py:25
  64.8 51.1 %copy-start.3 = (bf16[16,64,128]{2,1,0:T(8,128)(2,1)S(1)}, bf16[16,64,128]{2,1,0:T(8,128)(2,1)}, u32[]{:S(2)}) copy-start(bf16[16,64,128]{2,1,0:T(8,128)(2,1)} %param.9) | copy-start | bytes 786436
  64.8 5.7 %collective-permute-start = (f32[1024,64]{0,1:T(8,128)S(1)}, f32[1024,64]{0,1:T(8,128)S(1)}, u32[]{:S(2)}, u32[]{:S(2)}) collective-permute-start(f32[1024,64]{0,1:T(8,128)S(1)} %select_reduce_fusion), channel_id=1, source_target_pairs={{0,1},{1,0},{2,3},{3,2},{4,5},{5,4},{6,7},{7,6},{8,9},{9,8},{10,11... | collective-permute-start | bytes 786440 | tf_op jit(solution)/shard_map/ppermute | solution.py:71
  70.5 9.4 %collective-permute-start.1 = (f32[1024,64]{0,1:T(8,128)S(1)}, f32[1024,64]{0,1:T(8,128)S(1)}, u32[]{:S(2)}, u32[]{:S(2)}) collective-permute-start(f32[1024,64]{0,1:T(8,128)S(1)} %add.45), channel_id=1, source_target_pairs={{0,2},{1,3},{2,0},{3,1},{4,6},{5,7},{6,4},{7,5},{8,10},{9,11},{10,... | collective-permute-start | bytes 786440 | tf_op jit(solution)/shard_map/ppermute | solution.py:71
  80.0 15.6 %collective-permute-start.2 = (f32[1024,64]{0,1:T(8,128)S(1)}, f32[1024,64]{0,1:T(8,128)S(1)}, u32[]{:S(2)}, u32[]{:S(2)}) collective-permute-start(f32[1024,64]{0,1:T(8,128)S(1)} %add.46), channel_id=1, source_target_pairs={{0,4},{1,5},{2,6},{3,7},{4,0},{5,1},{6,2},{7,3},{8,12},{9,13},{10,... | collective-permute-start | bytes 786440 | tf_op jit(solution)/shard_map/ppermute | solution.py:71
  95.6 20.3 %collective-permute-start.3 = (f32[1024,64]{0,1:T(8,128)S(1)}, f32[1024,64]{0,1:T(8,128)S(1)}, u32[]{:S(2)}, u32[]{:S(2)}) collective-permute-start(f32[1024,64]{0,1:T(8,128)S(1)} %add.47), channel_id=1, source_target_pairs={{0,8},{1,9},{2,10},{3,11},{4,12},{5,13},{6,14},{7,15},{8,0},{9,1},... | collective-permute-start | bytes 786440 | tf_op jit(solution)/shard_map/ppermute | solution.py:71
  117.4 17.5 %all-to-all-start.1 = ((bf16[32,32,128]{2,1,0:T(8,128)(2,1)}), bf16[32,32,128]{2,1,0:T(8,128)(2,1)S(1)}, u32[]{:S(2)}, u32[]{:S(2)}) async-start(bf16[32,32,128]{2,1,0:T(8,128)(2,1)} %bitcast.7), calls=%async_computation.1 | async-start | bytes 524288 | tf_op jit(solution)/shard_map/all_to_all | solution.py:83
Sparse Core Ops, SparseCore 0:
  9.5 64.1 all-gather.1

commit v2 on v1

--- a/solution.py
+++ b/solution.py
@@ -2,6 +2,34 @@
 import jax.numpy as jnp
 from jax import lax
 from jax.sharding import PartitionSpec as P
+
+
+def tensor_sum(partial_value, tensor_count):
+    position = lax.axis_index("tensor")
+    block = partial_value
+    steps = []
+    step = 1
+    while step < tensor_count:
+        half = block.shape[0] // 2
+        upper = (position // step) % 2
+        low_part = block[:half]
+        high_part = block[half:]
+        keep = jnp.where(upper == 1, high_part, low_part)
+        send = jnp.where(upper == 1, low_part, high_part)
+        exchange = [(i, i ^ step) for i in range(tensor_count)]
+        block = keep + lax.ppermute(send, "tensor", exchange)
+        steps.append((step, upper))
+        step *= 2
+    block = block.astype(jnp.bfloat16)
+    for step, upper in reversed(steps):
+        exchange = [(i, i ^ step) for i in range(tensor_count)]
+        other = lax.ppermute(block, "tensor", exchange)
+        block = jnp.where(
+            upper == 1,
+            jnp.concatenate([other, block], axis=0),
+            jnp.concatenate([block, other], axis=0),
+        )
+    return block
 
 
 def body(
@@ -14,6 +42,7 @@
 ):
     row_count, feature_portion = tokens.shape
     wide_count = lax.axis_size("wide")
+    tensor_count = lax.axis_size("tensor")
     capacity = 2 * row_count // wide_count
     present_adapters = adapter_down_maps.shape[1]
     rank_dimension = adapter_down_maps.shape[2]
@@ -21,13 +50,16 @@
     total_adapters = adapter_storage_slot.shape[0]
     slot_count = wide_count * capacity
     lane = 128
+    row_tiles = capacity * feature_portion // lane
+    info_rows = 8
 
     gathered = lax.all_gather(tokens, "tensor", axis=1, tiled=True)
     base_projection_output = jnp.dot(
         gathered, key_value_weight, preferred_element_type=jnp.float32
     )
 
-    storage_position = jnp.take(adapter_storage_slot, adapter_per_row, axis=0)
+    adapter_match = adapter_per_row[:, None] == jnp.arange(total_adapters, dtype=jnp.int32)[None, :]
+    storage_position = jnp.sum(jnp.where(adapter_match, adapter_storage_slot[None, :], 0), axis=1)
     owner_index = storage_position // present_adapters
     local_index = storage_position % present_adapters
 
@@ -44,33 +76,30 @@
         jnp.arange(slot_count, dtype=jnp.int32)[:, None] == destination[None, :]
     ).astype(jnp.bfloat16)
 
-    local_onehot = (
-        local_index[:, None] == jnp.arange(lane, dtype=jnp.int32)[None, :]
-    ).astype(jnp.bfloat16)
-    extended = jnp.concatenate([tokens, local_onehot], axis=1)
-    send_rows = jnp.dot(placement, extended, preferred_element_type=jnp.float32).astype(
+    local_code = jnp.broadcast_to(
+        (local_index + 1).astype(jnp.bfloat16)[:, None], (row_count, lane)
+    )
+    extended = jnp.concatenate([tokens, local_code], axis=1)
+    placed = jnp.dot(placement, extended, preferred_element_type=jnp.float32).astype(
         jnp.bfloat16
     )
-    send_rows = send_rows.reshape(wide_count, capacity, feature_portion + lane)
+    send_rows = placed[:, :feature_portion].reshape(wide_count, row_tiles, lane)
+    slot_code = placed[:, feature_portion].reshape(wide_count, 1, capacity)
+    slot_code = jnp.pad(slot_code, ((0, 0), (0, info_rows - 1), (0, lane - capacity)))
+    send_block = jnp.concatenate([send_rows, slot_code], axis=1)
 
-    got_rows = lax.all_to_all(send_rows, "wide", split_axis=0, concat_axis=0, tiled=True)
-    got_rows = got_rows.reshape(slot_count, feature_portion + lane)
-    flat_rows = got_rows[:, :feature_portion]
-    got_onehot = got_rows[:, feature_portion : feature_portion + present_adapters]
+    got_block = lax.all_to_all(send_block, "wide", split_axis=0, concat_axis=0, tiled=True)
+    flat_rows = got_block[:, :row_tiles, :].reshape(slot_count, feature_portion)
+    got_code = got_block[:, row_tiles, :capacity].reshape(slot_count).astype(jnp.int32)
+    selected = (
+        got_code[:, None] == jnp.arange(1, present_adapters + 1, dtype=jnp.int32)[None, :]
+    )[:, :, None]
 
     down_matrix = adapter_down_maps.reshape(feature_portion, present_adapters * rank_dimension)
     all_ranks = jnp.dot(flat_rows, down_matrix, preferred_element_type=jnp.float32)
     all_ranks = all_ranks.reshape(slot_count, present_adapters, rank_dimension)
-    selected = got_onehot[:, :, None] > 0
     partial_value = jnp.sum(jnp.where(selected, all_ranks, 0.0), axis=1)
-    summed = partial_value
-    tensor_count = lax.axis_size("tensor")
-    step = 1
-    while step < tensor_count:
-        exchange = [(i, i ^ step) for i in range(tensor_count)]
-        summed = summed + lax.ppermute(summed, "tensor", exchange)
-        step *= 2
-    reduced_rows = summed.astype(jnp.bfloat16)
+    reduced_rows = tensor_sum(partial_value, tensor_count)
 
     expanded_rows = jnp.where(
         selected, reduced_rows[:, None, :], jnp.zeros((), jnp.bfloat16)

time: 144 us -> 146 us (1.014)
  blocking collectives: 47.3 us -> 0 us
  starting transfers between devices: 26.3 us -> 63.5 us
  waiting for transfers between devices: 37 us -> 44.4 us
  other arithmetic: 1.03 us -> 3.18 us
  local copies, waits for them, and re-layouts: 5.43 us -> 6.95 us
    all_to_all x1 -> x0, blocking collectives: 47.3 us -> none  [body(): lax.all_to_all(send_rows, 'wide', split_axis=0, concat_axis=0, tiled=True)]
    all_to_all x0 -> x1, waiting for transfers between devices: none -> 26.8 us  [body(): lax.all_to_all(send_block, 'wide', split_axis=0, concat_axis=0, tiled=True)]
    ppermute x4 -> x8, starting transfers between devices: 20.3 us -> 42.8 us  [the longest x4 22.6 us: tensor_sum(): other = lax.ppermute(block, 'tensor', exchange)]
    ppermute x4 -> x8, waiting for transfers between devices: 30.6 us -> 11.1 us  [the longest x4 5.63 us: tensor_sum(): other = lax.ppermute(block, 'tensor', exchange)]
    all_to_all x0 -> x1, starting transfers between devices: none -> 13.7 us  [body(): lax.all_to_all(send_block, 'wide', split_axis=0, concat_axis=0, tiled=True)]
    gather x1 -> x0, local copies, waits for them, and re-layouts: 3.62 us -> none  [body(): storage_position = jnp.take(adapter_storage_slot, adapter_per_row, axis=0)]
    reshape x0 -> x2, local copies, waits for them, and re-layouts: none -> 3.43 us  [the longest x1 1.73 us: body(): flat_rows = got_block[:, :row_tiles, :].reshape(slot_count, feature_portion)]
    slice x1 -> x4, local copies, waits for them, and re-layouts: 0.74 us -> 2.62 us  [the longest x2 1.43 us: body(): send_rows = placed[:, :feature_portion].reshape(wide_count, row_tiles, lane)]
  transfers between devices with their start and end apart: 6 -> 11, of which waited for: 5 -> 10; matrix products, arithmetic and copies ran while one was open for 12% -> 15% of each run, Pallas kernels for 0% -> 0%
where the time goes in v2:
time: 146 us; the launch traced here: 145 us
  starting transfers between devices  63.5 us (43%)
  waiting for transfers between devices  44.4 us (30%)
  between operations  13.8 us (9%)
  matrix products  13.4 us (9%)
  local copies, waits for them, and re-layouts  6.95 us (5%)
  other arithmetic  3.18 us (2%)
    all_to_all x1, waiting for transfers between devices, body(): lax.all_to_all(send_block, 'wide', split_axis=0, concat_axis=0, tiled=True)  26.8 us
    ppermute x4, starting transfers between devices, tensor_sum(): other = lax.ppermute(block, 'tensor', exchange)  22.6 us
    ppermute x4, starting transfers between devices, tensor_sum(): block = keep + lax.ppermute(send, 'tensor', exchange)  20.2 us
    all_to_all x1, starting transfers between devices, body(): lax.all_to_all(send_block, 'wide', split_axis=0, concat_axis=0, tiled=True)  13.7 us
    all_to_all x1, starting transfers between devices, body(): lax.all_to_all(adapter_correction, 'wide', split_axis=0, concat_axis=0, t...  6.97 us
    all_to_all x1, waiting for transfers between devices, body(): lax.all_to_all(adapter_correction, 'wide', split_axis=0, concat_axis=0, t...  5.84 us
    dot_general x1, matrix products, body(): jnp.dot(gathered, key_value_weight, preferred_element_type=jnp.float32)  5.7 us
    ppermute x4, waiting for transfers between devices, tensor_sum(): other = lax.ppermute(block, 'tensor', exchange)  5.63 us
  transfers between devices with their start and end apart: 11, of which 10 were waited for; matrix products, arithmetic and copies ran while one was open for 15% of the time, Pallas kernels for 0%

profile of v2, /device:TPU:1, one launch (start us, length us, event | category | flops | bytes accessed | tf_op | source)
XLA Modules:
  0.0 145.2 jit_solution(7096211707593905683)
XLA Ops:
  6.5 0.7 all-gather.2.cloned.1.call-update
  7.3 0.9 select_reduce_fusion.1
  8.7 2.0 %fusion.6 = bf16[1024,640]{0,1:T(8,128)(2,1)S(1)} fusion(s32[512]{0:T(512)S(1)} %convert_add_fusion, bf16[512,128]{1,0:T(8,128)(2,1)S(1)} %broadcast_in_dim.39, bf16[512,512]{1,0:T(8,128)(2,1)} %param.6), kind=kOutput, calls=%fused_computation.9 | convolution fusion | flops 673579008 | bytes 1968128 | tf_op jit(solution)/shard_map/dot_general | solution.py:83
  10.8 1.4 copy.10
  12.2 1.7 %reshape.158 = bf16[32,128,128]{2,1,0:T(8,128)(2,1)S(1)} reshape(bf16[1024,512]{1,0:T(8,128)(2,1)} %copy.10) | data formatting | bytes 2097152 | tf_op jit(solution)/shard_map/reshape | solution.py:86
  13.9 1.2 fusion.16
  15.1 13.7 %all-to-all-start = ((bf16[32,136,128]{2,1,0:T(8,128)(2,1)}), bf16[32,136,128]{2,1,0:T(8,128)(2,1)S(1)}, u32[]{:S(2)}, u32[]{:S(2)}) async-start(bf16[32,136,128]{2,1,0:T(8,128)(2,1)} %fusion.16), calls=%async_computation | async-start | bytes 2228224 | tf_op jit(solution)/shard_map/all_to_all | solution.py:91
  29.3 26.8 %all-to-all-done = bf16[32,136,128]{2,1,0:T(8,128)(2,1)S(1)} async-done(((bf16[32,136,128]{2,1,0:T(8,128)(2,1)}), bf16[32,136,128]{2,1,0:T(8,128)(2,1)S(1)}, u32[]{:S(2)}, u32[]{:S(2)}) %all-to-all-start) | async-done | bytes 1114144 | tf_op jit(solution)/shard_map/all_to_all | solution.py:91
  56.9 1.2 slice.51
  58.0 1.7 %reshape.164 = bf16[1024,512,1]{1,0,2:T(8,128)(2,1)S(1)} reshape(bf16[32,128,128]{2,1,0:T(8,128)(2,1)} %slice.51) | data formatting | bytes 2097152 | tf_op jit(solution)/shard_map/reshape | solution.py:92
  59.9 2.5 %select_reduce_fusion = f32[1024,64]{0,1:T(8,128)S(1)} fusion(bf16[1024,512,1]{1,0,2:T(8,128)(2,1)S(1)} %reshape.164, pred[1024,16]{0,1:T(8,128)(4,1)S(1)} %broadcast_compare_fusion, bf16[512,16,64]{0,2,1:T(8,128)(2,1)} %param.8), kind=kOutput, calls=%fused_computation | convolution fusion | flops 1075773440 | bytes 2375680 | tf_op jit(solution)/shard_map/dot_general | solution.py:99
  62.5 5.1 %collective-permute-start = (f32[512,64]{0,1:T(8,128)S(1)}, f32[512,64]{0,1:T(8,128)S(1)}, u32[]{:S(2)}, u32[]{:S(2)}) collective-permute-start(f32[512,64]{0,1:T(8,128)S(1)} %slice_select_fusion), channel_id=1, source_target_pairs={{0,1},{1,0},{2,3},{3,2},{4,5},{5,4},{6,7},{7,6},{8,9},{9,8},{10,11... | collective-permute-start | bytes 393224 | tf_op jit(solution)/shard_map/ppermute | solution.py:20
  67.6 0.9 collective-permute-done
  68.6 3.2 %collective-permute-start.1 = (f32[256,64]{0,1:T(8,128)S(1)}, f32[256,64]{0,1:T(8,128)S(1)}, u32[]{:S(2)}, u32[]{:S(2)}) collective-permute-start(f32[256,64]{0,1:T(8,128)S(1)} %slice_select_fusion.1), channel_id=1, source_target_pairs={{0,2},{1,3},{2,0},{3,1},{4,6},{5,7},{6,4},{7,5},{8,10},{9,11},{10,... | collective-permute-start | bytes 196616 | tf_op jit(solution)/shard_map/ppermute | solution.py:20
  71.8 1.8 %collective-permute-done.1 = f32[256,64]{0,1:T(8,128)S(1)} collective-permute-done((f32[256,64]{0,1:T(8,128)S(1)}, f32[256,64]{0,1:T(8,128)S(1)}, u32[]{:S(2)}, u32[]{:S(2)}) %collective-permute-start.1) | collective-permute-done | bytes 65568 | tf_op jit(solution)/shard_map/ppermute | solution.py:20
  73.6 4.2 %collective-permute-start.2 = (f32[128,64]{0,1:T(8,128)S(1)}, f32[128,64]{0,1:T(8,128)S(1)}, u32[]{:S(2)}, u32[]{:S(2)}) collective-permute-start(f32[128,64]{0,1:T(8,128)S(1)} %slice_select_fusion.3), channel_id=1, source_target_pairs={{0,4},{1,5},{2,6},{3,7},{4,0},{5,1},{6,2},{7,3},{8,12},{9,13},{10,... | collective-permute-start | bytes 98312 | tf_op jit(solution)/shard_map/ppermute | solution.py:20
  77.8 1.4 collective-permute-done.2
  79.3 7.7 %collective-permute-start.3 = (f32[64,64]{0,1:T(8,128)S(1)}, f32[64,64]{0,1:T(8,128)S(1)}, u32[]{:S(2)}, u32[]{:S(2)}) collective-permute-start(f32[64,64]{0,1:T(8,128)S(1)} %slice_select_fusion.2), channel_id=1, source_target_pairs={{0,8},{1,9},{2,10},{3,11},{4,12},{5,13},{6,14},{7,15},{8,0},{9,1},... | collective-permute-start | bytes 49160 | tf_op jit(solution)/shard_map/ppermute | solution.py:20
  87.0 1.4 collective-permute-done.3
  88.5 7.2 %collective-permute-start.4 = (bf16[64,64]{0,1:T(8,128)(2,1)S(1)}, bf16[64,64]{0,1:T(8,128)(2,1)S(1)}, u32[]{:S(2)}, u32[]{:S(2)}) collective-permute-start(bf16[64,64]{0,1:T(8,128)(2,1)S(1)} %add_convert_fusion), channel_id=1, source_target_pairs={{0,8},{1,9},{2,10},{3,11},{4,12},{5,13},{6,14},{7,15},{8,0},{9,1},... | collective-permute-start | bytes 24584 | tf_op jit(solution)/shard_map/ppermute | solution.py:26
  95.7 1.2 collective-permute-done.4
  96.9 3.6 %collective-permute-start.5 = (bf16[128,64]{0,1:T(8,128)(2,1)S(1)}, bf16[128,64]{0,1:T(8,128)(2,1)S(1)}, u32[]{:S(2)}, u32[]{:S(2)}) collective-permute-start(bf16[128,64]{0,1:T(8,128)(2,1)S(1)} %maximum_select_fusion.3), channel_id=1, source_target_pairs={{0,4},{1,5},{2,6},{3,7},{4,0},{5,1},{6,2},{7,3},{8,12},{9,13},{10,... | collective-permute-start | bytes 49160 | tf_op jit(solution)/shard_map/ppermute | solution.py:26
  100.6 1.7 %collective-permute-done.5 = bf16[128,64]{0,1:T(8,128)(2,1)S(1)} collective-permute-done((bf16[128,64]{0,1:T(8,128)(2,1)S(1)}, bf16[128,64]{0,1:T(8,128)(2,1)S(1)}, u32[]{:S(2)}, u32[]{:S(2)}) %collective-permute-start.5) | collective-permute-done | bytes 16416 | tf_op jit(solution)/shard_map/ppermute | solution.py:26
  102.3 2.8 %collective-permute-start.6 = (bf16[256,64]{0,1:T(8,128)(2,1)S(1)}, bf16[256,64]{0,1:T(8,128)(2,1)S(1)}, u32[]{:S(2)}, u32[]{:S(2)}) collective-permute-start(bf16[256,64]{0,1:T(8,128)(2,1)S(1)} %maximum_select_fusion.2), channel_id=1, source_target_pairs={{0,2},{1,3},{2,0},{3,1},{4,6},{5,7},{6,4},{7,5},{8,10},{9,11},{10,... | collective-permute-start | bytes 98312 | tf_op jit(solution)/shard_map/ppermute | solution.py:26
  105.1 1.9 %collective-permute-done.6 = bf16[256,64]{0,1:T(8,128)(2,1)S(1)} collective-permute-done((bf16[256,64]{0,1:T(8,128)(2,1)S(1)}, bf16[256,64]{0,1:T(8,128)(2,1)S(1)}, u32[]{:S(2)}, u32[]{:S(2)}) %collective-permute-start.6) | collective-permute-done | bytes 32800 | tf_op jit(solution)/shard_map/ppermute | solution.py:26
  107.0 9.0 %collective-permute-start.7 = (bf16[512,64]{0,1:T(8,128)(2,1)S(1)}, bf16[512,64]{0,1:T(8,128)(2,1)S(1)}, u32[]{:S(2)}, u32[]{:S(2)}) collective-permute-start(bf16[512,64]{0,1:T(8,128)(2,1)S(1)} %maximum_select_fusion.1), channel_id=1, source_target_pairs={{0,1},{1,0},{2,3},{3,2},{4,5},{5,4},{6,7},{7,6},{8,9},{9,8},{10,11... | collective-permute-start | bytes 196616 | tf_op jit(solution)/shard_map/ppermute | solution.py:26
  116.0 0.9 collective-permute-done.7
  116.9 1.5 %fusion.10 = bf16[1024,128]{1,0:T(8,128)(2,1)} fusion(bf16[16,64,128]{2,1,0:T(8,128)(2,1)S(1)} %copy-done.5, pred[1024,16]{0,1:T(8,128)(4,1)S(1)} %broadcast_compare_fusion, bf16[1024,64]{0,1:T(8,128)(2,1)S(1)} %maximum_select_fusion), kind=kOutput, calls=%fused_computation.11 | convolution fusion | flops 269615104 | bytes 671744 | tf_op jit(solution)/shard_map/dot_general | solution.py:108
  118.4 7.0 %all-to-all-start.1 = ((bf16[32,32,128]{2,1,0:T(8,128)(2,1)}), bf16[32,32,128]{2,1,0:T(8,128)(2,1)S(1)}, u32[]{:S(2)}, u32[]{:S(2)}) async-start(bf16[32,32,128]{2,1,0:T(8,128)(2,1)} %bitcast.4), calls=%async_computation.1 | async-start | bytes 524288 | tf_op jit(solution)/shard_map/all_to_all | solution.py:112
  125.4 5.7 %fusion.32 = f32[512,128]{1,0:T(8,128)S(1)} fusion(bf16[512,8192]{1,0:T(8,128)(2,1)} %all-gather.2.cloned.1.call-done, bf16[8192,128]{1,0:T(8,128)(2,1)S(1)} %copy-done), kind=kOutput, calls=%fused_computation.60 | convolution fusion | flops 1073741824 | bytes 10747904 | tf_op jit(solution)/shard_map/dot_general | solution.py:57
  131.1 5.8 %all-to-all-done.1 = bf16[32,32,128]{2,1,0:T(8,128)(2,1)S(1)} async-done(((bf16[32,32,128]{2,1,0:T(8,128)(2,1)}), bf16[32,32,128]{2,1,0:T(8,128)(2,1)S(1)}, u32[]{:S(2)}, u32[]{:S(2)}) %all-to-all-start.1) | async-done | bytes 262176 | tf_op jit(solution)/shard_map/all_to_all | solution.py:112
  137.0 1.4 fusion.14
  (37 shorter events, 2.4 us)
Async XLA Ops:
  6.5 118.9 %copy-start = (bf16[8192,128]{1,0:T(8,128)(2,1)S(1)}, bf16[8192,128]{1,0:T(8,128)(2,1)}, u32[]{:S(2)}) copy-start(bf16[8192,128]{1,0:T(8,128)(2,1)} %param.7) | copy-start | bytes 6291460
  6.5 118.9 %all-gather.2.cloned.1.call-start = ((), (), s32[]{:S(2)}) async-start(), calls=%async_computation.2 | async-start | bytes 8912896 | tf_op jit(solution)/shard_map/all_gather | solution.py:56
  8.5 2.2 %copy-start.2 = (s32[512]{0:T(512)}, s32[512]{0:T(512)S(1)}, u32[]{:S(2)}) copy-start(s32[512]{0:T(512)S(1)} %convert_add_fusion) | copy-start | bytes 6148
  15.1 41.1 %all-to-all-start = ((bf16[32,136,128]{2,1,0:T(8,128)(2,1)}), bf16[32,136,128]{2,1,0:T(8,128)(2,1)S(1)}, u32[]{:S(2)}, u32[]{:S(2)}) async-start(bf16[32,136,128]{2,1,0:T(8,128)(2,1)} %fusion.16), calls=%async_computation | async-start | bytes 2228224 | tf_op jit(solution)/shard_map/all_to_all | solution.py:91
  58.0 1.7 %copy-start.1 = (s32[1024]{0:T(1024)S(1)}, s32[1024]{0:T(1024)}, u32[]{:S(2)}) copy-start(s32[1024]{0:T(1024)} %reshape.163) | copy-start | bytes 12292
  58.0 1.8 %copy-start.4 = (s32[16]{0:T(128)S(1)}, s32[16]{0:T(128)}, u32[]{:S(2)}) copy-start(s32[16]{0:T(128)} %iota_add_fusion) | copy-start | bytes 196
  62.4 54.5 %copy-start.5 = (bf16[16,64,128]{2,1,0:T(8,128)(2,1)S(1)}, bf16[16,64,128]{2,1,0:T(8,128)(2,1)}, u32[]{:S(2)}) copy-start(bf16[16,64,128]{2,1,0:T(8,128)(2,1)} %param.9) | copy-start | bytes 786436
  62.5 6.1 %collective-permute-start = (f32[512,64]{0,1:T(8,128)S(1)}, f32[512,64]{0,1:T(8,128)S(1)}, u32[]{:S(2)}, u32[]{:S(2)}) collective-permute-start(f32[512,64]{0,1:T(8,128)S(1)} %slice_select_fusion), channel_id=1, source_target_pairs={{0,1},{1,0},{2,3},{3,2},{4,5},{5,4},{6,7},{7,6},{8,9},{9,8},{10,11... | collective-permute-start | bytes 393224 | tf_op jit(solution)/shard_map/ppermute | solution.py:20
  68.6 5.0 %collective-permute-start.1 = (f32[256,64]{0,1:T(8,128)S(1)}, f32[256,64]{0,1:T(8,128)S(1)}, u32[]{:S(2)}, u32[]{:S(2)}) collective-permute-start(f32[256,64]{0,1:T(8,128)S(1)} %slice_select_fusion.1), channel_id=1, source_target_pairs={{0,2},{1,3},{2,0},{3,1},{4,6},{5,7},{6,4},{7,5},{8,10},{9,11},{10,... | collective-permute-start | bytes 196616 | tf_op jit(solution)/shard_map/ppermute | solution.py:20
  73.6 5.6 %collective-permute-start.2 = (f32[128,64]{0,1:T(8,128)S(1)}, f32[128,64]{0,1:T(8,128)S(1)}, u32[]{:S(2)}, u32[]{:S(2)}) collective-permute-start(f32[128,64]{0,1:T(8,128)S(1)} %slice_select_fusion.3), channel_id=1, source_target_pairs={{0,4},{1,5},{2,6},{3,7},{4,0},{5,1},{6,2},{7,3},{8,12},{9,13},{10,... | collective-permute-start | bytes 98312 | tf_op jit(solution)/shard_map/ppermute | solution.py:20
  79.3 9.1 %collective-permute-start.3 = (f32[64,64]{0,1:T(8,128)S(1)}, f32[64,64]{0,1:T(8,128)S(1)}, u32[]{:S(2)}, u32[]{:S(2)}) collective-permute-start(f32[64,64]{0,1:T(8,128)S(1)} %slice_select_fusion.2), channel_id=1, source_target_pairs={{0,8},{1,9},{2,10},{3,11},{4,12},{5,13},{6,14},{7,15},{8,0},{9,1},... | collective-permute-start | bytes 49160 | tf_op jit(solution)/shard_map/ppermute | solution.py:20
  88.5 8.4 %collective-permute-start.4 = (bf16[64,64]{0,1:T(8,128)(2,1)S(1)}, bf16[64,64]{0,1:T(8,128)(2,1)S(1)}, u32[]{:S(2)}, u32[]{:S(2)}) collective-permute-start(bf16[64,64]{0,1:T(8,128)(2,1)S(1)} %add_convert_fusion), channel_id=1, source_target_pairs={{0,8},{1,9},{2,10},{3,11},{4,12},{5,13},{6,14},{7,15},{8,0},{9,1},... | collective-permute-start | bytes 24584 | tf_op jit(solution)/shard_map/ppermute | solution.py:26
  96.9 5.4 %collective-permute-start.5 = (bf16[128,64]{0,1:T(8,128)(2,1)S(1)}, bf16[128,64]{0,1:T(8,128)(2,1)S(1)}, u32[]{:S(2)}, u32[]{:S(2)}) collective-permute-start(bf16[128,64]{0,1:T(8,128)(2,1)S(1)} %maximum_select_fusion.3), channel_id=1, source_target_pairs={{0,4},{1,5},{2,6},{3,7},{4,0},{5,1},{6,2},{7,3},{8,12},{9,13},{10,... | collective-permute-start | bytes 49160 | tf_op jit(solution)/shard_map/ppermute | solution.py:26
  102.3 4.7 %collective-permute-start.6 = (bf16[256,64]{0,1:T(8,128)(2,1)S(1)}, bf16[256,64]{0,1:T(8,128)(2,1)S(1)}, u32[]{:S(2)}, u32[]{:S(2)}) collective-permute-start(bf16[256,64]{0,1:T(8,128)(2,1)S(1)} %maximum_select_fusion.2), channel_id=1, source_target_pairs={{0,2},{1,3},{2,0},{3,1},{4,6},{5,7},{6,4},{7,5},{8,10},{9,11},{10,... | collective-permute-start | bytes 98312 | tf_op jit(solution)/shard_map/ppermute | solution.py:26
  107.0 9.8 %collective-permute-start.7 = (bf16[512,64]{0,1:T(8,128)(2,1)S(1)}, bf16[512,64]{0,1:T(8,128)(2,1)S(1)}, u32[]{:S(2)}, u32[]{:S(2)}) collective-permute-start(bf16[512,64]{0,1:T(8,128)(2,1)S(1)} %maximum_select_fusion.1), channel_id=1, source_target_pairs={{0,1},{1,0},{2,3},{3,2},{4,5},{5,4},{6,7},{7,6},{8,9},{9,8},{10,11... | collective-permute-start | bytes 196616 | tf_op jit(solution)/shard_map/ppermute | solution.py:26
  118.4 18.6 %all-to-all-start.1 = ((bf16[32,32,128]{2,1,0:T(8,128)(2,1)}), bf16[32,32,128]{2,1,0:T(8,128)(2,1)S(1)}, u32[]{:S(2)}, u32[]{:S(2)}) async-start(bf16[32,32,128]{2,1,0:T(8,128)(2,1)} %bitcast.4), calls=%async_computation.1 | async-start | bytes 524288 | tf_op jit(solution)/shard_map/all_to_all | solution.py:112
  125.4 11.6 %copy-start.3 = (s32[512]{0:T(512)S(1)}, s32[512]{0:T(512)}, u32[]{:S(2)}) copy-start(s32[512]{0:T(512)} %copy-done.2) | copy-start | bytes 6148
Sparse Core Ops, SparseCore 0:
  9.5 64.1 all-gather.1

commit v3 on v2

--- a/solution.py
+++ b/solution.py
@@ -99,7 +99,10 @@
     all_ranks = jnp.dot(flat_rows, down_matrix, preferred_element_type=jnp.float32)
     all_ranks = all_ranks.reshape(slot_count, present_adapters, rank_dimension)
     partial_value = jnp.sum(jnp.where(selected, all_ranks, 0.0), axis=1)
-    reduced_rows = tensor_sum(partial_value, tensor_count)
+    ordered = partial_value + 0.0 * gathered[0, 0].astype(jnp.float32)
+    scattered = lax.psum_scatter(ordered, "tensor", scatter_dimension=0, tiled=True)
+    wide_block = jnp.pad(scattered.astype(jnp.bfloat16), ((0, 0), (0, 448)))
+    reduced_rows = lax.all_gather(wide_block, "tensor", axis=0, tiled=True)[:, :64]
 
     expanded_rows = jnp.where(
         selected, reduced_rows[:, None, :], jnp.zeros((), jnp.bfloat16)

time: 146 us -> 210 us (1.44)
  waiting for transfers between devices: 44.4 us -> 142 us
  starting transfers between devices: 63.5 us -> 23.7 us
  local copies, waits for them, and re-layouts: 6.95 us -> 13.2 us
    unnamed x1 -> x4, waiting for transfers between devices: 0.71 us -> 56.6 us
    ppermute x8 -> x0, starting transfers between devices: 42.8 us -> none  [the longest x4 22.6 us: tensor_sum(): other = lax.ppermute(block, 'tensor', exchange)]
    all_gather x0 -> x1, waiting for transfers between devices: none -> 42.7 us  [body(): lax.all_gather(wide_block, 'tensor', axis=0, tiled=True)[:, :64]]
    ppermute x8 -> x0, waiting for transfers between devices: 11.1 us -> none  [the longest x4 5.63 us: tensor_sum(): other = lax.ppermute(block, 'tensor', exchange)]
    all_gather x1, waiting for transfers between devices: 0.02 us -> 9.94 us  [body(): gathered = lax.all_gather(tokens, 'tensor', axis=1, tiled=True)]
    unnamed x12 -> x9, local copies, waits for them, and re-layouts: 0.03 us -> 3.15 us
    all_to_all x1, starting transfers between devices: 6.97 us -> 9.95 us  [body(): lax.all_to_all(adapter_correction, 'wide', split_axis=0, concat_axis=0, t...]
    slice x0 -> x3, local copies, waits for them, and re-layouts: none -> 2.29 us  [the longest x1 1.19 us: body(): ordered = partial_value + 0.0 * gathered[0, 0].astype(jnp.float32)]
  transfers between devices with their start and end apart: 11 -> 5, of which waited for: 10 -> 5; matrix products, arithmetic and copies ran while one was open for 15% -> 10% of each run, Pallas kernels for 0% -> 0%
where the time goes in v3:
time: 210 us; the launch traced here: 209 us
  waiting for transfers between devices  142 us (68%)
  starting transfers between devices  23.7 us (11%)
  between operations  13.9 us (7%)
  matrix products  13.4 us (6%)
  local copies, waits for them, and re-layouts  13.2 us (6%)
  other arithmetic  2.31 us (1%)
    unnamed x4, waiting for transfers between devices  56.6 us
    all_gather x1, waiting for transfers between devices, body(): lax.all_gather(wide_block, 'tensor', axis=0, tiled=True)[:, :64]  42.7 us
    all_to_all x1, waiting for transfers between devices, body(): lax.all_to_all(send_block, 'wide', split_axis=0, concat_axis=0, tiled=True)  27.3 us
    all_to_all x1, starting transfers between devices, body(): lax.all_to_all(send_block, 'wide', split_axis=0, concat_axis=0, tiled=True)  13.7 us
    all_to_all x1, starting transfers between devices, body(): lax.all_to_all(adapter_correction, 'wide', split_axis=0, concat_axis=0, t...  9.95 us
    all_gather x1, waiting for transfers between devices, body(): gathered = lax.all_gather(tokens, 'tensor', axis=1, tiled=True)  9.94 us
    all_to_all x1, waiting for transfers between devices, body(): lax.all_to_all(adapter_correction, 'wide', split_axis=0, concat_axis=0, t...  5.95 us
    dot_general x1, matrix products, body(): jnp.dot(gathered, key_value_weight, preferred_element_type=jnp.float32)  5.7 us
  transfers between devices with their start and end apart: 5, of which 5 were waited for; matrix products, arithmetic and copies ran while one was open for 10% of the time, Pallas kernels for 0%

profile of v3, /device:TPU:1, one launch (start us, length us, event | category | flops | bytes accessed | tf_op | source)
XLA Modules:
  0.0 209.0 jit_solution(6343781459754959343)
XLA Ops:
  6.5 0.7 all-gather.3.cloned.1.call-update
  7.3 0.9 select_reduce_fusion.1
  8.2 0.3 fusion.15
  8.5 0.1 broadcast_in_dim.39
  8.7 2.0 fusion.6
  10.6 1.2 copy-done.1
  11.9 1.3 copy.14
  13.2 1.7 reshape.117
  14.9 0.7 slice_reduce_fusion
  15.6 0.1 reshape_squeeze.5
  15.7 1.2 fusion.16
  16.9 13.7 %all-to-all-start = ((bf16[32,136,128]{2,1,0:T(8,128)(2,1)}), bf16[32,136,128]{2,1,0:T(8,128)(2,1)S(1)}, u32[]{:S(2)}, u32[]{:S(2)}) async-start(bf16[32,136,128]{2,1,0:T(8,128)(2,1)} %fusion.16), calls=%async_computation | async-start | bytes 2228224 | tf_op jit(solution)/shard_map/all_to_all | solution.py:91
  30.7 27.3 %all-to-all-done = bf16[32,136,128]{2,1,0:T(8,128)(2,1)S(1)} async-done(((bf16[32,136,128]{2,1,0:T(8,128)(2,1)}), bf16[32,136,128]{2,1,0:T(8,128)(2,1)S(1)}, u32[]{:S(2)}, u32[]{:S(2)}) %all-to-all-start) | async-done | bytes 1114144 | tf_op jit(solution)/shard_map/all_to_all | solution.py:91
  58.1 1.2 slice.27
  59.3 1.8 reshape.123
  61.1 0.1 broadcast_compare_fusion
  61.2 2.5 %select_reduce_fusion = f32[1024,64]{0,1:T(8,128)S(1)} fusion(bf16[1024,512,1]{1,0,2:T(8,128)(2,1)S(1)} %reshape.123, pred[1024,16]{0,1:T(8,128)(4,1)S(1)} %broadcast_compare_fusion, bf16[512,16,64]{0,2,1:T(8,128)(2,1)} %param.8), kind=kOutput, calls=%fused_computation | convolution fusion | flops 1075773440 | bytes 2375680 | tf_op jit(solution)/shard_map/dot_general | solution.py:99
  63.7 9.9 %all-gather.3.cloned.1.call-done = bf16[512,8192]{1,0:T(8,128)(2,1)} async-done(((bf16[512,512]{1,0:T(8,128)(2,1)}), bf16[512,8192]{1,0:T(8,128)(2,1)}) %all-gather.3.cloned.1.call-update) | async-done | bytes 8388624 | tf_op jit(solution)/shard_map/all_gather | solution.py:56
  73.7 1.2 slice.28
  75.5 1.1 copy.18
  76.7 55.9 %reduce-scatter.4.cloned.1.call-done = f32[64,64]{1,0:T(8,128)} async-done(((f32[1024,64]{1,0:T(8,128)}), f32[64,64]{1,0:T(8,128)}) %reduce-scatter.4.cloned.1.call-update) | async-done | bytes 16400
  132.6 0.8 copy.19
  133.4 0.1 copy.20
  133.5 0.7 pad.9.clone
  134.2 42.7 %all-gather.5.cloned.1.call-done = bf16[1024,512]{1,0:T(8,128)(2,1)} async-done(((bf16[64,512]{1,0:T(8,128)(2,1)}), bf16[1024,512]{1,0:T(8,128)(2,1)}) %all-gather.5.cloned.1.call-update) | async-done | bytes 1048592 | tf_op jit(solution)/shard_map/all_gather | solution.py:105
  176.9 1.0 slice.29
  177.8 0.1 copy.17
  178.0 1.5 fusion.10
  179.5 9.9 %all-to-all-start.1 = ((bf16[32,32,128]{2,1,0:T(8,128)(2,1)}), bf16[32,32,128]{2,1,0:T(8,128)(2,1)S(1)}, u32[]{:S(2)}, u32[]{:S(2)}) async-start(bf16[32,32,128]{2,1,0:T(8,128)(2,1)} %bitcast.5), calls=%async_computation.1 | async-start | bytes 524288 | tf_op jit(solution)/shard_map/all_to_all | solution.py:115
  189.4 5.7 %fusion.32 = f32[512,128]{1,0:T(8,128)S(1)} fusion(bf16[512,8192]{1,0:T(8,128)(2,1)} %all-gather.3.cloned.1.call-done, bf16[8192,128]{1,0:T(8,128)(2,1)S(1)} %copy-done), kind=kOutput, calls=%fused_computation.49 | convolution fusion | flops 1073741824 | bytes 10747904 | tf_op jit(solution)/shard_map/dot_general | solution.py:57
  195.1 5.9 %all-to-all-done.1 = bf16[32,32,128]{2,1,0:T(8,128)(2,1)S(1)} async-done(((bf16[32,32,128]{2,1,0:T(8,128)(2,1)}), bf16[32,32,128]{2,1,0:T(8,128)(2,1)S(1)}, u32[]{:S(2)}, u32[]{:S(2)}) %all-to-all-start.1) | async-done | bytes 262176 | tf_op jit(solution)/shard_map/all_to_all | solution.py:115
  201.1 1.4 fusion.14
  (17 shorter events, 0.4 us)
Async XLA Ops:
  6.5 182.9 %copy-start = (bf16[8192,128]{1,0:T(8,128)(2,1)S(1)}, bf16[8192,128]{1,0:T(8,128)(2,1)}, u32[]{:S(2)}) copy-start(bf16[8192,128]{1,0:T(8,128)(2,1)} %param.7) | copy-start | bytes 6291460
  6.5 67.1 %all-gather.3.cloned.1.call-start = ((), (), s32[]{:S(2)}) async-start(), calls=%async_computation.3 | async-start | bytes 8912896 | tf_op jit(solution)/shard_map/all_gather | solution.py:56
  10.6 1.2 copy-start.1
  16.9 41.1 %all-to-all-start = ((bf16[32,136,128]{2,1,0:T(8,128)(2,1)}), bf16[32,136,128]{2,1,0:T(8,128)(2,1)S(1)}, u32[]{:S(2)}, u32[]{:S(2)}) async-start(bf16[32,136,128]{2,1,0:T(8,128)(2,1)} %fusion.16), calls=%async_computation | async-start | bytes 2228224 | tf_op jit(solution)/shard_map/all_to_all | solution.py:91
  30.6 101.9 %reduce-scatter.4.cloned.1.call-start = ((), (), s32[]{:S(2)}) async-start(), calls=%async_computation.5 | async-start | bytes 557056
  63.7 114.2 %copy-start.2 = (bf16[16,64,128]{2,1,0:T(8,128)(2,1)S(1)}, bf16[16,64,128]{2,1,0:T(8,128)(2,1)}, u32[]{:S(2)}) copy-start(bf16[16,64,128]{2,1,0:T(8,128)(2,1)} %param.9) | copy-start | bytes 786436
  76.6 100.2 %all-gather.5.cloned.1.call-start = ((), (), s32[]{:S(2)}) async-start(), calls=%async_computation.4 | async-start | bytes 1114112 | tf_op jit(solution)/shard_map/all_gather | solution.py:105
  179.5 21.6 %all-to-all-start.1 = ((bf16[32,32,128]{2,1,0:T(8,128)(2,1)}), bf16[32,32,128]{2,1,0:T(8,128)(2,1)S(1)}, u32[]{:S(2)}, u32[]{:S(2)}) async-start(bf16[32,32,128]{2,1,0:T(8,128)(2,1)} %bitcast.5), calls=%async_computation.1 | async-start | bytes 524288 | tf_op jit(solution)/shard_map/all_to_all | solution.py:115
Sparse Core Ops, SparseCore 0:
  9.5 64.1 all-gather.2
  76.7 55.7 reduce-scatter.3
  134.9 41.9 all-gather.4

commit v4 on v2

--- a/solution.py
+++ b/solution.py
@@ -2,34 +2,6 @@
 import jax.numpy as jnp
 from jax import lax
 from jax.sharding import PartitionSpec as P
-
-
-def tensor_sum(partial_value, tensor_count):
-    position = lax.axis_index("tensor")
-    block = partial_value
-    steps = []
-    step = 1
-    while step < tensor_count:
-        half = block.shape[0] // 2
-        upper = (position // step) % 2
-        low_part = block[:half]
-        high_part = block[half:]
-        keep = jnp.where(upper == 1, high_part, low_part)
-        send = jnp.where(upper == 1, low_part, high_part)
-        exchange = [(i, i ^ step) for i in range(tensor_count)]
-        block = keep + lax.ppermute(send, "tensor", exchange)
-        steps.append((step, upper))
-        step *= 2
-    block = block.astype(jnp.bfloat16)
-    for step, upper in reversed(steps):
-        exchange = [(i, i ^ step) for i in range(tensor_count)]
-        other = lax.ppermute(block, "tensor", exchange)
-        block = jnp.where(
-            upper == 1,
-            jnp.concatenate([other, block], axis=0),
-            jnp.concatenate([block, other], axis=0),
-        )
-    return block
 
 
 def body(
@@ -99,7 +71,12 @@
     all_ranks = jnp.dot(flat_rows, down_matrix, preferred_element_type=jnp.float32)
     all_ranks = all_ranks.reshape(slot_count, present_adapters, rank_dimension)
     partial_value = jnp.sum(jnp.where(selected, all_ranks, 0.0), axis=1)
-    reduced_rows = tensor_sum(partial_value, tensor_count)
+    slot_blocks = partial_value.reshape(tensor_count, slot_count // tensor_count, rank_dimension)
+    gathered_blocks = lax.all_to_all(slot_blocks, "tensor", split_axis=0, concat_axis=0, tiled=True)
+    own_sum = jnp.sum(gathered_blocks, axis=0).astype(jnp.bfloat16)
+    spread = jnp.broadcast_to(own_sum[None], (tensor_count,) + own_sum.shape)
+    reduced_rows = lax.all_to_all(spread, "tensor", split_axis=0, concat_axis=0, tiled=True)
+    reduced_rows = reduced_rows.reshape(slot_count, rank_dimension)
 
     expanded_rows = jnp.where(
         selected, reduced_rows[:, None, :], jnp.zeros((), jnp.bfloat16)

time: 146 us -> 127 us (0.87)
  starting transfers between devices: 63.5 us -> 19 us
  blocking collectives: 0 us -> 33.5 us
  waiting for transfers between devices: 44.4 us -> 34.6 us
  local copies, waits for them, and re-layouts: 6.95 us -> 8.6 us
    ppermute x8 -> x0, starting transfers between devices: 42.8 us -> none  [the longest x4 22.6 us: tensor_sum(): other = lax.ppermute(block, 'tensor', exchange)]
    all_to_all x0 -> x2, blocking collectives: none -> 33.5 us  [the longest x1 21.6 us: body(): lax.all_to_all(slot_blocks, 'tensor', split_axis=0, concat_axis=0, tiled=...]
    ppermute x8 -> x0, waiting for transfers between devices: 11.1 us -> none  [the longest x4 5.63 us: tensor_sum(): other = lax.ppermute(block, 'tensor', exchange)]
    all_to_all x1, starting transfers between devices: 6.97 us -> 5.33 us  [body(): lax.all_to_all(adapter_correction, 'wide', split_axis=0, concat_axis=0, t...]
  transfers between devices with their start and end apart: 11 -> 3, of which waited for: 10 -> 2; matrix products, arithmetic and copies ran while one was open for 15% -> 19% of each run, Pallas kernels for 0% -> 0%
where the time goes in v4:
time: 127 us; the launch traced here: 126 us
  waiting for transfers between devices  34.6 us (27%)
  blocking collectives  33.5 us (26%)
  starting transfers between devices  19 us (15%)
  between operations  13.6 us (11%)
  matrix products  13.4 us (11%)
  local copies, waits for them, and re-layouts  8.6 us (7%)
  other arithmetic  3.61 us (3%)
    all_to_all x1, waiting for transfers between devices, body(): lax.all_to_all(send_block, 'wide', split_axis=0, concat_axis=0, tiled=True)  27.3 us
    all_to_all x1, blocking collectives, body(): lax.all_to_all(slot_blocks, 'tensor', split_axis=0, concat_axis=0, tiled=...  21.6 us
    all_to_all x1, starting transfers between devices, body(): lax.all_to_all(send_block, 'wide', split_axis=0, concat_axis=0, tiled=True)  13.7 us
    all_to_all x1, blocking collectives, body(): lax.all_to_all(spread, 'tensor', split_axis=0, concat_axis=0, tiled=True)  11.9 us
    all_to_all x1, waiting for transfers between devices, body(): lax.all_to_all(adapter_correction, 'wide', split_axis=0, concat_axis=0, t...  6.53 us
    dot_general x1, matrix products, body(): jnp.dot(gathered, key_value_weight, preferred_element_type=jnp.float32)  5.71 us
    all_to_all x1, starting transfers between devices, body(): lax.all_to_all(adapter_correction, 'wide', split_axis=0, concat_axis=0, t...  5.33 us
    dot_general x1, matrix products, body(): jnp.dot(flat_rows, down_matrix, preferred_element_type=jnp.float32)  2.59 us
  transfers between devices with their start and end apart: 3, of which 2 were waited for; matrix products, arithmetic and copies ran while one was open for 19% of the time, Pallas kernels for 0%

profile of v4, /device:TPU:1, one launch (start us, length us, event | category | flops | bytes accessed | tf_op | source)
XLA Modules:
  0.0 126.3 jit_solution(1712603548768722369)
XLA Ops:
  6.5 0.7 all-gather.2.cloned.1.call-update
  7.3 0.9 select_reduce_fusion.1
  8.2 0.3 fusion.15
  8.5 0.1 broadcast_in_dim.70
  8.7 2.0 %fusion.6 = bf16[1024,640]{0,1:T(8,128)(2,1)S(1)} fusion(s32[512]{0:T(512)S(1)} %convert_add_fusion, bf16[512,128]{1,0:T(8,128)(2,1)S(1)} %broadcast_in_dim.70, bf16[512,512]{1,0:T(8,128)(2,1)} %param.6), kind=kOutput, calls=%fused_computation.9 | convolution fusion | flops 673579008 | bytes 1968128 | tf_op jit(solution)/shard_map/dot_general | solution.py:55
  10.7 0.1 reshape_squeeze.5
  10.8 1.4 %copy.19 = bf16[1024,512]{1,0:T(8,128)(2,1)} copy(bf16[1024,512]{0,1:T(8,128)(2,1)S(1)} %slice.16) | data formatting | bytes 2097152 | tf_op jit(solution)/shard_map/slice | solution.py:58
  12.2 1.7 %reshape.120 = bf16[32,128,128]{2,1,0:T(8,128)(2,1)S(1)} reshape(bf16[1024,512]{1,0:T(8,128)(2,1)} %copy.19) | data formatting | bytes 2097152 | tf_op jit(solution)/shard_map/reshape | solution.py:58
  13.9 1.2 fusion.16
  15.1 13.7 %all-to-all-start = ((bf16[32,136,128]{2,1,0:T(8,128)(2,1)}), bf16[32,136,128]{2,1,0:T(8,128)(2,1)S(1)}, u32[]{:S(2)}, u32[]{:S(2)}) async-start(bf16[32,136,128]{2,1,0:T(8,128)(2,1)} %fusion.16), calls=%async_computation | async-start | bytes 2228224 | tf_op jit(solution)/shard_map/all_to_all | solution.py:63
  28.8 27.3 %all-to-all-done = bf16[32,136,128]{2,1,0:T(8,128)(2,1)S(1)} async-done(((bf16[32,136,128]{2,1,0:T(8,128)(2,1)}), bf16[32,136,128]{2,1,0:T(8,128)(2,1)S(1)}, u32[]{:S(2)}, u32[]{:S(2)}) %all-to-all-start) | async-done | bytes 1114144 | tf_op jit(solution)/shard_map/all_to_all | solution.py:63
  56.3 1.2 slice.19
  57.5 1.7 %reshape.127 = bf16[1024,512,1]{1,0,2:T(8,128)(2,1)S(1)} reshape(bf16[32,128,128]{2,1,0:T(8,128)(2,1)} %slice.19) | data formatting | bytes 2097152 | tf_op jit(solution)/shard_map/reshape | solution.py:64
  59.2 0.1 broadcast_compare_fusion
  59.3 2.6 %select_reduce_fusion = f32[1024,64]{0,1:T(8,128)S(1)} fusion(bf16[1024,512,1]{1,0,2:T(8,128)(2,1)S(1)} %reshape.127, pred[1024,16]{0,1:T(8,128)(4,1)S(1)} %broadcast_compare_fusion, bf16[512,16,64]{0,2,1:T(8,128)(2,1)} %param.8), kind=kOutput, calls=%fused_computation | convolution fusion | flops 1075773440 | bytes 2375680 | tf_op jit(solution)/shard_map/dot_general | solution.py:71
  61.9 0.1 reshape.123
  62.0 0.2 copy.24
  62.2 0.3 reshape.138
  62.5 21.6 %all_to_all.20 = f32[16,1,4096]{2,1,0:T(1,128)S(1)} all-to-all(f32[16,1,4096]{2,1,0:T(1,128)S(1)} %reshape.138), channel_id=1, replica_groups=mesh['wide'=32,'tensor'=16] {'tensor'}, dimensions={0} | all-to-all | bytes 524288 | tf_op jit(solution)/shard_map/all_to_all | solution.py:75
  84.1 0.5 broadcast.150
  84.7 1.3 %reduce.6 = f32[16,4096]{1,0:T(8,128)S(1)} reduce(f32[16,1,4096]{2,1,0:T(1,128)S(1)} %all_to_all.20, f32[]{:T(128)} %broadcast.150), dimensions={1}, to_apply=%all_to_all.13.reduce_sub_computation | reduce | bytes 524292 | tf_op jit(solution)/shard_map/all_to_all | solution.py:75
  85.9 0.2 reshape.139
  86.3 0.2 reshape.140
  86.5 11.9 %all_to_all.21 = bf16[16,2,2048]{2,1,0:T(2,128)(2,1)S(1)} all-to-all(bf16[16,2,2048]{2,1,0:T(2,128)(2,1)S(1)} %reshape.140), channel_id=1, replica_groups=mesh['wide'=32,'tensor'=16] {'tensor'}, dimensions={0} | all-to-all | bytes 262144 | tf_op jit(solution)/shard_map/all_to_all | solution.py:78
  98.4 0.2 reshape.141
  98.6 0.2 copy.22
  98.8 0.2 broadcast_in_dim.74
  99.0 1.5 %fusion.10 = bf16[1024,128]{1,0:T(8,128)(2,1)} fusion(bf16[16,64,128]{2,1,0:T(8,128)(2,1)S(1)} %copy-done.1, pred[1024,16]{0,1:T(8,128)(4,1)S(1)} %broadcast_compare_fusion, bf16[1024,64]{0,1:T(8,128)(2,1)S(1)} %broadcast_in_dim.74), kind=kOutput, calls=%fused_computation.11 | convolution fusion | flops 269615104 | bytes 671744 | tf_op jit(solution)/shard_map/dot_general | solution.py:85
  100.5 5.3 %all-to-all-start.3 = ((bf16[32,32,128]{2,1,0:T(8,128)(2,1)}), bf16[32,32,128]{2,1,0:T(8,128)(2,1)S(1)}, u32[]{:S(2)}, u32[]{:S(2)}) async-start(bf16[32,32,128]{2,1,0:T(8,128)(2,1)} %bitcast.4), calls=%async_computation.3 | async-start | bytes 524288 | tf_op jit(solution)/shard_map/all_to_all | solution.py:89
  105.8 5.7 %fusion.32 = f32[512,128]{1,0:T(8,128)S(1)} fusion(bf16[512,8192]{1,0:T(8,128)(2,1)} %all-gather.2.cloned.1.call-done, bf16[8192,128]{1,0:T(8,128)(2,1)S(1)} %copy-done), kind=kOutput, calls=%fused_computation.51 | convolution fusion | flops 1073741824 | bytes 10747904 | tf_op jit(solution)/shard_map/dot_general | solution.py:29
  111.5 6.5 %all-to-all-done.3 = bf16[32,32,128]{2,1,0:T(8,128)(2,1)S(1)} async-done(((bf16[32,32,128]{2,1,0:T(8,128)(2,1)}), bf16[32,32,128]{2,1,0:T(8,128)(2,1)S(1)}, u32[]{:S(2)}, u32[]{:S(2)}) %all-to-all-start.3) | async-done | bytes 262176 | tf_op jit(solution)/shard_map/all_to_all | solution.py:89
  118.1 1.4 %fusion.14 = bf16[512,128]{1,0:T(8,128)(2,1)} fusion(f32[512,128]{1,0:T(8,128)S(1)} %fusion.32, bf16[1024,128]{1,0:T(8,128)(2,1)S(1)} %bitcast.32, s32[512]{0:T(512)S(1)} %convert_add_fusion), kind=kOutput, calls=%fused_computation.13 | convolution fusion | flops 134873088 | bytes 657408 | tf_op jit(solution)/shard_map/dot_general | solution.py:93
  (15 shorter events, 0.4 us)
Async XLA Ops:
  6.5 99.3 %copy-start = (bf16[8192,128]{1,0:T(8,128)(2,1)S(1)}, bf16[8192,128]{1,0:T(8,128)(2,1)}, u32[]{:S(2)}) copy-start(bf16[8192,128]{1,0:T(8,128)(2,1)} %param.7) | copy-start | bytes 6291460
  6.5 99.3 %all-gather.2.cloned.1.call-start = ((), (), s32[]{:S(2)}) async-start(), calls=%async_computation.4 | async-start | bytes 8912896 | tf_op jit(solution)/shard_map/all_gather | solution.py:28
  15.1 41.1 %all-to-all-start = ((bf16[32,136,128]{2,1,0:T(8,128)(2,1)}), bf16[32,136,128]{2,1,0:T(8,128)(2,1)S(1)}, u32[]{:S(2)}, u32[]{:S(2)}) async-start(bf16[32,136,128]{2,1,0:T(8,128)(2,1)} %fusion.16), calls=%async_computation | async-start | bytes 2228224 | tf_op jit(solution)/shard_map/all_to_all | solution.py:63
  84.1 14.8 %copy-start.1 = (bf16[16,64,128]{2,1,0:T(8,128)(2,1)S(1)}, bf16[16,64,128]{2,1,0:T(8,128)(2,1)}, u32[]{:S(2)}) copy-start(bf16[16,64,128]{2,1,0:T(8,128)(2,1)} %param.9) | copy-start | bytes 786436
  100.5 17.6 %all-to-all-start.3 = ((bf16[32,32,128]{2,1,0:T(8,128)(2,1)}), bf16[32,32,128]{2,1,0:T(8,128)(2,1)S(1)}, u32[]{:S(2)}, u32[]{:S(2)}) async-start(bf16[32,32,128]{2,1,0:T(8,128)(2,1)} %bitcast.4), calls=%async_computation.3 | async-start | bytes 524288 | tf_op jit(solution)/shard_map/all_to_all | solution.py:89
Sparse Core Ops, SparseCore 0:
  9.5 64.1 all-gather.1

commit v5 on v4

--- a/solution.py
+++ b/solution.py
@@ -22,7 +22,6 @@
     total_adapters = adapter_storage_slot.shape[0]
     slot_count = wide_count * capacity
     lane = 128
-    row_tiles = capacity * feature_portion // lane
     info_rows = 8
 
     gathered = lax.all_gather(tokens, "tensor", axis=1, tiled=True)
@@ -48,21 +47,33 @@
         jnp.arange(slot_count, dtype=jnp.int32)[:, None] == destination[None, :]
     ).astype(jnp.bfloat16)
 
+    lane_tiles = feature_portion // lane
     local_code = jnp.broadcast_to(
         (local_index + 1).astype(jnp.bfloat16)[:, None], (row_count, lane)
     )
-    extended = jnp.concatenate([tokens, local_code], axis=1)
-    placed = jnp.dot(placement, extended, preferred_element_type=jnp.float32).astype(
-        jnp.bfloat16
-    )
-    send_rows = placed[:, :feature_portion].reshape(wide_count, row_tiles, lane)
-    slot_code = placed[:, feature_portion].reshape(wide_count, 1, capacity)
-    slot_code = jnp.pad(slot_code, ((0, 0), (0, info_rows - 1), (0, lane - capacity)))
-    send_block = jnp.concatenate([send_rows, slot_code], axis=1)
+    pieces = []
+    for tile in range(lane_tiles):
+        placed = jnp.dot(
+            placement, tokens[:, tile * lane : (tile + 1) * lane],
+            preferred_element_type=jnp.float32,
+        ).astype(jnp.bfloat16)
+        pieces.append(placed.reshape(wide_count, capacity, lane))
+    placed_code = jnp.dot(placement, local_code, preferred_element_type=jnp.float32)
+    slot_code = placed_code[:, 0].astype(jnp.bfloat16).reshape(wide_count, 1, capacity)
+    pieces.append(jnp.pad(slot_code, ((0, 0), (0, info_rows - 1), (0, lane - capacity))))
+    send_block = jnp.concatenate(pieces, axis=1)
 
     got_block = lax.all_to_all(send_block, "wide", split_axis=0, concat_axis=0, tiled=True)
-    flat_rows = got_block[:, :row_tiles, :].reshape(slot_count, feature_portion)
-    got_code = got_block[:, row_tiles, :capacity].reshape(slot_count).astype(jnp.int32)
+    flat_rows = jnp.concatenate(
+        [
+            got_block[:, tile * capacity : (tile + 1) * capacity, :].reshape(slot_count, lane)
+            for tile in range(lane_tiles)
+        ],
+        axis=1,
+    )
+    got_code = (
+        got_block[:, lane_tiles * capacity, :capacity].reshape(slot_count).astype(jnp.int32)
+    )
     selected = (
         got_code[:, None] == jnp.arange(1, present_adapters + 1, dtype=jnp.int32)[None, :]
     )[:, :, None]

time: 127 us -> 127 us (level)
  starting transfers between devices: 19 us -> 21.1 us
    unnamed x9 -> x17, local copies, waits for them, and re-layouts: 1.04 us -> 5.23 us
    reshape x2 -> x0, local copies, waits for them, and re-layouts: 3.4 us -> none  [the longest x1 1.7 us: body(): send_rows = placed[:, :feature_portion].reshape(wide_count, row_tiles, lane)]
    slice x4 -> x2, local copies, waits for them, and re-layouts: 2.69 us -> 0.11 us  [the longest x1 0.08 us: body(): got_block[:, tile * capacity:(tile + 1) * capacity, :]]
    all_to_all x1, starting transfers between devices: 5.33 us -> 7.4 us  [body(): lax.all_to_all(adapter_correction, 'wide', split_axis=0, concat_axis=0, t...]
    dot_general x1 -> x5, matrix products: 1.96 us -> 3.35 us  [the longest x4 2.76 us: body(): jnp.dot(placement, tokens[:, tile * lane:(tile + 1) * lane], preferred_el...]
    dot_general x1, matrix products: 2.59 us -> 1.28 us  [body(): jnp.dot(flat_rows, down_matrix, preferred_element_type=jnp.float32)]
  transfers between devices with their start and end apart: 3 -> 3, of which waited for: 2 -> 2; matrix products, arithmetic and copies ran while one was open for 19% -> 17% of each run, Pallas kernels for 0% -> 0%
where the time goes in v5:
time: 127 us; the launch traced here: 126 us
  waiting for transfers between devices  34.6 us (27%)
  blocking collectives  33.5 us (26%)
  starting transfers between devices  21.1 us (17%)
  between operations  13.6 us (11%)
  matrix products  13.5 us (11%)
  local copies, waits for them, and re-layouts  7.38 us (6%)
  other arithmetic  2.49 us (2%)
    all_to_all x1, waiting for transfers between devices, body(): lax.all_to_all(send_block, 'wide', split_axis=0, concat_axis=0, tiled=True)  27.3 us
    all_to_all x1, blocking collectives, body(): lax.all_to_all(slot_blocks, 'tensor', split_axis=0, concat_axis=0, tiled=...  21.6 us
    all_to_all x1, starting transfers between devices, body(): lax.all_to_all(send_block, 'wide', split_axis=0, concat_axis=0, tiled=True)  13.7 us
    all_to_all x1, blocking collectives, body(): lax.all_to_all(spread, 'tensor', split_axis=0, concat_axis=0, tiled=True)  11.9 us
    all_to_all x1, starting transfers between devices, body(): lax.all_to_all(adapter_correction, 'wide', split_axis=0, concat_axis=0, t...  7.4 us
    all_to_all x1, waiting for transfers between devices, body(): lax.all_to_all(adapter_correction, 'wide', split_axis=0, concat_axis=0, t...  6.55 us
    dot_general x1, matrix products, body(): jnp.dot(gathered, key_value_weight, preferred_element_type=jnp.float32)  5.7 us
    unnamed x17, local copies, waits for them, and re-layouts  5.23 us
  transfers between devices with their start and end apart: 3, of which 2 were waited for; matrix products, arithmetic and copies ran while one was open for 17% of the time, Pallas kernels for 0%

profile of v5, /device:TPU:1, one launch (start us, length us, event | category | flops | bytes accessed | tf_op | source)
XLA Modules:
  0.0 126.2 jit_solution(16141024307924597499)
XLA Ops:
  6.5 0.7 all-gather.2.cloned.1.call-update
  7.3 1.0 select_reduce_fusion.1
  8.3 0.3 fusion.21
  8.6 0.6 fusion.3
  9.3 1.4 %fusion.15 = bf16[1024,128]{1,0:T(8,128)(2,1)S(1)} fusion(s32[512]{0:T(512)S(1)} %convert_add_fusion, bf16[512,512]{1,0:T(8,128)(2,1)} %param.6), kind=kOutput, calls=%fused_computation.13 | convolution fusion | flops 134873088 | bytes 395264 | tf_op jit(solution)/shard_map/dot_general | solution.py:56
  10.7 0.8 constant_dynamic-update-slice_fusion.3
  11.4 0.5 fusion.16
  11.9 0.8 constant_dynamic-update-slice_fusion.2
  12.7 0.5 fusion.17
  13.2 0.8 constant_dynamic-update-slice_fusion.1
  13.9 0.5 fusion.18
  14.4 0.8 constant_dynamic-update-slice_fusion
  15.2 0.7 pad_dynamic-update-slice_fusion
  15.9 13.7 %all-to-all-start = ((bf16[32,136,128]{2,1,0:T(8,128)(2,1)}), bf16[32,136,128]{2,1,0:T(8,128)(2,1)S(1)}, u32[]{:S(2)}, u32[]{:S(2)}) async-start(bf16[32,136,128]{2,1,0:T(8,128)(2,1)} %pad_dynamic-update-slice_fusion), calls=%async_computation | async-start | bytes 2228224 | tf_op jit(solution)/shard_map/all_to_all | solution.py:66
  29.6 27.3 %all-to-all-done = bf16[32,136,128]{2,1,0:T(8,128)(2,1)S(1)} async-done(((bf16[32,136,128]{2,1,0:T(8,128)(2,1)}), bf16[32,136,128]{2,1,0:T(8,128)(2,1)S(1)}, u32[]{:S(2)}, u32[]{:S(2)}) %all-to-all-start) | async-done | bytes 1114144 | tf_op jit(solution)/shard_map/all_to_all | solution.py:66
  57.3 1.1 copy-done.2
  58.3 1.3 %select_reduce_fusion = f32[1024,64]{0,1:T(8,128)S(1)} fusion(pred[1024,16]{0,1:T(8,128)(4,1)S(1)} %broadcast_compare_fusion, bf16[1024,128]{1,0:T(8,128)(2,1)S(1)} %bitcast.48, bf16[1024,128]{1,0:T(8,128)(2,1)S(1)} %bitcast.49, bf16[1024,128]{1,0:T(8,128)(2,1)S(1)} %bitcast.50, bf16[1024,128]{1,0:T(8,128)(2,1)S(1)} %bitcast.47, ...), kind=kOutput, calls=%fused_computation | convolution fusion | flops 1079967744 | bytes 2375680 | tf_op jit(solution)/shard_map/dot_general | solution.py:82
  60.0 0.3 reshape.173
  60.3 21.6 %all_to_all.20 = f32[16,1,4096]{2,1,0:T(1,128)S(1)} all-to-all(f32[16,1,4096]{2,1,0:T(1,128)S(1)} %reshape.173), channel_id=1, replica_groups=mesh['wide'=32,'tensor'=16] {'tensor'}, dimensions={0} | all-to-all | bytes 524288 | tf_op jit(solution)/shard_map/all_to_all | solution.py:86
  81.9 0.5 broadcast.146
  82.4 1.3 %reduce.6 = f32[16,4096]{1,0:T(8,128)S(1)} reduce(f32[16,1,4096]{2,1,0:T(1,128)S(1)} %all_to_all.20, f32[]{:T(128)} %broadcast.146), dimensions={1}, to_apply=%all_to_all.13.reduce_sub_computation | reduce | bytes 524292 | tf_op jit(solution)/shard_map/all_to_all | solution.py:86
  83.7 0.2 reshape.174
  84.0 0.2 reshape.175
  84.3 11.9 %all_to_all.21 = bf16[16,2,2048]{2,1,0:T(2,128)(2,1)S(1)} all-to-all(bf16[16,2,2048]{2,1,0:T(2,128)(2,1)S(1)} %reshape.175), channel_id=1, replica_groups=mesh['wide'=32,'tensor'=16] {'tensor'}, dimensions={0} | all-to-all | bytes 262144 | tf_op jit(solution)/shard_map/all_to_all | solution.py:89
  96.1 0.2 reshape.176
  96.3 0.2 copy.16
  96.5 0.2 broadcast_in_dim.74
  96.7 1.5 %fusion.12 = bf16[1024,128]{1,0:T(8,128)(2,1)} fusion(bf16[16,64,128]{2,1,0:T(8,128)(2,1)S(1)} %copy-done.3, pred[1024,16]{0,1:T(8,128)(4,1)S(1)} %broadcast_compare_fusion, bf16[1024,64]{0,1:T(8,128)(2,1)S(1)} %broadcast_in_dim.74), kind=kOutput, calls=%fused_computation.12 | convolution fusion | flops 269615104 | bytes 671744 | tf_op jit(solution)/shard_map/dot_general | solution.py:96
  98.2 7.4 %all-to-all-start.3 = ((bf16[32,32,128]{2,1,0:T(8,128)(2,1)}), bf16[32,32,128]{2,1,0:T(8,128)(2,1)S(1)}, u32[]{:S(2)}, u32[]{:S(2)}) async-start(bf16[32,32,128]{2,1,0:T(8,128)(2,1)} %bitcast.13), calls=%async_computation.3 | async-start | bytes 524288 | tf_op jit(solution)/shard_map/all_to_all | solution.py:100
  105.7 5.7 %fusion.51 = f32[512,128]{1,0:T(8,128)S(1)} fusion(bf16[512,8192]{1,0:T(8,128)(2,1)} %all-gather.2.cloned.1.call-done, bf16[8192,128]{1,0:T(8,128)(2,1)S(1)} %copy-done), kind=kOutput, calls=%fused_computation.75 | convolution fusion | flops 1073741824 | bytes 10747904 | tf_op jit(solution)/shard_map/dot_general | solution.py:28
  111.4 6.5 %all-to-all-done.3 = bf16[32,32,128]{2,1,0:T(8,128)(2,1)S(1)} async-done(((bf16[32,32,128]{2,1,0:T(8,128)(2,1)}), bf16[32,32,128]{2,1,0:T(8,128)(2,1)S(1)}, u32[]{:S(2)}, u32[]{:S(2)}) %all-to-all-start.3) | async-done | bytes 262176 | tf_op jit(solution)/shard_map/all_to_all | solution.py:100
  117.9 1.4 %fusion.20 = bf16[512,128]{1,0:T(8,128)(2,1)} fusion(f32[512,128]{1,0:T(8,128)S(1)} %fusion.51, bf16[1024,128]{1,0:T(8,128)(2,1)S(1)} %bitcast.42, s32[512]{0:T(512)S(1)} %convert_add_fusion), kind=kOutput, calls=%fused_computation.18 | convolution fusion | flops 134873088 | bytes 657408 | tf_op jit(solution)/shard_map/dot_general | solution.py:104
  (22 shorter events, 0.9 us)
Async XLA Ops:
  6.5 99.1 %copy-start = (bf16[8192,128]{1,0:T(8,128)(2,1)S(1)}, bf16[8192,128]{1,0:T(8,128)(2,1)}, u32[]{:S(2)}) copy-start(bf16[8192,128]{1,0:T(8,128)(2,1)} %param.7) | copy-start | bytes 6291460
  6.5 4.9 %copy-start.1 = (bf16[512,512]{1,0:T(8,128)(2,1)S(1)}, bf16[512,512]{1,0:T(8,128)(2,1)}, u32[]{:S(2)}) copy-start(bf16[512,512]{1,0:T(8,128)(2,1)} %param.6) | copy-start | bytes 1572868
  6.5 99.1 %all-gather.2.cloned.1.call-start = ((), (), s32[]{:S(2)}) async-start(), calls=%async_computation.4 | async-start | bytes 8912896 | tf_op jit(solution)/shard_map/all_gather | solution.py:27
  15.9 41.1 %all-to-all-start = ((bf16[32,136,128]{2,1,0:T(8,128)(2,1)}), bf16[32,136,128]{2,1,0:T(8,128)(2,1)S(1)}, u32[]{:S(2)}, u32[]{:S(2)}) async-start(bf16[32,136,128]{2,1,0:T(8,128)(2,1)} %pad_dynamic-update-slice_fusion), calls=%async_computation | async-start | bytes 2228224 | tf_op jit(solution)/shard_map/all_to_all | solution.py:66
  57.1 1.2 copy-start.2
  81.9 14.8 %copy-start.3 = (bf16[16,64,128]{2,1,0:T(8,128)(2,1)S(1)}, bf16[16,64,128]{2,1,0:T(8,128)(2,1)}, u32[]{:S(2)}) copy-start(bf16[16,64,128]{2,1,0:T(8,128)(2,1)} %param.9) | copy-start | bytes 786436
  98.2 19.7 %all-to-all-start.3 = ((bf16[32,32,128]{2,1,0:T(8,128)(2,1)}), bf16[32,32,128]{2,1,0:T(8,128)(2,1)S(1)}, u32[]{:S(2)}, u32[]{:S(2)}) async-start(bf16[32,32,128]{2,1,0:T(8,128)(2,1)} %bitcast.13), calls=%async_computation.3 | async-start | bytes 524288 | tf_op jit(solution)/shard_map/all_to_all | solution.py:100
Sparse Core Ops, SparseCore 0:
  9.5 64.1 all-gather.1

commit v6 on v5

--- a/solution.py
+++ b/solution.py
@@ -83,8 +83,10 @@
     all_ranks = all_ranks.reshape(slot_count, present_adapters, rank_dimension)
     partial_value = jnp.sum(jnp.where(selected, all_ranks, 0.0), axis=1)
     slot_blocks = partial_value.reshape(tensor_count, slot_count // tensor_count, rank_dimension)
-    gathered_blocks = lax.all_to_all(slot_blocks, "tensor", split_axis=0, concat_axis=0, tiled=True)
-    own_sum = jnp.sum(gathered_blocks, axis=0).astype(jnp.bfloat16)
+    gathered_blocks = lax.all_to_all(
+        slot_blocks.astype(jnp.bfloat16), "tensor", split_axis=0, concat_axis=0, tiled=True
+    )
+    own_sum = jnp.sum(gathered_blocks.astype(jnp.float32), axis=0).astype(jnp.bfloat16)
     spread = jnp.broadcast_to(own_sum[None], (tensor_count,) + own_sum.shape)
     reduced_rows = lax.all_to_all(spread, "tensor", split_axis=0, concat_axis=0, tiled=True)
     reduced_rows = reduced_rows.reshape(slot_count, rank_dimension)

time: 127 us -> 121 us (0.953)
  blocking collectives: 33.5 us -> 30.7 us
    all_to_all x1, blocking collectives: 21.6 us -> 19.1 us  [body(): lax.all_to_all(slot_blocks.astype(jnp.bfloat16), 'tensor', split_axis=0,...]
    all_to_all x1 -> x0, other arithmetic: 1.28 us -> none  [body(): lax.all_to_all(slot_blocks, 'tensor', split_axis=0, concat_axis=0, tiled=...]
  transfers between devices with their start and end apart: 3 -> 3, of which waited for: 2 -> 2; matrix products, arithmetic and copies ran while one was open for 17% -> 16% of each run, Pallas kernels for 0% -> 0%
where the time goes in v6:
time: 121 us
  waiting for transfers between devices  34.6 us (29%)
  blocking collectives  30.7 us (25%)
  starting transfers between devices  20.7 us (17%)
  between operations  13.6 us (11%)
  matrix products  13.5 us (11%)
  local copies, waits for them, and re-layouts  6.72 us (6%)
  other arithmetic  1.23 us (1%)
    all_to_all x1, waiting for transfers between devices, body(): lax.all_to_all(send_block, 'wide', split_axis=0, concat_axis=0, tiled=True)  27.3 us
    all_to_all x1, blocking collectives, body(): lax.all_to_all(slot_blocks.astype(jnp.bfloat16), 'tensor', split_axis=0,...  19.1 us
    all_to_all x1, starting transfers between devices, body(): lax.all_to_all(send_block, 'wide', split_axis=0, concat_axis=0, tiled=True)  13.7 us
    all_to_all x1, blocking collectives, body(): lax.all_to_all(spread, 'tensor', split_axis=0, concat_axis=0, tiled=True)  11.6 us
    all_to_all x1, starting transfers between devices, body(): lax.all_to_all(adapter_correction, 'wide', split_axis=0, concat_axis=0, t...  6.96 us
    all_to_all x1, waiting for transfers between devices, body(): lax.all_to_all(adapter_correction, 'wide', split_axis=0, concat_axis=0, t...  6.54 us
    dot_general x1, matrix products, body(): jnp.dot(gathered, key_value_weight, preferred_element_type=jnp.float32)  5.7 us
    unnamed x17, local copies, waits for them, and re-layouts  5.14 us
  transfers between devices with their start and end apart: 3, of which 2 were waited for; matrix products, arithmetic and copies ran while one was open for 16% of the time, Pallas kernels for 0%

profile of v6, /device:TPU:1, one launch (start us, length us, event | category | flops | bytes accessed | tf_op | source)
XLA Modules:
  0.0 121.0 jit_solution(8759317598897131417)
XLA Ops:
  6.5 0.7 all-gather.2.cloned.1.call-update
  7.3 1.0 select_reduce_fusion.1
  8.3 0.3 fusion.21
  8.6 0.6 fusion.3
  9.3 1.4 %fusion.15 = bf16[1024,128]{1,0:T(8,128)(2,1)S(1)} fusion(s32[512]{0:T(512)S(1)} %convert_add_fusion, bf16[512,512]{1,0:T(8,128)(2,1)} %param.6), kind=kOutput, calls=%fused_computation.13 | convolution fusion | flops 134873088 | bytes 395264 | tf_op jit(solution)/shard_map/dot_general | solution.py:56
  10.7 0.8 constant_dynamic-update-slice_fusion.3
  11.4 0.5 fusion.16
  11.9 0.8 constant_dynamic-update-slice_fusion.2
  12.7 0.5 fusion.17
  13.2 0.8 constant_dynamic-update-slice_fusion.1
  13.9 0.5 fusion.18
  14.4 0.8 constant_dynamic-update-slice_fusion
  15.2 0.7 pad_dynamic-update-slice_fusion
  15.9 13.7 %all-to-all-start = ((bf16[32,136,128]{2,1,0:T(8,128)(2,1)}), bf16[32,136,128]{2,1,0:T(8,128)(2,1)S(1)}, u32[]{:S(2)}, u32[]{:S(2)}) async-start(bf16[32,136,128]{2,1,0:T(8,128)(2,1)} %pad_dynamic-update-slice_fusion), calls=%async_computation | async-start | bytes 2228224 | tf_op jit(solution)/shard_map/all_to_all | solution.py:66
  29.6 27.3 %all-to-all-done = bf16[32,136,128]{2,1,0:T(8,128)(2,1)S(1)} async-done(((bf16[32,136,128]{2,1,0:T(8,128)(2,1)}), bf16[32,136,128]{2,1,0:T(8,128)(2,1)S(1)}, u32[]{:S(2)}, u32[]{:S(2)}) %all-to-all-start) | async-done | bytes 1114144 | tf_op jit(solution)/shard_map/all_to_all | solution.py:66
  57.2 0.1 fusion.50
  57.3 1.1 copy-done.2
  58.3 1.3 %select_reduce_fusion = bf16[1024,64]{0,1:T(8,128)(2,1)S(1)} fusion(pred[1024,16]{0,1:T(8,128)(4,1)S(1)} %broadcast_compare_fusion, bf16[1024,128]{1,0:T(8,128)(2,1)S(1)} %bitcast.48, bf16[1024,128]{1,0:T(8,128)(2,1)S(1)} %bitcast.49, bf16[1024,128]{1,0:T(8,128)(2,1)S(1)} %bitcast.50, bf16[1024,128]{1,0:T(8,128)(2,1)S(1)} %bitcast.47, ...), kind=kOutput, calls=%fused_computation | convolution fusion | flops 1079967744 | bytes 2244608 | tf_op jit(solution)/shard_map/dot_general | solution.py:82
  59.6 0.2 convert_element_type.76
  59.9 0.2 reshape.169
  60.2 19.1 %all_to_all.20 = bf16[16,2,2048]{2,1,0:T(2,128)(2,1)S(1)} all-to-all(bf16[16,2,2048]{2,1,0:T(2,128)(2,1)S(1)} %reshape.169), channel_id=1, replica_groups=mesh['wide'=32,'tensor'=16] {'tensor'}, dimensions={0} | all-to-all | bytes 262144 | tf_op jit(solution)/shard_map/all_to_all | solution.py:86
  79.2 0.2 reshape.170
  79.6 0.2 reshape.171
  79.8 11.6 %all_to_all.21 = bf16[16,2,2048]{2,1,0:T(2,128)(2,1)S(1)} all-to-all(bf16[16,2,2048]{2,1,0:T(2,128)(2,1)S(1)} %reshape.171), channel_id=1, replica_groups=mesh['wide'=32,'tensor'=16] {'tensor'}, dimensions={0} | all-to-all | bytes 262144 | tf_op jit(solution)/shard_map/all_to_all | solution.py:91
  91.4 0.2 reshape.172
  91.6 0.2 copy.16
  91.8 0.2 broadcast_in_dim.74
  92.0 1.5 %fusion.12 = bf16[1024,128]{1,0:T(8,128)(2,1)} fusion(bf16[16,64,128]{2,1,0:T(8,128)(2,1)S(1)} %copy-done.3, pred[1024,16]{0,1:T(8,128)(4,1)S(1)} %broadcast_compare_fusion, bf16[1024,64]{0,1:T(8,128)(2,1)S(1)} %broadcast_in_dim.74), kind=kOutput, calls=%fused_computation.12 | convolution fusion | flops 269615104 | bytes 671744 | tf_op jit(solution)/shard_map/dot_general | solution.py:98
  93.5 7.0 %all-to-all-start.3 = ((bf16[32,32,128]{2,1,0:T(8,128)(2,1)}), bf16[32,32,128]{2,1,0:T(8,128)(2,1)S(1)}, u32[]{:S(2)}, u32[]{:S(2)}) async-start(bf16[32,32,128]{2,1,0:T(8,128)(2,1)} %bitcast.13), calls=%async_computation.3 | async-start | bytes 524288 | tf_op jit(solution)/shard_map/all_to_all | solution.py:102
  100.5 5.7 %fusion.51 = f32[512,128]{1,0:T(8,128)S(1)} fusion(bf16[512,8192]{1,0:T(8,128)(2,1)} %all-gather.2.cloned.1.call-done, bf16[8192,128]{1,0:T(8,128)(2,1)S(1)} %copy-done), kind=kOutput, calls=%fused_computation.75 | convolution fusion | flops 1073741824 | bytes 10747904 | tf_op jit(solution)/shard_map/dot_general | solution.py:28
  106.2 6.5 %all-to-all-done.3 = bf16[32,32,128]{2,1,0:T(8,128)(2,1)S(1)} async-done(((bf16[32,32,128]{2,1,0:T(8,128)(2,1)}), bf16[32,32,128]{2,1,0:T(8,128)(2,1)S(1)}, u32[]{:S(2)}, u32[]{:S(2)}) %all-to-all-start.3) | async-done | bytes 262176 | tf_op jit(solution)/shard_map/all_to_all | solution.py:102
  112.8 1.4 %fusion.20 = bf16[512,128]{1,0:T(8,128)(2,1)} fusion(f32[512,128]{1,0:T(8,128)S(1)} %fusion.51, bf16[1024,128]{1,0:T(8,128)(2,1)S(1)} %bitcast.42, s32[512]{0:T(512)S(1)} %convert_add_fusion), kind=kOutput, calls=%fused_computation.18 | convolution fusion | flops 134873088 | bytes 657408 | tf_op jit(solution)/shard_map/dot_general | solution.py:106
  (20 shorter events, 0.6 us)
Async XLA Ops:
  6.5 94.0 %copy-start = (bf16[8192,128]{1,0:T(8,128)(2,1)S(1)}, bf16[8192,128]{1,0:T(8,128)(2,1)}, u32[]{:S(2)}) copy-start(bf16[8192,128]{1,0:T(8,128)(2,1)} %param.7) | copy-start | bytes 6291460
  6.5 4.9 %copy-start.1 = (bf16[512,512]{1,0:T(8,128)(2,1)S(1)}, bf16[512,512]{1,0:T(8,128)(2,1)}, u32[]{:S(2)}) copy-start(bf16[512,512]{1,0:T(8,128)(2,1)} %param.6) | copy-start | bytes 1572868
  6.5 94.0 %all-gather.2.cloned.1.call-start = ((), (), s32[]{:S(2)}) async-start(), calls=%async_computation.4 | async-start | bytes 8912896 | tf_op jit(solution)/shard_map/all_gather | solution.py:27
  15.9 41.1 %all-to-all-start = ((bf16[32,136,128]{2,1,0:T(8,128)(2,1)}), bf16[32,136,128]{2,1,0:T(8,128)(2,1)S(1)}, u32[]{:S(2)}, u32[]{:S(2)}) async-start(bf16[32,136,128]{2,1,0:T(8,128)(2,1)} %pad_dynamic-update-slice_fusion), calls=%async_computation | async-start | bytes 2228224 | tf_op jit(solution)/shard_map/all_to_all | solution.py:66
  57.1 1.2 %copy-start.2 = (bf16[512,16,64]{0,2,1:T(8,128)(2,1)S(1)}, bf16[512,16,64]{0,2,1:T(8,128)(2,1)}, u32[]{:S(2)}) copy-start(bf16[512,16,64]{0,2,1:T(8,128)(2,1)} %param.8) | copy-start | bytes 3145732
  59.8 32.2 %copy-start.3 = (bf16[16,64,128]{2,1,0:T(8,128)(2,1)S(1)}, bf16[16,64,128]{2,1,0:T(8,128)(2,1)}, u32[]{:S(2)}) copy-start(bf16[16,64,128]{2,1,0:T(8,128)(2,1)} %param.9) | copy-start | bytes 786436
  93.5 19.3 %all-to-all-start.3 = ((bf16[32,32,128]{2,1,0:T(8,128)(2,1)}), bf16[32,32,128]{2,1,0:T(8,128)(2,1)S(1)}, u32[]{:S(2)}, u32[]{:S(2)}) async-start(bf16[32,32,128]{2,1,0:T(8,128)(2,1)} %bitcast.13), calls=%async_computation.3 | async-start | bytes 524288 | tf_op jit(solution)/shard_map/all_to_all | solution.py:102
Sparse Core Ops, SparseCore 0:
  9.5 64.1 all-gather.1

commit v7 on v6

--- a/solution.py
+++ b/solution.py
@@ -82,14 +82,32 @@
     all_ranks = jnp.dot(flat_rows, down_matrix, preferred_element_type=jnp.float32)
     all_ranks = all_ranks.reshape(slot_count, present_adapters, rank_dimension)
     partial_value = jnp.sum(jnp.where(selected, all_ranks, 0.0), axis=1)
-    slot_blocks = partial_value.reshape(tensor_count, slot_count // tensor_count, rank_dimension)
+    core = lax.axis_index("tensor") % 2
+    chip_count = tensor_count // 2
+    chip_groups = [list(range(c, tensor_count, 2)) for c in range(2)]
+    pair_swap = [(i, i ^ 1) for i in range(tensor_count)]
+    half = slot_count // 2
+    low_half, high_half = partial_value[:half], partial_value[half:]
+    keep = jnp.where(core == 1, high_half, low_half)
+    send = jnp.where(core == 1, low_half, high_half)
+    pair_sum = keep + lax.ppermute(send, "tensor", pair_swap)
+    slot_blocks = pair_sum.reshape(chip_count, half // chip_count, rank_dimension)
     gathered_blocks = lax.all_to_all(
-        slot_blocks.astype(jnp.bfloat16), "tensor", split_axis=0, concat_axis=0, tiled=True
+        slot_blocks, "tensor", split_axis=0, concat_axis=0, tiled=True,
+        axis_index_groups=chip_groups,
     )
-    own_sum = jnp.sum(gathered_blocks.astype(jnp.float32), axis=0).astype(jnp.bfloat16)
-    spread = jnp.broadcast_to(own_sum[None], (tensor_count,) + own_sum.shape)
-    reduced_rows = lax.all_to_all(spread, "tensor", split_axis=0, concat_axis=0, tiled=True)
-    reduced_rows = reduced_rows.reshape(slot_count, rank_dimension)
+    own_sum = jnp.sum(gathered_blocks, axis=0).astype(jnp.bfloat16)
+    spread = jnp.broadcast_to(own_sum[None], (chip_count,) + own_sum.shape)
+    half_rows = lax.all_to_all(
+        spread, "tensor", split_axis=0, concat_axis=0, tiled=True,
+        axis_index_groups=chip_groups,
+    ).reshape(half, rank_dimension)
+    other_rows = lax.ppermute(half_rows, "tensor", pair_swap)
+    reduced_rows = jnp.where(
+        core == 1,
+        jnp.concatenate([other_rows, half_rows], axis=0),
+        jnp.concatenate([half_rows, other_rows], axis=0),
+    )
 
     expanded_rows = jnp.where(
         selected, reduced_rows[:, None, :], jnp.zeros((), jnp.bfloat16)

time: 121 us -> 126 us (1.041)
  starting transfers between devices: 20.7 us -> 29.4 us
  blocking collectives: 30.7 us -> 24.1 us
    ppermute x0 -> x2, starting transfers between devices: none -> 10.3 us  [the longest x1 5.18 us: body(): other_rows = lax.ppermute(half_rows, 'tensor', pair_swap)]
    all_to_all x2, blocking collectives: 30.7 us -> 24.1 us  [the longest x1 14.5 us: body(): lax.all_to_all(slot_blocks, 'tensor', split_axis=0, concat_axis=0, tiled=...]
    ppermute x0 -> x2, waiting for transfers between devices: none -> 1.84 us  [the longest x1 0.96 us: body(): pair_sum = keep + lax.ppermute(send, 'tensor', pair_swap)]
    all_to_all x1, starting transfers between devices: 6.96 us -> 5.32 us  [body(): lax.all_to_all(adapter_correction, 'wide', split_axis=0, concat_axis=0, t...]
  transfers between devices with their start and end apart: 3 -> 5, of which waited for: 2 -> 4; matrix products, arithmetic and copies ran while one was open for 16% -> 16% of each run, Pallas kernels for 0% -> 0%
where the time goes in v7:
time: 126 us; the launch traced here: 125 us
  waiting for transfers between devices  35.8 us (28%)
  starting transfers between devices  29.4 us (23%)
  blocking collectives  24.1 us (19%)
  between operations  13.6 us (11%)
  matrix products  13.5 us (11%)
  local copies, waits for them, and re-layouts  6.66 us (5%)
  other arithmetic  2.23 us (2%)
    all_to_all x1, waiting for transfers between devices, body(): lax.all_to_all(send_block, 'wide', split_axis=0, concat_axis=0, tiled=True)  27.3 us
    all_to_all x1, blocking collectives, body(): lax.all_to_all(slot_blocks, 'tensor', split_axis=0, concat_axis=0, tiled=...  14.5 us
    all_to_all x1, starting transfers between devices, body(): lax.all_to_all(send_block, 'wide', split_axis=0, concat_axis=0, tiled=True)  13.7 us
    all_to_all x1, blocking collectives, body(): lax.all_to_all(spread, 'tensor', split_axis=0, concat_axis=0, tiled=True,...  9.6 us
    all_to_all x1, waiting for transfers between devices, body(): lax.all_to_all(adapter_correction, 'wide', split_axis=0, concat_axis=0, t...  5.85 us
    dot_general x1, matrix products, body(): jnp.dot(gathered, key_value_weight, preferred_element_type=jnp.float32)  5.7 us
    all_to_all x1, starting transfers between devices, body(): lax.all_to_all(adapter_correction, 'wide', split_axis=0, concat_axis=0, t...  5.32 us
    ppermute x1, starting transfers between devices, body(): other_rows = lax.ppermute(half_rows, 'tensor', pair_swap)  5.18 us
  transfers between devices with their start and end apart: 5, of which 4 were waited for; matrix products, arithmetic and copies ran while one was open for 16% of the time, Pallas kernels for 0%

profile of v7, /device:TPU:1, one launch (start us, length us, event | category | flops | bytes accessed | tf_op | source)
XLA Modules:
  0.0 125.2 jit_solution(432040595521652633)
XLA Ops:
  6.5 0.7 all-gather.2.cloned.1.call-update
  7.3 1.0 select_reduce_fusion.1
  8.3 0.3 fusion.21
  8.6 0.6 fusion.3
  9.3 1.4 %fusion.15 = bf16[1024,128]{1,0:T(8,128)(2,1)S(1)} fusion(s32[512]{0:T(512)S(1)} %convert_add_fusion, bf16[512,512]{1,0:T(8,128)(2,1)} %param.6), kind=kOutput, calls=%fused_computation.13 | convolution fusion | flops 134873088 | bytes 395264 | tf_op jit(solution)/shard_map/dot_general | solution.py:56
  10.7 0.8 constant_dynamic-update-slice_fusion.3
  11.4 0.5 fusion.16
  11.9 0.8 constant_dynamic-update-slice_fusion.2
  12.7 0.5 fusion.17
  13.2 0.8 constant_dynamic-update-slice_fusion.1
  13.9 0.5 fusion.18
  14.4 0.8 constant_dynamic-update-slice_fusion
  15.2 0.7 pad_dynamic-update-slice_fusion
  15.9 13.7 %all-to-all-start = ((bf16[32,136,128]{2,1,0:T(8,128)(2,1)}), bf16[32,136,128]{2,1,0:T(8,128)(2,1)S(1)}, u32[]{:S(2)}, u32[]{:S(2)}) async-start(bf16[32,136,128]{2,1,0:T(8,128)(2,1)} %pad_dynamic-update-slice_fusion), calls=%async_computation | async-start | bytes 2228224 | tf_op jit(solution)/shard_map/all_to_all | solution.py:66
  29.6 27.3 %all-to-all-done = bf16[32,136,128]{2,1,0:T(8,128)(2,1)S(1)} async-done(((bf16[32,136,128]{2,1,0:T(8,128)(2,1)}), bf16[32,136,128]{2,1,0:T(8,128)(2,1)S(1)}, u32[]{:S(2)}, u32[]{:S(2)}) %all-to-all-start) | async-done | bytes 1114144 | tf_op jit(solution)/shard_map/all_to_all | solution.py:66
  57.3 1.1 copy-done.2
  58.3 1.3 %select_reduce_fusion = f32[1024,64]{0,1:T(8,128)S(1)} fusion(pred[1024,16]{0,1:T(8,128)(4,1)S(1)} %broadcast_compare_fusion, bf16[1024,128]{1,0:T(8,128)(2,1)S(1)} %bitcast.48, bf16[1024,128]{1,0:T(8,128)(2,1)S(1)} %bitcast.49, bf16[1024,128]{1,0:T(8,128)(2,1)S(1)} %bitcast.50, bf16[1024,128]{1,0:T(8,128)(2,1)S(1)} %bitcast.47, ...), kind=kOutput, calls=%fused_computation | convolution fusion | flops 1079967744 | bytes 2375680 | tf_op jit(solution)/shard_map/dot_general | solution.py:82
  59.7 5.1 %collective-permute-start = (f32[512,64]{0,1:T(8,128)S(1)}, f32[512,64]{0,1:T(8,128)S(1)}, u32[]{:S(2)}, u32[]{:S(2)}) collective-permute-start(f32[512,64]{0,1:T(8,128)S(1)} %slice_select_fusion), channel_id=1, source_target_pairs={{0,1},{1,0},{2,3},{3,2},{4,5},{5,4},{6,7},{7,6},{8,9},{9,8},{10,11... | collective-permute-start | bytes 393224 | tf_op jit(solution)/shard_map/ppermute | solution.py:93
  64.8 1.0 collective-permute-done
  66.0 0.2 reshape.207
  66.2 14.5 %all_to_all.20 = f32[8,1,4096]{2,1,0:T(1,128)S(1)} all-to-all(f32[8,1,4096]{2,1,0:T(1,128)S(1)} %reshape.207), channel_id=1, replica_groups={{0,2,4,6,8,10,12,14},{1,3,5,7,9,11,13,15},{16,18,20,22,24,26,28,30},{17..., dimensions={0} | all-to-all | bytes 262144 | tf_op jit(solution)/shard_map/all_to_all | solution.py:95
  80.6 0.5 broadcast.151
  81.1 1.0 reduce.6
  82.2 0.2 reshape.209
  82.4 9.6 %all_to_all.21 = bf16[8,2,2048]{2,1,0:T(2,128)(2,1)S(1)} all-to-all(bf16[8,2,2048]{2,1,0:T(2,128)(2,1)S(1)} %reshape.209), channel_id=1, replica_groups={{0,2,4,6,8,10,12,14},{1,3,5,7,9,11,13,15},{16,18,20,22,24,26,28,30},{17..., dimensions={0} | all-to-all | bytes 131072 | tf_op jit(solution)/shard_map/all_to_all | solution.py:101
  92.4 5.2 %collective-permute-start.1 = (bf16[512,64]{0,1:T(8,128)(2,1)S(1)}, bf16[512,64]{0,1:T(8,128)(2,1)S(1)}, u32[]{:S(2)}, u32[]{:S(2)}) collective-permute-start(bf16[512,64]{0,1:T(8,128)(2,1)S(1)} %reshape.193), channel_id=1, source_target_pairs={{0,1},{1,0},{2,3},{3,2},{4,5},{5,4},{6,7},{7,6},{8,9},{9,8},{10,11... | collective-permute-start | bytes 196616 | tf_op jit(solution)/shard_map/ppermute | solution.py:105
  97.6 0.9 collective-permute-done.1
  98.5 1.5 %fusion.12 = bf16[1024,128]{1,0:T(8,128)(2,1)} fusion(bf16[16,64,128]{2,1,0:T(8,128)(2,1)S(1)} %copy-done.3, pred[1024,16]{0,1:T(8,128)(4,1)S(1)} %broadcast_compare_fusion, bf16[1024,64]{0,1:T(8,128)(2,1)S(1)} %maximum_select_fusion), kind=kOutput, calls=%fused_computation.12 | convolution fusion | flops 269615104 | bytes 671744 | tf_op jit(solution)/shard_map/dot_general | solution.py:116
  100.0 5.3 %all-to-all-start.3 = ((bf16[32,32,128]{2,1,0:T(8,128)(2,1)}), bf16[32,32,128]{2,1,0:T(8,128)(2,1)S(1)}, u32[]{:S(2)}, u32[]{:S(2)}) async-start(bf16[32,32,128]{2,1,0:T(8,128)(2,1)} %bitcast.13), calls=%async_computation.3 | async-start | bytes 524288 | tf_op jit(solution)/shard_map/all_to_all | solution.py:120
  105.4 5.7 %fusion.51 = f32[512,128]{1,0:T(8,128)S(1)} fusion(bf16[512,8192]{1,0:T(8,128)(2,1)} %all-gather.2.cloned.1.call-done, bf16[8192,128]{1,0:T(8,128)(2,1)S(1)} %copy-done), kind=kOutput, calls=%fused_computation.78 | convolution fusion | flops 1073741824 | bytes 10747904 | tf_op jit(solution)/shard_map/dot_general | solution.py:28
  111.1 5.9 %all-to-all-done.3 = bf16[32,32,128]{2,1,0:T(8,128)(2,1)S(1)} async-done(((bf16[32,32,128]{2,1,0:T(8,128)(2,1)}), bf16[32,32,128]{2,1,0:T(8,128)(2,1)S(1)}, u32[]{:S(2)}, u32[]{:S(2)}) %all-to-all-start.3) | async-done | bytes 262176 | tf_op jit(solution)/shard_map/all_to_all | solution.py:120
  116.9 1.4 %fusion.20 = bf16[512,128]{1,0:T(8,128)(2,1)} fusion(f32[512,128]{1,0:T(8,128)S(1)} %fusion.51, bf16[1024,128]{1,0:T(8,128)(2,1)S(1)} %bitcast.42, s32[512]{0:T(512)S(1)} %convert_add_fusion), kind=kOutput, calls=%fused_computation.18 | convolution fusion | flops 134873088 | bytes 657408 | tf_op jit(solution)/shard_map/dot_general | solution.py:124
  (29 shorter events, 1.2 us)
Async XLA Ops:
  6.5 98.8 %copy-start = (bf16[8192,128]{1,0:T(8,128)(2,1)S(1)}, bf16[8192,128]{1,0:T(8,128)(2,1)}, u32[]{:S(2)}) copy-start(bf16[8192,128]{1,0:T(8,128)(2,1)} %param.7) | copy-start | bytes 6291460
  6.5 4.9 %copy-start.1 = (bf16[512,512]{1,0:T(8,128)(2,1)S(1)}, bf16[512,512]{1,0:T(8,128)(2,1)}, u32[]{:S(2)}) copy-start(bf16[512,512]{1,0:T(8,128)(2,1)} %param.6) | copy-start | bytes 1572868
  6.5 98.8 %all-gather.2.cloned.1.call-start = ((), (), s32[]{:S(2)}) async-start(), calls=%async_computation.4 | async-start | bytes 8912896 | tf_op jit(solution)/shard_map/all_gather | solution.py:27
  15.9 41.1 %all-to-all-start = ((bf16[32,136,128]{2,1,0:T(8,128)(2,1)}), bf16[32,136,128]{2,1,0:T(8,128)(2,1)S(1)}, u32[]{:S(2)}, u32[]{:S(2)}) async-start(bf16[32,136,128]{2,1,0:T(8,128)(2,1)} %pad_dynamic-update-slice_fusion), calls=%async_computation | async-start | bytes 2228224 | tf_op jit(solution)/shard_map/all_to_all | solution.py:66
  57.1 1.2 copy-start.2
  59.7 38.8 %copy-start.3 = (bf16[16,64,128]{2,1,0:T(8,128)(2,1)S(1)}, bf16[16,64,128]{2,1,0:T(8,128)(2,1)}, u32[]{:S(2)}) copy-start(bf16[16,64,128]{2,1,0:T(8,128)(2,1)} %param.9) | copy-start | bytes 786436
  59.7 6.1 %collective-permute-start = (f32[512,64]{0,1:T(8,128)S(1)}, f32[512,64]{0,1:T(8,128)S(1)}, u32[]{:S(2)}, u32[]{:S(2)}) collective-permute-start(f32[512,64]{0,1:T(8,128)S(1)} %slice_select_fusion), channel_id=1, source_target_pairs={{0,1},{1,0},{2,3},{3,2},{4,5},{5,4},{6,7},{7,6},{8,9},{9,8},{10,11... | collective-permute-start | bytes 393224 | tf_op jit(solution)/shard_map/ppermute | solution.py:93
  92.4 6.1 %collective-permute-start.1 = (bf16[512,64]{0,1:T(8,128)(2,1)S(1)}, bf16[512,64]{0,1:T(8,128)(2,1)S(1)}, u32[]{:S(2)}, u32[]{:S(2)}) collective-permute-start(bf16[512,64]{0,1:T(8,128)(2,1)S(1)} %reshape.193), channel_id=1, source_target_pairs={{0,1},{1,0},{2,3},{3,2},{4,5},{5,4},{6,7},{7,6},{8,9},{9,8},{10,11... | collective-permute-start | bytes 196616 | tf_op jit(solution)/shard_map/ppermute | solution.py:105
  100.0 16.9 %all-to-all-start.3 = ((bf16[32,32,128]{2,1,0:T(8,128)(2,1)}), bf16[32,32,128]{2,1,0:T(8,128)(2,1)S(1)}, u32[]{:S(2)}, u32[]{:S(2)}) async-start(bf16[32,32,128]{2,1,0:T(8,128)(2,1)} %bitcast.13), calls=%async_computation.3 | async-start | bytes 524288 | tf_op jit(solution)/shard_map/all_to_all | solution.py:120
Sparse Core Ops, SparseCore 0:
  9.5 64.1 all-gather.1

commit v8 on v5

--- a/solution.py
+++ b/solution.py
@@ -51,13 +51,12 @@
     local_code = jnp.broadcast_to(
         (local_index + 1).astype(jnp.bfloat16)[:, None], (row_count, lane)
     )
-    pieces = []
-    for tile in range(lane_tiles):
-        placed = jnp.dot(
-            placement, tokens[:, tile * lane : (tile + 1) * lane],
-            preferred_element_type=jnp.float32,
-        ).astype(jnp.bfloat16)
-        pieces.append(placed.reshape(wide_count, capacity, lane))
+    placement_blocks = placement.reshape(wide_count, capacity, row_count)
+    token_tiles = tokens.reshape(row_count, lane_tiles, lane)
+    placed = jnp.einsum(
+        "dcr,rjl->djcl", placement_blocks, token_tiles, preferred_element_type=jnp.float32
+    ).astype(jnp.bfloat16)
+    pieces = [placed.reshape(wide_count, lane_tiles * capacity, lane)]
     placed_code = jnp.dot(placement, local_code, preferred_element_type=jnp.float32)
     slot_code = placed_code[:, 0].astype(jnp.bfloat16).reshape(wide_count, 1, capacity)
     pieces.append(jnp.pad(slot_code, ((0, 0), (0, info_rows - 1), (0, lane - capacity))))

time: 127 us -> 124 us (0.976)
  local copies, waits for them, and re-layouts: 7.38 us -> 3.54 us
    unnamed x17 -> x11, local copies, waits for them, and re-layouts: 5.23 us -> 2.09 us
    dot_general x4 -> x1, matrix products: 2.76 us -> 1.8 us  [body(): jnp.einsum('dcr,rjl->djcl', placement_blocks, token_tiles, preferred_elem...]
  transfers between devices with their start and end apart: 3 -> 3, of which waited for: 2 -> 2; matrix products, arithmetic and copies ran while one was open for 17% -> 14% of each run, Pallas kernels for 0% -> 0%
where the time goes in v8:
time: 124 us; the launch traced here: 123 us
  blocking collectives  34.7 us (28%)
  waiting for transfers between devices  34.6 us (28%)
  starting transfers between devices  21 us (17%)
  between operations  13.6 us (11%)
  matrix products  12.5 us (10%)
  other arithmetic  3.62 us (3%)
  local copies, waits for them, and re-layouts  3.54 us (3%)
    all_to_all x1, waiting for transfers between devices, body(): lax.all_to_all(send_block, 'wide', split_axis=0, concat_axis=0, tiled=True)  27.3 us
    all_to_all x1, blocking collectives, body(): lax.all_to_all(slot_blocks, 'tensor', split_axis=0, concat_axis=0, tiled=...  22.3 us
    all_to_all x1, starting transfers between devices, body(): lax.all_to_all(send_block, 'wide', split_axis=0, concat_axis=0, tiled=True)  13.7 us
    all_to_all x1, blocking collectives, body(): lax.all_to_all(spread, 'tensor', split_axis=0, concat_axis=0, tiled=True)  12.4 us
    all_to_all x1, starting transfers between devices, body(): lax.all_to_all(adapter_correction, 'wide', split_axis=0, concat_axis=0, t...  7.24 us
    all_to_all x1, waiting for transfers between devices, body(): lax.all_to_all(adapter_correction, 'wide', split_axis=0, concat_axis=0, t...  6.54 us
    dot_general x1, matrix products, body(): jnp.dot(gathered, key_value_weight, preferred_element_type=jnp.float32)  5.7 us
  transfers between devices with their start and end apart: 3, of which 2 were waited for; matrix products, arithmetic and copies ran while one was open for 14% of the time, Pallas kernels for 0%

profile of v8, /device:TPU:1, one launch (start us, length us, event | category | flops | bytes accessed | tf_op | source)
XLA Modules:
  0.0 123.5 jit_solution(6068988658767693155)
XLA Ops:
  6.5 0.7 all-gather.2.cloned.1.call-update
  7.3 0.9 select_reduce_fusion.1
  8.2 0.3 fusion.20
  8.5 0.6 fusion.4
  9.1 0.1 convert_element_type.70
  9.2 1.8 %fusion.9 = bf16[32,32,4,128]{3,1,2,0:T(8,128)(2,1)S(1)} fusion(s32[512]{0:T(512)S(1)} %convert_add_fusion, s32[32,32]{1,0:T(8,128)S(1)} %multiply_add_fusion, bf16[512,512]{1,0:T(8,128)(2,1)} %param.6), kind=kOutput, calls=%fused_computation.12 | convolution fusion | flops 537919488 | bytes 1579008 | tf_op jit(solution)/shard_map/dcr,rjl->djcl/dot_general | solution.py:56
  11.0 1.2 fusion.21
  12.2 13.7 %all-to-all-start = ((bf16[32,136,128]{2,1,0:T(8,128)(2,1)}), bf16[32,136,128]{2,1,0:T(8,128)(2,1)S(1)}, u32[]{:S(2)}, u32[]{:S(2)}) async-start(bf16[32,136,128]{2,1,0:T(8,128)(2,1)} %fusion.21), calls=%async_computation | async-start | bytes 2228224 | tf_op jit(solution)/shard_map/all_to_all | solution.py:65
  25.9 27.3 %all-to-all-done = bf16[32,136,128]{2,1,0:T(8,128)(2,1)S(1)} async-done(((bf16[32,136,128]{2,1,0:T(8,128)(2,1)}), bf16[32,136,128]{2,1,0:T(8,128)(2,1)S(1)}, u32[]{:S(2)}, u32[]{:S(2)}) %all-to-all-start) | async-done | bytes 1114144 | tf_op jit(solution)/shard_map/all_to_all | solution.py:65
  53.3 0.1 fusion.38
  53.3 0.1 reshape.172
  53.4 0.1 broadcast_compare_fusion
  53.5 0.1 fusion.45
  53.6 1.1 copy-done.1
  54.7 1.3 %select_reduce_fusion = f32[1024,64]{0,1:T(8,128)S(1)} fusion(pred[1024,16]{0,1:T(8,128)(4,1)S(1)} %broadcast_compare_fusion, bf16[1024,128]{1,0:T(8,128)(2,1)S(1)} %bitcast.61, bf16[1024,128]{1,0:T(8,128)(2,1)S(1)} %bitcast.62, bf16[1024,128]{1,0:T(8,128)(2,1)S(1)} %bitcast.63, bf16[1024,128]{1,0:T(8,128)(2,1)S(1)} %bitcast.60, ...), kind=kOutput, calls=%fused_computation | convolution fusion | flops 1079967744 | bytes 2375680 | tf_op jit(solution)/shard_map/dot_general | solution.py:81
  55.9 0.1 reshape.169
  56.1 0.2 copy.29
  56.3 0.3 reshape.185
  56.6 22.3 %all_to_all.20 = f32[16,1,4096]{2,1,0:T(1,128)S(1)} all-to-all(f32[16,1,4096]{2,1,0:T(1,128)S(1)} %reshape.185), channel_id=1, replica_groups=mesh['wide'=32,'tensor'=16] {'tensor'}, dimensions={0} | all-to-all | bytes 524288 | tf_op jit(solution)/shard_map/all_to_all | solution.py:85
  78.9 0.5 broadcast.168
  79.4 1.3 %reduce.6 = f32[16,4096]{1,0:T(8,128)S(1)} reduce(f32[16,1,4096]{2,1,0:T(1,128)S(1)} %all_to_all.20, f32[]{:T(128)} %broadcast.168), dimensions={1}, to_apply=%all_to_all.13.reduce_sub_computation | reduce | bytes 524292 | tf_op jit(solution)/shard_map/all_to_all | solution.py:85
  80.7 0.2 reshape.186
  81.0 0.2 reshape.187
  81.2 12.4 %all_to_all.21 = bf16[16,2,2048]{2,1,0:T(2,128)(2,1)S(1)} all-to-all(bf16[16,2,2048]{2,1,0:T(2,128)(2,1)S(1)} %reshape.187), channel_id=1, replica_groups=mesh['wide'=32,'tensor'=16] {'tensor'}, dimensions={0} | all-to-all | bytes 262144 | tf_op jit(solution)/shard_map/all_to_all | solution.py:88
  93.6 0.2 reshape.188
  93.8 0.2 copy.21
  94.0 0.2 broadcast_in_dim.74
  94.2 1.5 %fusion.15 = bf16[1024,128]{1,0:T(8,128)(2,1)} fusion(bf16[16,64,128]{2,1,0:T(8,128)(2,1)S(1)} %copy-done.2, pred[1024,16]{0,1:T(8,128)(4,1)S(1)} %broadcast_compare_fusion, bf16[1024,64]{0,1:T(8,128)(2,1)S(1)} %broadcast_in_dim.74), kind=kOutput, calls=%fused_computation.14 | convolution fusion | flops 269615104 | bytes 671744 | tf_op jit(solution)/shard_map/dot_general | solution.py:95
  95.7 7.2 %all-to-all-start.3 = ((bf16[32,32,128]{2,1,0:T(8,128)(2,1)}), bf16[32,32,128]{2,1,0:T(8,128)(2,1)S(1)}, u32[]{:S(2)}, u32[]{:S(2)}) async-start(bf16[32,32,128]{2,1,0:T(8,128)(2,1)} %bitcast.14), calls=%async_computation.3 | async-start | bytes 524288 | tf_op jit(solution)/shard_map/all_to_all | solution.py:99
  103.0 5.7 %fusion.46 = f32[512,128]{1,0:T(8,128)S(1)} fusion(bf16[512,8192]{1,0:T(8,128)(2,1)} %all-gather.2.cloned.1.call-done, bf16[8192,128]{1,0:T(8,128)(2,1)S(1)} %copy-done), kind=kOutput, calls=%fused_computation.66 | convolution fusion | flops 1073741824 | bytes 10747904 | tf_op jit(solution)/shard_map/dot_general | solution.py:28
  108.7 6.5 %all-to-all-done.3 = bf16[32,32,128]{2,1,0:T(8,128)(2,1)S(1)} async-done(((bf16[32,32,128]{2,1,0:T(8,128)(2,1)}), bf16[32,32,128]{2,1,0:T(8,128)(2,1)S(1)}, u32[]{:S(2)}, u32[]{:S(2)}) %all-to-all-start.3) | async-done | bytes 262176 | tf_op jit(solution)/shard_map/all_to_all | solution.py:99
  115.3 1.4 %fusion.19 = bf16[512,128]{1,0:T(8,128)(2,1)} fusion(f32[512,128]{1,0:T(8,128)S(1)} %fusion.46, bf16[1024,128]{1,0:T(8,128)(2,1)S(1)} %bitcast.59, s32[512]{0:T(512)S(1)} %convert_add_fusion), kind=kOutput, calls=%fused_computation.16 | convolution fusion | flops 134873088 | bytes 657408 | tf_op jit(solution)/shard_map/dot_general | solution.py:103
  (14 shorter events, 0.2 us)
Async XLA Ops:
  6.5 96.5 %copy-start = (bf16[8192,128]{1,0:T(8,128)(2,1)S(1)}, bf16[8192,128]{1,0:T(8,128)(2,1)}, u32[]{:S(2)}) copy-start(bf16[8192,128]{1,0:T(8,128)(2,1)} %param.7) | copy-start | bytes 6291460
  6.5 96.5 %all-gather.2.cloned.1.call-start = ((), (), s32[]{:S(2)}) async-start(), calls=%async_computation.4 | async-start | bytes 8912896 | tf_op jit(solution)/shard_map/all_gather | solution.py:27
  12.2 41.1 %all-to-all-start = ((bf16[32,136,128]{2,1,0:T(8,128)(2,1)}), bf16[32,136,128]{2,1,0:T(8,128)(2,1)S(1)}, u32[]{:S(2)}, u32[]{:S(2)}) async-start(bf16[32,136,128]{2,1,0:T(8,128)(2,1)} %fusion.21), calls=%async_computation | async-start | bytes 2228224 | tf_op jit(solution)/shard_map/all_to_all | solution.py:65
  53.4 1.2 copy-start.1
  78.9 15.4 %copy-start.2 = (bf16[16,64,128]{2,1,0:T(8,128)(2,1)S(1)}, bf16[16,64,128]{2,1,0:T(8,128)(2,1)}, u32[]{:S(2)}) copy-start(bf16[16,64,128]{2,1,0:T(8,128)(2,1)} %param.9) | copy-start | bytes 786436
  95.7 19.5 %all-to-all-start.3 = ((bf16[32,32,128]{2,1,0:T(8,128)(2,1)}), bf16[32,32,128]{2,1,0:T(8,128)(2,1)S(1)}, u32[]{:S(2)}, u32[]{:S(2)}) async-start(bf16[32,32,128]{2,1,0:T(8,128)(2,1)} %bitcast.14), calls=%async_computation.3 | async-start | bytes 524288 | tf_op jit(solution)/shard_map/all_to_all | solution.py:99
Sparse Core Ops, SparseCore 0:
  9.5 66.6 all-gather.1

commit v9 on v7

--- a/solution.py
+++ b/solution.py
@@ -51,13 +51,12 @@
     local_code = jnp.broadcast_to(
         (local_index + 1).astype(jnp.bfloat16)[:, None], (row_count, lane)
     )
-    pieces = []
-    for tile in range(lane_tiles):
-        placed = jnp.dot(
-            placement, tokens[:, tile * lane : (tile + 1) * lane],
-            preferred_element_type=jnp.float32,
-        ).astype(jnp.bfloat16)
-        pieces.append(placed.reshape(wide_count, capacity, lane))
+    placement_blocks = placement.reshape(wide_count, capacity, row_count)
+    token_tiles = tokens.reshape(row_count, lane_tiles, lane)
+    placed = jnp.einsum(
+        "dcr,rjl->djcl", placement_blocks, token_tiles, preferred_element_type=jnp.float32
+    ).astype(jnp.bfloat16)
+    pieces = [placed.reshape(wide_count, lane_tiles * capacity, lane)]
     placed_code = jnp.dot(placement, local_code, preferred_element_type=jnp.float32)
     slot_code = placed_code[:, 0].astype(jnp.bfloat16).reshape(wide_count, 1, capacity)
     pieces.append(jnp.pad(slot_code, ((0, 0), (0, info_rows - 1), (0, lane - capacity))))

time: 126 us -> 124 us (0.984)
  local copies, waits for them, and re-layouts: 6.66 us -> 2.82 us
  starting transfers between devices: 29.4 us -> 31.2 us
    unnamed x17 -> x11, local copies, waits for them, and re-layouts: 4.8 us -> 1.66 us
    all_to_all x1, starting transfers between devices: 5.32 us -> 7.18 us  [body(): lax.all_to_all(adapter_correction, 'wide', split_axis=0, concat_axis=0, t...]
    dot_general x4 -> x1, matrix products: 2.76 us -> 1.8 us  [body(): jnp.einsum('dcr,rjl->djcl', placement_blocks, token_tiles, preferred_elem...]
  transfers between devices with their start and end apart: 5 -> 5, of which waited for: 4 -> 4; matrix products, arithmetic and copies ran while one was open for 16% -> 13% of each run, Pallas kernels for 0% -> 0%
where the time goes in v9:
time: 124 us; the launch traced here: 123 us
  waiting for transfers between devices  35.8 us (29%)
  starting transfers between devices  31.2 us (25%)
  blocking collectives  24.1 us (19%)
  between operations  13.6 us (11%)
  matrix products  12.5 us (10%)
  other arithmetic  3.36 us (3%)
  local copies, waits for them, and re-layouts  2.82 us (2%)
    all_to_all x1, waiting for transfers between devices, body(): lax.all_to_all(send_block, 'wide', split_axis=0, concat_axis=0, tiled=True)  27.3 us
    all_to_all x1, blocking collectives, body(): lax.all_to_all(slot_blocks, 'tensor', split_axis=0, concat_axis=0, tiled=...  14.5 us
    all_to_all x1, starting transfers between devices, body(): lax.all_to_all(send_block, 'wide', split_axis=0, concat_axis=0, tiled=True)  13.7 us
    all_to_all x1, blocking collectives, body(): lax.all_to_all(spread, 'tensor', split_axis=0, concat_axis=0, tiled=True,...  9.6 us
    all_to_all x1, starting transfers between devices, body(): lax.all_to_all(adapter_correction, 'wide', split_axis=0, concat_axis=0, t...  7.18 us
    all_to_all x1, waiting for transfers between devices, body(): lax.all_to_all(adapter_correction, 'wide', split_axis=0, concat_axis=0, t...  5.85 us
    dot_general x1, matrix products, body(): jnp.dot(gathered, key_value_weight, preferred_element_type=jnp.float32)  5.7 us
    ppermute x1, starting transfers between devices, body(): other_rows = lax.ppermute(half_rows, 'tensor', pair_swap)  5.19 us
  transfers between devices with their start and end apart: 5, of which 4 were waited for; matrix products, arithmetic and copies ran while one was open for 13% of the time, Pallas kernels for 0%

profile of v9, /device:TPU:1, one launch (start us, length us, event | category | flops | bytes accessed | tf_op | source)
XLA Modules:
  0.0 123.4 jit_solution(18204273253999781648)
XLA Ops:
  6.5 0.7 all-gather.2.cloned.1.call-update
  7.3 0.9 select_reduce_fusion.1
  8.2 0.3 fusion.20
  8.5 0.6 fusion.4
  9.1 0.1 convert_element_type.70
  9.2 1.8 %fusion.9 = bf16[32,32,4,128]{3,1,2,0:T(8,128)(2,1)S(1)} fusion(s32[512]{0:T(512)S(1)} %convert_add_fusion, s32[32,32]{1,0:T(8,128)S(1)} %multiply_add_fusion, bf16[512,512]{1,0:T(8,128)(2,1)} %param.6), kind=kOutput, calls=%fused_computation.12 | convolution fusion | flops 537919488 | bytes 1579008 | tf_op jit(solution)/shard_map/dcr,rjl->djcl/dot_general | solution.py:56
  11.0 1.2 fusion.21
  12.2 13.7 %all-to-all-start = ((bf16[32,136,128]{2,1,0:T(8,128)(2,1)}), bf16[32,136,128]{2,1,0:T(8,128)(2,1)S(1)}, u32[]{:S(2)}, u32[]{:S(2)}) async-start(bf16[32,136,128]{2,1,0:T(8,128)(2,1)} %fusion.21), calls=%async_computation | async-start | bytes 2228224 | tf_op jit(solution)/shard_map/all_to_all | solution.py:65
  26.0 27.3 %all-to-all-done = bf16[32,136,128]{2,1,0:T(8,128)(2,1)S(1)} async-done(((bf16[32,136,128]{2,1,0:T(8,128)(2,1)}), bf16[32,136,128]{2,1,0:T(8,128)(2,1)S(1)}, u32[]{:S(2)}, u32[]{:S(2)}) %all-to-all-start) | async-done | bytes 1114144 | tf_op jit(solution)/shard_map/all_to_all | solution.py:65
  53.5 0.1 fusion.45
  53.6 1.1 copy-done.1
  54.7 1.3 %select_reduce_fusion = f32[1024,64]{0,1:T(8,128)S(1)} fusion(pred[1024,16]{0,1:T(8,128)(4,1)S(1)} %broadcast_compare_fusion, bf16[1024,128]{1,0:T(8,128)(2,1)S(1)} %bitcast.61, bf16[1024,128]{1,0:T(8,128)(2,1)S(1)} %bitcast.62, bf16[1024,128]{1,0:T(8,128)(2,1)S(1)} %bitcast.63, bf16[1024,128]{1,0:T(8,128)(2,1)S(1)} %bitcast.60, ...), kind=kOutput, calls=%fused_computation | convolution fusion | flops 1079967744 | bytes 2375680 | tf_op jit(solution)/shard_map/dot_general | solution.py:81
  56.0 5.1 %collective-permute-start = (f32[512,64]{0,1:T(8,128)S(1)}, f32[512,64]{0,1:T(8,128)S(1)}, u32[]{:S(2)}, u32[]{:S(2)}) collective-permute-start(f32[512,64]{0,1:T(8,128)S(1)} %slice_select_fusion), channel_id=1, source_target_pairs={{0,1},{1,0},{2,3},{3,2},{4,5},{5,4},{6,7},{7,6},{8,9},{9,8},{10,11... | collective-permute-start | bytes 393224 | tf_op jit(solution)/shard_map/ppermute | solution.py:92
  61.1 1.0 collective-permute-done
  62.1 0.1 reshape.202
  62.2 0.2 reshape.219
  62.4 14.5 %all_to_all.20 = f32[8,1,4096]{2,1,0:T(1,128)S(1)} all-to-all(f32[8,1,4096]{2,1,0:T(1,128)S(1)} %reshape.219), channel_id=1, replica_groups={{0,2,4,6,8,10,12,14},{1,3,5,7,9,11,13,15},{16,18,20,22,24,26,28,30},{17..., dimensions={0} | all-to-all | bytes 262144 | tf_op jit(solution)/shard_map/all_to_all | solution.py:94
  76.9 0.5 broadcast.173
  77.5 1.0 reduce.6
  78.4 0.1 reshape.220
  78.6 0.2 reshape.221
  78.7 9.6 %all_to_all.21 = bf16[8,2,2048]{2,1,0:T(2,128)(2,1)S(1)} all-to-all(bf16[8,2,2048]{2,1,0:T(2,128)(2,1)S(1)} %reshape.221), channel_id=1, replica_groups={{0,2,4,6,8,10,12,14},{1,3,5,7,9,11,13,15},{16,18,20,22,24,26,28,30},{17..., dimensions={0} | all-to-all | bytes 131072 | tf_op jit(solution)/shard_map/all_to_all | solution.py:100
  88.3 0.1 reshape.222
  88.5 0.1 copy.21
  88.6 0.1 reshape.203
  88.7 5.2 %collective-permute-start.1 = (bf16[512,64]{0,1:T(8,128)(2,1)S(1)}, bf16[512,64]{0,1:T(8,128)(2,1)S(1)}, u32[]{:S(2)}, u32[]{:S(2)}) collective-permute-start(bf16[512,64]{0,1:T(8,128)(2,1)S(1)} %reshape.203), channel_id=1, source_target_pairs={{0,1},{1,0},{2,3},{3,2},{4,5},{5,4},{6,7},{7,6},{8,9},{9,8},{10,11... | collective-permute-start | bytes 196616 | tf_op jit(solution)/shard_map/ppermute | solution.py:104
  93.9 0.9 collective-permute-done.1
  94.9 1.5 %fusion.15 = bf16[1024,128]{1,0:T(8,128)(2,1)} fusion(bf16[16,64,128]{2,1,0:T(8,128)(2,1)S(1)} %copy-done.2, pred[1024,16]{0,1:T(8,128)(4,1)S(1)} %broadcast_compare_fusion, bf16[1024,64]{0,1:T(8,128)(2,1)S(1)} %maximum_select_fusion), kind=kOutput, calls=%fused_computation.14 | convolution fusion | flops 269615104 | bytes 671744 | tf_op jit(solution)/shard_map/dot_general | solution.py:115
  96.3 7.2 %all-to-all-start.3 = ((bf16[32,32,128]{2,1,0:T(8,128)(2,1)}), bf16[32,32,128]{2,1,0:T(8,128)(2,1)S(1)}, u32[]{:S(2)}, u32[]{:S(2)}) async-start(bf16[32,32,128]{2,1,0:T(8,128)(2,1)} %bitcast.14), calls=%async_computation.3 | async-start | bytes 524288 | tf_op jit(solution)/shard_map/all_to_all | solution.py:119
  103.6 5.7 %fusion.46 = f32[512,128]{1,0:T(8,128)S(1)} fusion(bf16[512,8192]{1,0:T(8,128)(2,1)} %all-gather.2.cloned.1.call-done, bf16[8192,128]{1,0:T(8,128)(2,1)S(1)} %copy-done), kind=kOutput, calls=%fused_computation.69 | convolution fusion | flops 1073741824 | bytes 10747904 | tf_op jit(solution)/shard_map/dot_general | solution.py:28
  109.3 5.9 %all-to-all-done.3 = bf16[32,32,128]{2,1,0:T(8,128)(2,1)S(1)} async-done(((bf16[32,32,128]{2,1,0:T(8,128)(2,1)}), bf16[32,32,128]{2,1,0:T(8,128)(2,1)S(1)}, u32[]{:S(2)}, u32[]{:S(2)}) %all-to-all-start.3) | async-done | bytes 262176 | tf_op jit(solution)/shard_map/all_to_all | solution.py:119
  115.1 1.4 %fusion.19 = bf16[512,128]{1,0:T(8,128)(2,1)} fusion(f32[512,128]{1,0:T(8,128)S(1)} %fusion.46, bf16[1024,128]{1,0:T(8,128)(2,1)S(1)} %bitcast.59, s32[512]{0:T(512)S(1)} %convert_add_fusion), kind=kOutput, calls=%fused_computation.16 | convolution fusion | flops 134873088 | bytes 657408 | tf_op jit(solution)/shard_map/dot_general | solution.py:123
  (21 shorter events, 0.5 us)
Async XLA Ops:
  6.5 97.0 %copy-start = (bf16[8192,128]{1,0:T(8,128)(2,1)S(1)}, bf16[8192,128]{1,0:T(8,128)(2,1)}, u32[]{:S(2)}) copy-start(bf16[8192,128]{1,0:T(8,128)(2,1)} %param.7) | copy-start | bytes 6291460
  6.5 97.0 %all-gather.2.cloned.1.call-start = ((), (), s32[]{:S(2)}) async-start(), calls=%async_computation.4 | async-start | bytes 8912896 | tf_op jit(solution)/shard_map/all_gather | solution.py:27
  12.2 41.1 %all-to-all-start = ((bf16[32,136,128]{2,1,0:T(8,128)(2,1)}), bf16[32,136,128]{2,1,0:T(8,128)(2,1)S(1)}, u32[]{:S(2)}, u32[]{:S(2)}) async-start(bf16[32,136,128]{2,1,0:T(8,128)(2,1)} %fusion.21), calls=%async_computation | async-start | bytes 2228224 | tf_op jit(solution)/shard_map/all_to_all | solution.py:65
  53.4 1.2 copy-start.1
  56.0 38.9 %copy-start.2 = (bf16[16,64,128]{2,1,0:T(8,128)(2,1)S(1)}, bf16[16,64,128]{2,1,0:T(8,128)(2,1)}, u32[]{:S(2)}) copy-start(bf16[16,64,128]{2,1,0:T(8,128)(2,1)} %param.9) | copy-start | bytes 786436
  56.0 6.1 %collective-permute-start = (f32[512,64]{0,1:T(8,128)S(1)}, f32[512,64]{0,1:T(8,128)S(1)}, u32[]{:S(2)}, u32[]{:S(2)}) collective-permute-start(f32[512,64]{0,1:T(8,128)S(1)} %slice_select_fusion), channel_id=1, source_target_pairs={{0,1},{1,0},{2,3},{3,2},{4,5},{5,4},{6,7},{7,6},{8,9},{9,8},{10,11... | collective-permute-start | bytes 393224 | tf_op jit(solution)/shard_map/ppermute | solution.py:92
  88.7 6.1 %collective-permute-start.1 = (bf16[512,64]{0,1:T(8,128)(2,1)S(1)}, bf16[512,64]{0,1:T(8,128)(2,1)S(1)}, u32[]{:S(2)}, u32[]{:S(2)}) collective-permute-start(bf16[512,64]{0,1:T(8,128)(2,1)S(1)} %reshape.203), channel_id=1, source_target_pairs={{0,1},{1,0},{2,3},{3,2},{4,5},{5,4},{6,7},{7,6},{8,9},{9,8},{10,11... | collective-permute-start | bytes 196616 | tf_op jit(solution)/shard_map/ppermute | solution.py:104
  96.3 18.8 %all-to-all-start.3 = ((bf16[32,32,128]{2,1,0:T(8,128)(2,1)}), bf16[32,32,128]{2,1,0:T(8,128)(2,1)S(1)}, u32[]{:S(2)}, u32[]{:S(2)}) async-start(bf16[32,32,128]{2,1,0:T(8,128)(2,1)} %bitcast.14), calls=%async_computation.3 | async-start | bytes 524288 | tf_op jit(solution)/shard_map/all_to_all | solution.py:119
Sparse Core Ops, SparseCore 0:
  9.5 64.1 all-gather.1

commit v10 on v8

--- a/solution.py
+++ b/solution.py
@@ -81,10 +81,13 @@
     all_ranks = jnp.dot(flat_rows, down_matrix, preferred_element_type=jnp.float32)
     all_ranks = all_ranks.reshape(slot_count, present_adapters, rank_dimension)
     partial_value = jnp.sum(jnp.where(selected, all_ranks, 0.0), axis=1)
-    slot_blocks = partial_value.reshape(tensor_count, slot_count // tensor_count, rank_dimension)
+    block_rows = slot_count // tensor_count
+    dense_shape = (tensor_count, 8, block_rows * rank_dimension // 8)
+    slot_blocks = partial_value.reshape(dense_shape)
     gathered_blocks = lax.all_to_all(slot_blocks, "tensor", split_axis=0, concat_axis=0, tiled=True)
     own_sum = jnp.sum(gathered_blocks, axis=0).astype(jnp.bfloat16)
-    spread = jnp.broadcast_to(own_sum[None], (tensor_count,) + own_sum.shape)
+    spread_shape = (tensor_count, 16, block_rows * rank_dimension // 16)
+    spread = jnp.broadcast_to(own_sum.reshape(spread_shape[1:])[None], spread_shape)
     reduced_rows = lax.all_to_all(spread, "tensor", split_axis=0, concat_axis=0, tiled=True)
     reduced_rows = reduced_rows.reshape(slot_count, rank_dimension)
 

time: 124 us -> 121 us (0.976)
  local copies, waits for them, and re-layouts: 3.54 us -> 1.97 us
  other arithmetic: 3.62 us -> 2.32 us
    all_to_all x1 -> x0, other arithmetic: 1.28 us -> none  [body(): lax.all_to_all(slot_blocks, 'tensor', split_axis=0, concat_axis=0, tiled=...]
  transfers between devices with their start and end apart: 3 -> 3, of which waited for: 2 -> 2; matrix products, arithmetic and copies ran while one was open for 14% -> 12% of each run, Pallas kernels for 0% -> 0%
where the time goes in v10:
time: 121 us
  blocking collectives  35 us (29%)
  waiting for transfers between devices  34.6 us (29%)
  starting transfers between devices  20.7 us (17%)
  between operations  13.6 us (11%)
  matrix products  12.5 us (10%)
  other arithmetic  2.32 us (2%)
  local copies, waits for them, and re-layouts  1.97 us (2%)
    all_to_all x1, waiting for transfers between devices, body(): lax.all_to_all(send_block, 'wide', split_axis=0, concat_axis=0, tiled=True)  27.3 us
    all_to_all x1, blocking collectives, body(): lax.all_to_all(slot_blocks, 'tensor', split_axis=0, concat_axis=0, tiled=...  23.2 us
    all_to_all x1, starting transfers between devices, body(): lax.all_to_all(send_block, 'wide', split_axis=0, concat_axis=0, tiled=True)  13.7 us
    all_to_all x1, blocking collectives, body(): lax.all_to_all(spread, 'tensor', split_axis=0, concat_axis=0, tiled=True)  11.7 us
    all_to_all x1, starting transfers between devices, body(): lax.all_to_all(adapter_correction, 'wide', split_axis=0, concat_axis=0, t...  6.95 us
    all_to_all x1, waiting for transfers between devices, body(): lax.all_to_all(adapter_correction, 'wide', split_axis=0, concat_axis=0, t...  6.53 us
    dot_general x1, matrix products, body(): jnp.dot(gathered, key_value_weight, preferred_element_type=jnp.float32)  5.71 us
  transfers between devices with their start and end apart: 3, of which 2 were waited for; matrix products, arithmetic and copies ran while one was open for 12% of the time, Pallas kernels for 0%

profile of v10, /device:TPU:1, one launch (start us, length us, event | category | flops | bytes accessed | tf_op | source)
XLA Modules:
  0.0 120.6 jit_solution(14568717542717389603)
XLA Ops:
  6.5 0.0 copy-start
  6.5 0.0 all-gather.2.cloned.1.call-start
  6.5 0.7 all-gather.2.cloned.1.call-update
  7.3 0.9 select_reduce_fusion.1
  8.2 0.3 fusion.20
  8.5 0.6 fusion.4
  9.1 0.1 convert_element_type.74
  9.2 1.8 %fusion.9 = bf16[32,32,4,128]{3,1,2,0:T(8,128)(2,1)S(1)} fusion(s32[512]{0:T(512)S(1)} %convert_add_fusion, s32[32,32]{1,0:T(8,128)S(1)} %multiply_add_fusion, bf16[512,512]{1,0:T(8,128)(2,1)} %param.6), kind=kOutput, calls=%fused_computation.12 | convolution fusion | flops 537919488 | bytes 1579008 | tf_op jit(solution)/shard_map/dcr,rjl->djcl/dot_general | solution.py:56
  11.0 1.2 fusion.21
  12.2 13.7 %all-to-all-start = ((bf16[32,136,128]{2,1,0:T(8,128)(2,1)}), bf16[32,136,128]{2,1,0:T(8,128)(2,1)S(1)}, u32[]{:S(2)}, u32[]{:S(2)}) async-start(bf16[32,136,128]{2,1,0:T(8,128)(2,1)} %fusion.21), calls=%async_computation | async-start | bytes 2228224 | tf_op jit(solution)/shard_map/all_to_all | solution.py:65
  25.9 27.3 %all-to-all-done = bf16[32,136,128]{2,1,0:T(8,128)(2,1)S(1)} async-done(((bf16[32,136,128]{2,1,0:T(8,128)(2,1)}), bf16[32,136,128]{2,1,0:T(8,128)(2,1)S(1)}, u32[]{:S(2)}, u32[]{:S(2)}) %all-to-all-start) | async-done | bytes 1114144 | tf_op jit(solution)/shard_map/all_to_all | solution.py:65
  53.3 0.1 fusion.38
  53.3 0.1 reshape.175
  53.4 0.1 broadcast_compare_fusion
  53.5 0.1 fusion.45
  53.6 1.1 copy-done.1
  54.7 1.3 %select_reduce_fusion = f32[1024,64]{0,1:T(8,128)S(1)} fusion(pred[1024,16]{0,1:T(8,128)(4,1)S(1)} %broadcast_compare_fusion, bf16[1024,128]{1,0:T(8,128)(2,1)S(1)} %bitcast.47, bf16[1024,128]{1,0:T(8,128)(2,1)S(1)} %bitcast.48, bf16[1024,128]{1,0:T(8,128)(2,1)S(1)} %bitcast.49, bf16[1024,128]{1,0:T(8,128)(2,1)S(1)} %bitcast.46, ...), kind=kOutput, calls=%fused_computation | convolution fusion | flops 1079967744 | bytes 2375680 | tf_op jit(solution)/shard_map/dot_general | solution.py:81
  55.9 0.0 copy-start.2
  56.0 0.2 copy.18
  56.2 0.1 reshape.172
  56.3 23.2 %all_to_all.20 = f32[16,8,512]{2,1,0:T(8,128)S(1)} all-to-all(f32[16,8,512]{2,1,0:T(8,128)S(1)} %reshape.172), channel_id=1, replica_groups=mesh['wide'=32,'tensor'=16] {'tensor'}, dimensions={0} | all-to-all | bytes 524288 | tf_op jit(solution)/shard_map/all_to_all | solution.py:87
  79.6 11.7 %all_to_all.21 = bf16[16,16,256]{2,1,0:T(8,128)(2,1)S(1)} all-to-all(bf16[16,16,256]{2,1,0:T(8,128)(2,1)S(1)} %broadcast_in_dim.72), channel_id=1, replica_groups=mesh['wide'=32,'tensor'=16] {'tensor'}, dimensions={0} | all-to-all | bytes 262144 | tf_op jit(solution)/shard_map/all_to_all | solution.py:91
  91.3 0.2 broadcast_in_dim.73
  91.5 0.1 copy.19
  91.6 0.0 copy-done.2
  91.6 1.5 %fusion.15 = bf16[1024,128]{1,0:T(8,128)(2,1)} fusion(bf16[16,64,128]{2,1,0:T(8,128)(2,1)S(1)} %copy-done.2, pred[1024,16]{0,1:T(8,128)(4,1)S(1)} %broadcast_compare_fusion, bf16[1024,64]{0,1:T(8,128)(2,1)S(1)} %copy.19), kind=kOutput, calls=%fused_computation.14 | convolution fusion | flops 269615104 | bytes 671744 | tf_op jit(solution)/shard_map/dot_general | solution.py:98
  93.1 7.0 %all-to-all-start.3 = ((bf16[32,32,128]{2,1,0:T(8,128)(2,1)}), bf16[32,32,128]{2,1,0:T(8,128)(2,1)S(1)}, u32[]{:S(2)}, u32[]{:S(2)}) async-start(bf16[32,32,128]{2,1,0:T(8,128)(2,1)} %bitcast.14), calls=%async_computation.3 | async-start | bytes 524288 | tf_op jit(solution)/shard_map/all_to_all | solution.py:102
  100.1 0.0 all-gather.2.cloned.1.call-done
  100.1 0.0 copy-done
  100.1 5.7 %fusion.46 = f32[512,128]{1,0:T(8,128)S(1)} fusion(bf16[512,8192]{1,0:T(8,128)(2,1)} %all-gather.2.cloned.1.call-done, bf16[8192,128]{1,0:T(8,128)(2,1)S(1)} %copy-done), kind=kOutput, calls=%fused_computation.63 | convolution fusion | flops 1073741824 | bytes 10747904 | tf_op jit(solution)/shard_map/dot_general | solution.py:28
  105.8 6.5 %all-to-all-done.3 = bf16[32,32,128]{2,1,0:T(8,128)(2,1)S(1)} async-done(((bf16[32,32,128]{2,1,0:T(8,128)(2,1)}), bf16[32,32,128]{2,1,0:T(8,128)(2,1)S(1)}, u32[]{:S(2)}, u32[]{:S(2)}) %all-to-all-start.3) | async-done | bytes 262176 | tf_op jit(solution)/shard_map/all_to_all | solution.py:102
  112.4 1.4 %fusion.19 = bf16[512,128]{1,0:T(8,128)(2,1)} fusion(f32[512,128]{1,0:T(8,128)S(1)} %fusion.46, bf16[1024,128]{1,0:T(8,128)(2,1)S(1)} %bitcast.45, s32[512]{0:T(512)S(1)} %convert_add_fusion), kind=kOutput, calls=%fused_computation.16 | convolution fusion | flops 134873088 | bytes 657408 | tf_op jit(solution)/shard_map/dot_general | solution.py:106
  (9 shorter events, 0.1 us)
Async XLA Ops:
  6.5 93.6 %copy-start = (bf16[8192,128]{1,0:T(8,128)(2,1)S(1)}, bf16[8192,128]{1,0:T(8,128)(2,1)}, u32[]{:S(2)}) copy-start(bf16[8192,128]{1,0:T(8,128)(2,1)} %param.7) | copy-start | bytes 6291460
  6.5 93.6 %all-gather.2.cloned.1.call-start = ((), (), s32[]{:S(2)}) async-start(), calls=%async_computation.4 | async-start | bytes 8912896 | tf_op jit(solution)/shard_map/all_gather | solution.py:27
  12.2 41.1 %all-to-all-start = ((bf16[32,136,128]{2,1,0:T(8,128)(2,1)}), bf16[32,136,128]{2,1,0:T(8,128)(2,1)S(1)}, u32[]{:S(2)}, u32[]{:S(2)}) async-start(bf16[32,136,128]{2,1,0:T(8,128)(2,1)} %fusion.21), calls=%async_computation | async-start | bytes 2228224 | tf_op jit(solution)/shard_map/all_to_all | solution.py:65
  53.4 1.2 %copy-start.1 = (bf16[512,16,64]{0,2,1:T(8,128)(2,1)S(1)}, bf16[512,16,64]{0,2,1:T(8,128)(2,1)}, u32[]{:S(2)}) copy-start(bf16[512,16,64]{0,2,1:T(8,128)(2,1)} %param.8) | copy-start | bytes 3145732
  55.9 35.7 %copy-start.2 = (bf16[16,64,128]{2,1,0:T(8,128)(2,1)S(1)}, bf16[16,64,128]{2,1,0:T(8,128)(2,1)}, u32[]{:S(2)}) copy-start(bf16[16,64,128]{2,1,0:T(8,128)(2,1)} %param.9) | copy-start | bytes 786436
  93.1 19.2 %all-to-all-start.3 = ((bf16[32,32,128]{2,1,0:T(8,128)(2,1)}), bf16[32,32,128]{2,1,0:T(8,128)(2,1)S(1)}, u32[]{:S(2)}, u32[]{:S(2)}) async-start(bf16[32,32,128]{2,1,0:T(8,128)(2,1)} %bitcast.14), calls=%async_computation.3 | async-start | bytes 524288 | tf_op jit(solution)/shard_map/all_to_all | solution.py:102
Sparse Core Ops, SparseCore 0:
  9.5 67.1 all-gather.1

commit v11 on v10

--- a/solution.py
+++ b/solution.py
@@ -29,10 +29,15 @@
         gathered, key_value_weight, preferred_element_type=jnp.float32
     )
 
-    adapter_match = adapter_per_row[:, None] == jnp.arange(total_adapters, dtype=jnp.int32)[None, :]
-    storage_position = jnp.sum(jnp.where(adapter_match, adapter_storage_slot[None, :], 0), axis=1)
-    owner_index = storage_position // present_adapters
-    local_index = storage_position % present_adapters
+    adapter_match = (
+        adapter_per_row[:, None] == jnp.arange(total_adapters, dtype=jnp.int32)[None, :]
+    ).astype(jnp.bfloat16)
+    slot_parts = jnp.stack(
+        [adapter_storage_slot // present_adapters, adapter_storage_slot % present_adapters], axis=1
+    ).astype(jnp.bfloat16)
+    picked = jnp.dot(adapter_match, slot_parts, preferred_element_type=jnp.float32)
+    owner_index = picked[:, 0].astype(jnp.int32)
+    local_index = picked[:, 1].astype(jnp.int32)
 
     owner_onehot = (
         owner_index[:, None] == jnp.arange(wide_count, dtype=jnp.int32)[None, :]

time: 121 us -> 121 us (level)
  no operation moved by 1% of the time
where the time goes in v11:
time: 121 us; the launch traced here: 120 us
  blocking collectives  35.1 us (29%)
  waiting for transfers between devices  34.6 us (29%)
  starting transfers between devices  20.5 us (17%)
  between operations  13.6 us (11%)
  matrix products  12.5 us (10%)
  other arithmetic  2.16 us (2%)
  local copies, waits for them, and re-layouts  1.98 us (2%)
    all_to_all x1, waiting for transfers between devices, body(): lax.all_to_all(send_block, 'wide', split_axis=0, concat_axis=0, tiled=True)  27.3 us
    all_to_all x1, blocking collectives, body(): lax.all_to_all(slot_blocks, 'tensor', split_axis=0, concat_axis=0, tiled=...  23.3 us
    all_to_all x1, starting transfers between devices, body(): lax.all_to_all(send_block, 'wide', split_axis=0, concat_axis=0, tiled=True)  13.7 us
    all_to_all x1, blocking collectives, body(): lax.all_to_all(spread, 'tensor', split_axis=0, concat_axis=0, tiled=True)  11.7 us
    all_to_all x1, starting transfers between devices, body(): lax.all_to_all(adapter_correction, 'wide', split_axis=0, concat_axis=0, t...  6.83 us
    all_to_all x1, waiting for transfers between devices, body(): lax.all_to_all(adapter_correction, 'wide', split_axis=0, concat_axis=0, t...  6.54 us
    dot_general x1, matrix products, body(): jnp.dot(gathered, key_value_weight, preferred_element_type=jnp.float32)  5.7 us
  transfers between devices with their start and end apart: 3, of which 2 were waited for; matrix products, arithmetic and copies ran while one was open for 12% of the time, Pallas kernels for 0%

profile of v11, /device:TPU:1, one launch (start us, length us, event | category | flops | bytes accessed | tf_op | source)
XLA Modules:
  0.0 120.5 jit_solution(18328896237267685916)
XLA Ops:
  6.5 0.0 copy-start
  6.5 0.0 all-gather.2.cloned.1.call-start
  6.5 0.7 all-gather.2.cloned.1.call-update
  7.3 0.8 fusion.42
  8.0 1.1 fusion.35
  9.1 0.3 fusion.20
  9.4 0.6 fusion.4
  10.1 0.1 convert_element_type.88
  10.1 0.0 copy-done.1
  10.2 0.8 fusion.9
  10.9 1.2 fusion.21
  12.1 13.7 %all-to-all-start = ((bf16[32,136,128]{2,1,0:T(8,128)(2,1)}), bf16[32,136,128]{2,1,0:T(8,128)(2,1)S(1)}, u32[]{:S(2)}, u32[]{:S(2)}) async-start(bf16[32,136,128]{2,1,0:T(8,128)(2,1)} %fusion.21), calls=%async_computation | async-start | bytes 2228224 | tf_op jit(solution)/shard_map/all_to_all | solution.py:70
  25.8 27.3 %all-to-all-done = bf16[32,136,128]{2,1,0:T(8,128)(2,1)S(1)} async-done(((bf16[32,136,128]{2,1,0:T(8,128)(2,1)}), bf16[32,136,128]{2,1,0:T(8,128)(2,1)S(1)}, u32[]{:S(2)}, u32[]{:S(2)}) %all-to-all-start) | async-done | bytes 1114144 | tf_op jit(solution)/shard_map/all_to_all | solution.py:70
  53.2 0.1 fusion.40
  53.2 0.1 reshape.133
  53.3 0.1 broadcast_compare_fusion
  53.4 0.1 fusion.54
  53.5 1.0 copy-done.2
  54.5 1.3 %select_reduce_fusion = f32[1024,64]{0,1:T(8,128)S(1)} fusion(pred[1024,16]{0,1:T(8,128)(4,1)S(1)} %broadcast_compare_fusion, bf16[1024,128]{1,0:T(8,128)(2,1)S(1)} %bitcast.49, bf16[1024,128]{1,0:T(8,128)(2,1)S(1)} %bitcast.50, bf16[1024,128]{1,0:T(8,128)(2,1)S(1)} %bitcast.51, bf16[1024,128]{1,0:T(8,128)(2,1)S(1)} %bitcast.48, ...), kind=kOutput, calls=%fused_computation | convolution fusion | flops 1079967744 | bytes 2375680 | tf_op jit(solution)/shard_map/dot_general | solution.py:86
  55.8 0.0 copy-start.3
  55.8 0.2 copy.14
  56.0 0.1 reshape.130
  56.2 23.3 %all_to_all.20 = f32[16,8,512]{2,1,0:T(8,128)S(1)} all-to-all(f32[16,8,512]{2,1,0:T(8,128)S(1)} %reshape.130), channel_id=1, replica_groups=mesh['wide'=32,'tensor'=16] {'tensor'}, dimensions={0} | all-to-all | bytes 524288 | tf_op jit(solution)/shard_map/all_to_all | solution.py:92
  79.6 11.7 %all_to_all.21 = bf16[16,16,256]{2,1,0:T(8,128)(2,1)S(1)} all-to-all(bf16[16,16,256]{2,1,0:T(8,128)(2,1)S(1)} %broadcast_in_dim.60), channel_id=1, replica_groups=mesh['wide'=32,'tensor'=16] {'tensor'}, dimensions={0} | all-to-all | bytes 262144 | tf_op jit(solution)/shard_map/all_to_all | solution.py:96
  91.3 0.2 broadcast_in_dim.61
  91.5 0.1 copy.15
  91.6 1.5 %fusion.15 = bf16[1024,128]{1,0:T(8,128)(2,1)} fusion(bf16[16,64,128]{2,1,0:T(8,128)(2,1)S(1)} %copy-done.3, pred[1024,16]{0,1:T(8,128)(4,1)S(1)} %broadcast_compare_fusion, bf16[1024,64]{0,1:T(8,128)(2,1)S(1)} %copy.15), kind=kOutput, calls=%fused_computation.14 | convolution fusion | flops 269615104 | bytes 671744 | tf_op jit(solution)/shard_map/dot_general | solution.py:103
  93.1 6.8 %all-to-all-start.3 = ((bf16[32,32,128]{2,1,0:T(8,128)(2,1)}), bf16[32,32,128]{2,1,0:T(8,128)(2,1)S(1)}, u32[]{:S(2)}, u32[]{:S(2)}) async-start(bf16[32,32,128]{2,1,0:T(8,128)(2,1)} %bitcast.16), calls=%async_computation.3 | async-start | bytes 524288 | tf_op jit(solution)/shard_map/all_to_all | solution.py:107
  100.0 0.0 all-gather.2.cloned.1.call-done
  100.0 5.7 %fusion.55 = f32[512,128]{1,0:T(8,128)S(1)} fusion(bf16[512,8192]{1,0:T(8,128)(2,1)} %all-gather.2.cloned.1.call-done, bf16[8192,128]{1,0:T(8,128)(2,1)S(1)} %copy-done), kind=kOutput, calls=%fused_computation.74 | convolution fusion | flops 1073741824 | bytes 10747904 | tf_op jit(solution)/shard_map/dot_general | solution.py:28
  105.7 6.5 %all-to-all-done.3 = bf16[32,32,128]{2,1,0:T(8,128)(2,1)S(1)} async-done(((bf16[32,32,128]{2,1,0:T(8,128)(2,1)}), bf16[32,32,128]{2,1,0:T(8,128)(2,1)S(1)}, u32[]{:S(2)}, u32[]{:S(2)}) %all-to-all-start.3) | async-done | bytes 262176 | tf_op jit(solution)/shard_map/all_to_all | solution.py:107
  112.3 1.4 %fusion.19 = bf16[512,128]{1,0:T(8,128)(2,1)} fusion(f32[512,128]{1,0:T(8,128)S(1)} %fusion.55, bf16[1024,128]{1,0:T(8,128)(2,1)S(1)} %bitcast.47, s32[512]{0:T(512)S(1)} %convert_add_fusion), kind=kOutput, calls=%fused_computation.16 | convolution fusion | flops 134873088 | bytes 657408 | tf_op jit(solution)/shard_map/dot_general | solution.py:111
  (16 shorter events, 0.2 us)
Async XLA Ops:
  6.5 93.5 %copy-start = (bf16[8192,128]{1,0:T(8,128)(2,1)S(1)}, bf16[8192,128]{1,0:T(8,128)(2,1)}, u32[]{:S(2)}) copy-start(bf16[8192,128]{1,0:T(8,128)(2,1)} %param.7) | copy-start | bytes 6291460
  6.5 3.6 %copy-start.1 = (bf16[512,512]{1,0:T(8,128)(2,1)S(1)}, bf16[512,512]{1,0:T(8,128)(2,1)}, u32[]{:S(2)}) copy-start(bf16[512,512]{1,0:T(8,128)(2,1)} %param.6) | copy-start | bytes 1572868
  6.5 93.5 %all-gather.2.cloned.1.call-start = ((), (), s32[]{:S(2)}) async-start(), calls=%async_computation.4 | async-start | bytes 8912896 | tf_op jit(solution)/shard_map/all_gather | solution.py:27
  12.1 41.1 %all-to-all-start = ((bf16[32,136,128]{2,1,0:T(8,128)(2,1)}), bf16[32,136,128]{2,1,0:T(8,128)(2,1)S(1)}, u32[]{:S(2)}, u32[]{:S(2)}) async-start(bf16[32,136,128]{2,1,0:T(8,128)(2,1)} %fusion.21), calls=%async_computation | async-start | bytes 2228224 | tf_op jit(solution)/shard_map/all_to_all | solution.py:70
  53.3 1.2 %copy-start.2 = (bf16[512,16,64]{0,2,1:T(8,128)(2,1)S(1)}, bf16[512,16,64]{0,2,1:T(8,128)(2,1)}, u32[]{:S(2)}) copy-start(bf16[512,16,64]{0,2,1:T(8,128)(2,1)} %param.8) | copy-start | bytes 3145732
  55.8 35.8 %copy-start.3 = (bf16[16,64,128]{2,1,0:T(8,128)(2,1)S(1)}, bf16[16,64,128]{2,1,0:T(8,128)(2,1)}, u32[]{:S(2)}) copy-start(bf16[16,64,128]{2,1,0:T(8,128)(2,1)} %param.9) | copy-start | bytes 786436
  93.1 19.1 %all-to-all-start.3 = ((bf16[32,32,128]{2,1,0:T(8,128)(2,1)}), bf16[32,32,128]{2,1,0:T(8,128)(2,1)S(1)}, u32[]{:S(2)}, u32[]{:S(2)}) async-start(bf16[32,32,128]{2,1,0:T(8,128)(2,1)} %bitcast.16), calls=%async_computation.3 | async-start | bytes 524288 | tf_op jit(solution)/shard_map/all_to_all | solution.py:107
Sparse Core Ops, SparseCore 0:
  9.5 67.3 all-gather.1

commit v12 on v11

--- a/solution.py
+++ b/solution.py
@@ -87,8 +87,7 @@
     all_ranks = all_ranks.reshape(slot_count, present_adapters, rank_dimension)
     partial_value = jnp.sum(jnp.where(selected, all_ranks, 0.0), axis=1)
     block_rows = slot_count // tensor_count
-    dense_shape = (tensor_count, 8, block_rows * rank_dimension // 8)
-    slot_blocks = partial_value.reshape(dense_shape)
+    slot_blocks = partial_value.reshape(tensor_count, block_rows, rank_dimension)
     gathered_blocks = lax.all_to_all(slot_blocks, "tensor", split_axis=0, concat_axis=0, tiled=True)
     own_sum = jnp.sum(gathered_blocks, axis=0).astype(jnp.bfloat16)
     spread_shape = (tensor_count, 16, block_rows * rank_dimension // 16)

time: 121 us -> 123 us (1.017)
  other arithmetic: 2.16 us -> 3.46 us
    all_to_all x0 -> x1, other arithmetic: none -> 1.28 us  [body(): lax.all_to_all(slot_blocks, 'tensor', split_axis=0, concat_axis=0, tiled=...]
  transfers between devices with their start and end apart: 3 -> 3, of which waited for: 2 -> 2; matrix products, arithmetic and copies ran while one was open for 12% -> 14% of each run, Pallas kernels for 0% -> 0%
where the time goes in v12:
time: 123 us
  blocking collectives  34.8 us (28%)
  waiting for transfers between devices  34.6 us (28%)
  starting transfers between devices  20.8 us (17%)
  between operations  13.6 us (11%)
  matrix products  12.5 us (10%)
  other arithmetic  3.46 us (3%)
  local copies, waits for them, and re-layouts  3.18 us (3%)
    all_to_all x1, waiting for transfers between devices, body(): lax.all_to_all(send_block, 'wide', split_axis=0, concat_axis=0, tiled=True)  27.3 us
    all_to_all x1, blocking collectives, body(): lax.all_to_all(slot_blocks, 'tensor', split_axis=0, concat_axis=0, tiled=...  22.4 us
    all_to_all x1, starting transfers between devices, body(): lax.all_to_all(send_block, 'wide', split_axis=0, concat_axis=0, tiled=True)  13.7 us
    all_to_all x1, blocking collectives, body(): lax.all_to_all(spread, 'tensor', split_axis=0, concat_axis=0, tiled=True)  12.4 us
    all_to_all x1, starting transfers between devices, body(): lax.all_to_all(adapter_correction, 'wide', split_axis=0, concat_axis=0, t...  7.13 us
    all_to_all x1, waiting for transfers between devices, body(): lax.all_to_all(adapter_correction, 'wide', split_axis=0, concat_axis=0, t...  6.54 us
    dot_general x1, matrix products, body(): jnp.dot(gathered, key_value_weight, preferred_element_type=jnp.float32)  5.7 us
  transfers between devices with their start and end apart: 3, of which 2 were waited for; matrix products, arithmetic and copies ran while one was open for 14% of the time, Pallas kernels for 0%

profile of v12, /device:TPU:1, one launch (start us, length us, event | category | flops | bytes accessed | tf_op | source)
XLA Modules:
  0.0 123.0 jit_solution(10217559153307379817)
XLA Ops:
  6.5 0.7 all-gather.2.cloned.1.call-update
  7.3 0.8 fusion.42
  8.0 1.1 fusion.35
  9.1 0.3 fusion.20
  9.4 0.6 fusion.4
  10.1 0.1 convert_element_type.88
  10.2 0.8 fusion.9
  10.9 1.2 fusion.21
  12.1 13.7 %all-to-all-start = ((bf16[32,136,128]{2,1,0:T(8,128)(2,1)}), bf16[32,136,128]{2,1,0:T(8,128)(2,1)S(1)}, u32[]{:S(2)}, u32[]{:S(2)}) async-start(bf16[32,136,128]{2,1,0:T(8,128)(2,1)} %fusion.21), calls=%async_computation | async-start | bytes 2228224 | tf_op jit(solution)/shard_map/all_to_all | solution.py:70
  25.8 27.3 %all-to-all-done = bf16[32,136,128]{2,1,0:T(8,128)(2,1)S(1)} async-done(((bf16[32,136,128]{2,1,0:T(8,128)(2,1)}), bf16[32,136,128]{2,1,0:T(8,128)(2,1)S(1)}, u32[]{:S(2)}, u32[]{:S(2)}) %all-to-all-start) | async-done | bytes 1114144 | tf_op jit(solution)/shard_map/all_to_all | solution.py:70
  53.2 0.1 reshape.133
  53.3 0.1 broadcast_compare_fusion
  53.4 0.1 fusion.54
  53.5 1.0 copy-done.2
  54.5 1.3 %select_reduce_fusion = f32[1024,64]{0,1:T(8,128)S(1)} fusion(pred[1024,16]{0,1:T(8,128)(4,1)S(1)} %broadcast_compare_fusion, bf16[1024,128]{1,0:T(8,128)(2,1)S(1)} %bitcast.57, bf16[1024,128]{1,0:T(8,128)(2,1)S(1)} %bitcast.58, bf16[1024,128]{1,0:T(8,128)(2,1)S(1)} %bitcast.59, bf16[1024,128]{1,0:T(8,128)(2,1)S(1)} %bitcast.56, ...), kind=kOutput, calls=%fused_computation | convolution fusion | flops 1079967744 | bytes 2375680 | tf_op jit(solution)/shard_map/dot_general | solution.py:86
  55.8 0.1 reshape.130
  56.0 0.2 copy.34
  56.2 0.3 reshape.147
  56.5 22.4 %all_to_all.20 = f32[16,1,4096]{2,1,0:T(1,128)S(1)} all-to-all(f32[16,1,4096]{2,1,0:T(1,128)S(1)} %reshape.147), channel_id=1, replica_groups=mesh['wide'=32,'tensor'=16] {'tensor'}, dimensions={0} | all-to-all | bytes 524288 | tf_op jit(solution)/shard_map/all_to_all | solution.py:91
  78.9 0.5 broadcast.97
  79.4 1.3 %reduce.8 = f32[16,4096]{1,0:T(8,128)S(1)} reduce(f32[16,1,4096]{2,1,0:T(1,128)S(1)} %all_to_all.20, f32[]{:T(128)} %broadcast.97), dimensions={1}, to_apply=%all_to_all.13.reduce_sub_computation | reduce | bytes 524292 | tf_op jit(solution)/shard_map/all_to_all | solution.py:91
  80.6 0.2 reshape.148
  80.9 0.1 copy.24
  81.0 0.1 convert_element_type.84
  81.1 12.4 %all_to_all.21 = bf16[16,16,256]{2,1,0:T(8,128)(2,1)S(1)} all-to-all(bf16[16,16,256]{2,1,0:T(8,128)(2,1)S(1)} %broadcast_in_dim.60), channel_id=1, replica_groups=mesh['wide'=32,'tensor'=16] {'tensor'}, dimensions={0} | all-to-all | bytes 262144 | tf_op jit(solution)/shard_map/all_to_all | solution.py:95
  93.5 0.2 broadcast_in_dim.61
  93.7 0.1 copy.25
  93.9 1.5 %fusion.15 = bf16[1024,128]{1,0:T(8,128)(2,1)} fusion(bf16[16,64,128]{2,1,0:T(8,128)(2,1)S(1)} %copy-done.3, pred[1024,16]{0,1:T(8,128)(4,1)S(1)} %broadcast_compare_fusion, bf16[1024,64]{0,1:T(8,128)(2,1)S(1)} %copy.25), kind=kOutput, calls=%fused_computation.14 | convolution fusion | flops 269615104 | bytes 671744 | tf_op jit(solution)/shard_map/dot_general | solution.py:102
  95.3 7.1 %all-to-all-start.3 = ((bf16[32,32,128]{2,1,0:T(8,128)(2,1)}), bf16[32,32,128]{2,1,0:T(8,128)(2,1)S(1)}, u32[]{:S(2)}, u32[]{:S(2)}) async-start(bf16[32,32,128]{2,1,0:T(8,128)(2,1)} %bitcast.16), calls=%async_computation.3 | async-start | bytes 524288 | tf_op jit(solution)/shard_map/all_to_all | solution.py:106
  102.5 5.7 %fusion.55 = f32[512,128]{1,0:T(8,128)S(1)} fusion(bf16[512,8192]{1,0:T(8,128)(2,1)} %all-gather.2.cloned.1.call-done, bf16[8192,128]{1,0:T(8,128)(2,1)S(1)} %copy-done), kind=kOutput, calls=%fused_computation.76 | convolution fusion | flops 1073741824 | bytes 10747904 | tf_op jit(solution)/shard_map/dot_general | solution.py:28
  108.2 6.5 %all-to-all-done.3 = bf16[32,32,128]{2,1,0:T(8,128)(2,1)S(1)} async-done(((bf16[32,32,128]{2,1,0:T(8,128)(2,1)}), bf16[32,32,128]{2,1,0:T(8,128)(2,1)S(1)}, u32[]{:S(2)}, u32[]{:S(2)}) %all-to-all-start.3) | async-done | bytes 262176 | tf_op jit(solution)/shard_map/all_to_all | solution.py:106
  114.8 1.4 %fusion.19 = bf16[512,128]{1,0:T(8,128)(2,1)} fusion(f32[512,128]{1,0:T(8,128)S(1)} %fusion.55, bf16[1024,128]{1,0:T(8,128)(2,1)S(1)} %bitcast.55, s32[512]{0:T(512)S(1)} %convert_add_fusion), kind=kOutput, calls=%fused_computation.16 | convolution fusion | flops 134873088 | bytes 657408 | tf_op jit(solution)/shard_map/dot_general | solution.py:110
  (21 shorter events, 0.3 us)
Async XLA Ops:
  6.5 96.0 %copy-start = (bf16[8192,128]{1,0:T(8,128)(2,1)S(1)}, bf16[8192,128]{1,0:T(8,128)(2,1)}, u32[]{:S(2)}) copy-start(bf16[8192,128]{1,0:T(8,128)(2,1)} %param.7) | copy-start | bytes 6291460
  6.5 3.6 %copy-start.1 = (bf16[512,512]{1,0:T(8,128)(2,1)S(1)}, bf16[512,512]{1,0:T(8,128)(2,1)}, u32[]{:S(2)}) copy-start(bf16[512,512]{1,0:T(8,128)(2,1)} %param.6) | copy-start | bytes 1572868
  6.5 96.0 %all-gather.2.cloned.1.call-start = ((), (), s32[]{:S(2)}) async-start(), calls=%async_computation.4 | async-start | bytes 8912896 | tf_op jit(solution)/shard_map/all_gather | solution.py:27
  12.1 41.1 %all-to-all-start = ((bf16[32,136,128]{2,1,0:T(8,128)(2,1)}), bf16[32,136,128]{2,1,0:T(8,128)(2,1)S(1)}, u32[]{:S(2)}, u32[]{:S(2)}) async-start(bf16[32,136,128]{2,1,0:T(8,128)(2,1)} %fusion.21), calls=%async_computation | async-start | bytes 2228224 | tf_op jit(solution)/shard_map/all_to_all | solution.py:70
  53.3 1.2 copy-start.2
  56.1 37.7 %copy-start.3 = (bf16[16,64,128]{2,1,0:T(8,128)(2,1)S(1)}, bf16[16,64,128]{2,1,0:T(8,128)(2,1)}, u32[]{:S(2)}) copy-start(bf16[16,64,128]{2,1,0:T(8,128)(2,1)} %param.9) | copy-start | bytes 786436
  95.3 19.4 %all-to-all-start.3 = ((bf16[32,32,128]{2,1,0:T(8,128)(2,1)}), bf16[32,32,128]{2,1,0:T(8,128)(2,1)S(1)}, u32[]{:S(2)}, u32[]{:S(2)}) async-start(bf16[32,32,128]{2,1,0:T(8,128)(2,1)} %bitcast.16), calls=%async_computation.3 | async-start | bytes 524288 | tf_op jit(solution)/shard_map/all_to_all | solution.py:106
Sparse Core Ops, SparseCore 0:
  9.5 66.8 all-gather.1

commit v13 on v11

--- a/solution.py
+++ b/solution.py
@@ -96,8 +96,9 @@
     reduced_rows = lax.all_to_all(spread, "tensor", split_axis=0, concat_axis=0, tiled=True)
     reduced_rows = reduced_rows.reshape(slot_count, rank_dimension)
 
+    base_tie = (base_projection_output[0, 0] * 0.0).astype(jnp.bfloat16)
     expanded_rows = jnp.where(
-        selected, reduced_rows[:, None, :], jnp.zeros((), jnp.bfloat16)
+        selected, reduced_rows[:, None, :] + base_tie, jnp.zeros((), jnp.bfloat16)
     ).reshape(slot_count, present_adapters * rank_dimension)
     up_matrix = adapter_up_maps.reshape(present_adapters * rank_dimension, column_portion)
     adapter_correction = jnp.dot(

time: 121 us -> 121 us (level)
  blocking collectives: 35.1 us -> 42 us
  waiting for transfers between devices: 34.6 us -> 29.4 us
  starting transfers between devices: 20.5 us -> 17.1 us
  local copies, waits for them, and re-layouts: 1.98 us -> 3.23 us
    all_to_all x1, blocking collectives: 11.7 us -> 18.7 us  [body(): lax.all_to_all(adapter_correction, 'wide', split_axis=0, concat_axis=0, t...]
    all_to_all x1, waiting for transfers between devices: 6.54 us -> 1.37 us  [body(): lax.all_to_all(spread, 'tensor', split_axis=0, concat_axis=0, tiled=True)]
    all_to_all x1, starting transfers between devices: 6.83 us -> 3.41 us  [body(): lax.all_to_all(spread, 'tensor', split_axis=0, concat_axis=0, tiled=True)]
  transfers between devices with their start and end apart: 3 -> 3, of which waited for: 2 -> 2; matrix products, arithmetic and copies ran while one was open for 12% -> 11% of each run, Pallas kernels for 0% -> 0%
where the time goes in v13:
time: 121 us; the launch traced here: 120 us
  blocking collectives  42 us (35%)
  waiting for transfers between devices  29.4 us (24%)
  starting transfers between devices  17.1 us (14%)
  between operations  14.3 us (12%)
  matrix products  11.9 us (10%)
  local copies, waits for them, and re-layouts  3.23 us (3%)
  other arithmetic  2.17 us (2%)
    all_to_all x1, waiting for transfers between devices, body(): lax.all_to_all(send_block, 'wide', split_axis=0, concat_axis=0, tiled=True)  27.3 us
    all_to_all x1, blocking collectives, body(): lax.all_to_all(slot_blocks, 'tensor', split_axis=0, concat_axis=0, tiled=...  23.4 us
    all_to_all x1, blocking collectives, body(): lax.all_to_all(adapter_correction, 'wide', split_axis=0, concat_axis=0, t...  18.7 us
    all_to_all x1, starting transfers between devices, body(): lax.all_to_all(send_block, 'wide', split_axis=0, concat_axis=0, tiled=True)  13.7 us
    dot_general x1, matrix products, body(): jnp.dot(gathered, key_value_weight, preferred_element_type=jnp.float32)  5.74 us
    all_to_all x1, starting transfers between devices, body(): lax.all_to_all(spread, 'tensor', split_axis=0, concat_axis=0, tiled=True)  3.41 us
  transfers between devices with their start and end apart: 3, of which 2 were waited for; matrix products, arithmetic and copies ran while one was open for 11% of the time, Pallas kernels for 0%

profile of v13, /device:TPU:1, one launch (start us, length us, event | category | flops | bytes accessed | tf_op | source)
XLA Modules:
  0.0 120.1 jit_solution(12623591039854566695)
XLA Ops:
  6.5 0.7 all-gather.2.cloned.1.call-update
  7.3 0.8 fusion.42
  8.0 1.1 fusion.35
  9.1 0.3 fusion.20
  9.4 0.6 fusion.4
  10.1 0.1 convert_element_type.96
  10.1 0.0 copy-done.1
  10.2 0.8 fusion.9
  10.9 1.2 fusion.21
  12.1 13.7 %all-to-all-start = ((bf16[32,136,128]{2,1,0:T(8,128)(2,1)}), bf16[32,136,128]{2,1,0:T(8,128)(2,1)S(1)}, u32[]{:S(2)}, u32[]{:S(2)}) async-start(bf16[32,136,128]{2,1,0:T(8,128)(2,1)} %fusion.21), calls=%async_computation | async-start | bytes 2228224 | tf_op jit(solution)/shard_map/all_to_all | solution.py:70
  25.8 27.3 %all-to-all-done = bf16[32,136,128]{2,1,0:T(8,128)(2,1)S(1)} async-done(((bf16[32,136,128]{2,1,0:T(8,128)(2,1)}), bf16[32,136,128]{2,1,0:T(8,128)(2,1)S(1)}, u32[]{:S(2)}, u32[]{:S(2)}) %all-to-all-start) | async-done | bytes 1114144 | tf_op jit(solution)/shard_map/all_to_all | solution.py:70
  53.2 0.1 fusion.40
  53.2 0.1 reshape.144
  53.3 0.1 broadcast_compare_fusion
  53.4 0.1 fusion.54
  53.5 1.0 copy-done.2
  54.5 1.3 %select_reduce_fusion = f32[1024,64]{0,1:T(8,128)S(1)} fusion(pred[1024,16]{0,1:T(8,128)(4,1)S(1)} %broadcast_compare_fusion, bf16[1024,128]{1,0:T(8,128)(2,1)S(1)} %bitcast.51, bf16[1024,128]{1,0:T(8,128)(2,1)S(1)} %bitcast.52, bf16[1024,128]{1,0:T(8,128)(2,1)S(1)} %bitcast.53, bf16[1024,128]{1,0:T(8,128)(2,1)S(1)} %bitcast.50, ...), kind=kOutput, calls=%fused_computation | convolution fusion | flops 1079967744 | bytes 2375680 | tf_op jit(solution)/shard_map/dot_general | solution.py:86
  55.8 0.2 copy.14
  56.0 0.1 reshape.141
  56.2 23.4 %all_to_all.20 = f32[16,8,512]{2,1,0:T(8,128)S(1)} all-to-all(f32[16,8,512]{2,1,0:T(8,128)S(1)} %reshape.141), channel_id=1, replica_groups=mesh['wide'=32,'tensor'=16] {'tensor'}, dimensions={0} | all-to-all | bytes 524288 | tf_op jit(solution)/shard_map/all_to_all | solution.py:92
  79.6 0.7 broadcast_in_dim.58
  80.2 3.4 %all-to-all-start.2 = ((bf16[16,16,256]{2,1,0:T(8,128)(2,1)}), bf16[16,16,256]{2,1,0:T(8,128)(2,1)S(1)}, u32[]{:S(2)}, u32[]{:S(2)}) async-start(bf16[16,16,256]{2,1,0:T(8,128)(2,1)} %broadcast_in_dim.58), calls=%async_computation.2 | async-start | bytes 262144 | tf_op jit(solution)/shard_map/all_to_all | solution.py:96
  83.7 0.0 copy-start.3
  83.7 0.0 all-gather.2.cloned.1.call-done
  83.7 5.7 %fusion.55 = f32[512,128]{1,0:T(8,128)S(1)} fusion(bf16[512,8192]{1,0:T(8,128)(2,1)} %all-gather.2.cloned.1.call-done, bf16[8192,128]{1,0:T(8,128)(2,1)S(1)} %copy-done), kind=kOutput, calls=%fused_computation.75 | convolution fusion | flops 1073741824 | bytes 10747904 | tf_op jit(solution)/shard_map/dot_general | solution.py:28
  89.5 0.6 slice.45
  90.8 1.4 %all-to-all-done.2 = bf16[16,16,256]{2,1,0:T(8,128)(2,1)S(1)} async-done(((bf16[16,16,256]{2,1,0:T(8,128)(2,1)}), bf16[16,16,256]{2,1,0:T(8,128)(2,1)S(1)}, u32[]{:S(2)}, u32[]{:S(2)}) %all-to-all-start.2) | async-done | bytes 131104 | tf_op jit(solution)/shard_map/all_to_all | solution.py:96
  92.1 0.2 add.55
  92.3 0.1 copy.15
  92.5 0.8 fusion.15
  93.2 18.7 %all_to_all.21 = bf16[32,32,128]{2,1,0:T(8,128)(2,1)S(1)} all-to-all(bf16[32,32,128]{2,1,0:T(8,128)(2,1)S(1)} %bitcast.49), channel_id=1, replica_groups=mesh['wide'=32,'tensor'=16] {'wide'}, dimensions={0} | all-to-all | bytes 524288 | tf_op jit(solution)/shard_map/all_to_all | solution.py:108
  111.9 1.4 %fusion.19 = bf16[512,128]{1,0:T(8,128)(2,1)} fusion(f32[512,128]{1,0:T(8,128)S(1)} %fusion.55, bf16[1024,128]{1,0:T(8,128)(2,1)S(1)} %bitcast.48, s32[512]{0:T(512)S(1)} %convert_add_fusion), kind=kOutput, calls=%fused_computation.16 | convolution fusion | flops 134873088 | bytes 657408 | tf_op jit(solution)/shard_map/dot_general | solution.py:112
  (18 shorter events, 0.2 us)
Async XLA Ops:
  6.5 77.2 %copy-start = (bf16[8192,128]{1,0:T(8,128)(2,1)S(1)}, bf16[8192,128]{1,0:T(8,128)(2,1)}, u32[]{:S(2)}) copy-start(bf16[8192,128]{1,0:T(8,128)(2,1)} %param.7) | copy-start | bytes 6291460
  6.5 3.6 %copy-start.1 = (bf16[512,512]{1,0:T(8,128)(2,1)S(1)}, bf16[512,512]{1,0:T(8,128)(2,1)}, u32[]{:S(2)}) copy-start(bf16[512,512]{1,0:T(8,128)(2,1)} %param.6) | copy-start | bytes 1572868
  6.5 77.2 %all-gather.2.cloned.1.call-start = ((), (), s32[]{:S(2)}) async-start(), calls=%async_computation.4 | async-start | bytes 8912896 | tf_op jit(solution)/shard_map/all_gather | solution.py:27
  12.1 41.1 %all-to-all-start = ((bf16[32,136,128]{2,1,0:T(8,128)(2,1)}), bf16[32,136,128]{2,1,0:T(8,128)(2,1)S(1)}, u32[]{:S(2)}, u32[]{:S(2)}) async-start(bf16[32,136,128]{2,1,0:T(8,128)(2,1)} %fusion.21), calls=%async_computation | async-start | bytes 2228224 | tf_op jit(solution)/shard_map/all_to_all | solution.py:70
  53.3 1.2 %copy-start.2 = (bf16[512,16,64]{0,2,1:T(8,128)(2,1)S(1)}, bf16[512,16,64]{0,2,1:T(8,128)(2,1)}, u32[]{:S(2)}) copy-start(bf16[512,16,64]{0,2,1:T(8,128)(2,1)} %param.8) | copy-start | bytes 3145732
  80.2 11.9 %all-to-all-start.2 = ((bf16[16,16,256]{2,1,0:T(8,128)(2,1)}), bf16[16,16,256]{2,1,0:T(8,128)(2,1)S(1)}, u32[]{:S(2)}, u32[]{:S(2)}) async-start(bf16[16,16,256]{2,1,0:T(8,128)(2,1)} %broadcast_in_dim.58), calls=%async_computation.2 | async-start | bytes 262144 | tf_op jit(solution)/shard_map/all_to_all | solution.py:96
  83.7 8.8 %copy-start.3 = (bf16[16,64,128]{2,1,0:T(8,128)(2,1)S(1)}, bf16[16,64,128]{2,1,0:T(8,128)(2,1)}, u32[]{:S(2)}) copy-start(bf16[16,64,128]{2,1,0:T(8,128)(2,1)} %param.9) | copy-start | bytes 786436
Sparse Core Ops, SparseCore 0:
  9.5 67.3 all-gather.1

commit v14 on v13

--- a/solution.py
+++ b/solution.py
@@ -104,7 +104,7 @@
     adapter_correction = jnp.dot(
         expanded_rows, up_matrix, preferred_element_type=jnp.float32
     ).astype(jnp.bfloat16)
-    adapter_correction = adapter_correction.reshape(wide_count, capacity, column_portion)
+    adapter_correction = adapter_correction.reshape(wide_count, capacity // 2, 2 * column_portion)
     returned_rows = lax.all_to_all(
         adapter_correction, "wide", split_axis=0, concat_axis=0, tiled=True
     )

time: 121 us -> 121 us (level)
  no operation moved by 1% of the time
where the time goes in v14:
time: 121 us; the launch traced here: 120 us
  blocking collectives  42 us (35%)
  waiting for transfers between devices  29.4 us (24%)
  starting transfers between devices  17.1 us (14%)
  between operations  14.3 us (12%)
  matrix products  11.9 us (10%)
  local copies, waits for them, and re-layouts  3.41 us (3%)
  other arithmetic  2.17 us (2%)
    all_to_all x1, waiting for transfers between devices, body(): lax.all_to_all(send_block, 'wide', split_axis=0, concat_axis=0, tiled=True)  27.3 us
    all_to_all x1, blocking collectives, body(): lax.all_to_all(slot_blocks, 'tensor', split_axis=0, concat_axis=0, tiled=...  23.4 us
    all_to_all x1, blocking collectives, body(): lax.all_to_all(adapter_correction, 'wide', split_axis=0, concat_axis=0, t...  18.7 us
    all_to_all x1, starting transfers between devices, body(): lax.all_to_all(send_block, 'wide', split_axis=0, concat_axis=0, tiled=True)  13.7 us
    dot_general x1, matrix products, body(): jnp.dot(gathered, key_value_weight, preferred_element_type=jnp.float32)  5.74 us
    all_to_all x1, starting transfers between devices, body(): lax.all_to_all(spread, 'tensor', split_axis=0, concat_axis=0, tiled=True)  3.41 us
  transfers between devices with their start and end apart: 3, of which 2 were waited for; matrix products, arithmetic and copies ran while one was open for 11% of the time, Pallas kernels for 0%

profile of v14, /device:TPU:1, one launch (start us, length us, event | category | flops | bytes accessed | tf_op | source)
XLA Modules:
  0.0 120.3 jit_solution(13964304186043475297)
XLA Ops:
  6.5 0.7 all-gather.2.cloned.1.call-update
  7.3 0.8 fusion.42
  8.0 1.1 fusion.35
  9.1 0.3 fusion.20
  9.4 0.6 fusion.4
  10.1 0.1 convert_element_type.96
  10.2 0.8 fusion.9
  10.9 1.2 fusion.21
  12.1 13.7 %all-to-all-start = ((bf16[32,136,128]{2,1,0:T(8,128)(2,1)}), bf16[32,136,128]{2,1,0:T(8,128)(2,1)S(1)}, u32[]{:S(2)}, u32[]{:S(2)}) async-start(bf16[32,136,128]{2,1,0:T(8,128)(2,1)} %fusion.21), calls=%async_computation | async-start | bytes 2228224 | tf_op jit(solution)/shard_map/all_to_all | solution.py:70
  25.8 27.3 %all-to-all-done = bf16[32,136,128]{2,1,0:T(8,128)(2,1)S(1)} async-done(((bf16[32,136,128]{2,1,0:T(8,128)(2,1)}), bf16[32,136,128]{2,1,0:T(8,128)(2,1)S(1)}, u32[]{:S(2)}, u32[]{:S(2)}) %all-to-all-start) | async-done | bytes 1114144 | tf_op jit(solution)/shard_map/all_to_all | solution.py:70
  53.2 0.1 fusion.40
  53.2 0.1 reshape.144
  53.3 0.1 broadcast_compare_fusion
  53.4 0.1 fusion.54
  53.5 1.0 copy-done.2
  54.5 1.3 %select_reduce_fusion = f32[1024,64]{0,1:T(8,128)S(1)} fusion(pred[1024,16]{0,1:T(8,128)(4,1)S(1)} %broadcast_compare_fusion, bf16[1024,128]{1,0:T(8,128)(2,1)S(1)} %bitcast.47, bf16[1024,128]{1,0:T(8,128)(2,1)S(1)} %bitcast.48, bf16[1024,128]{1,0:T(8,128)(2,1)S(1)} %bitcast.49, bf16[1024,128]{1,0:T(8,128)(2,1)S(1)} %bitcast.46, ...), kind=kOutput, calls=%fused_computation | convolution fusion | flops 1079967744 | bytes 2375680 | tf_op jit(solution)/shard_map/dot_general | solution.py:86
  55.8 0.2 copy.14
  56.0 0.1 reshape.141
  56.2 23.4 %all_to_all.20 = f32[16,8,512]{2,1,0:T(8,128)S(1)} all-to-all(f32[16,8,512]{2,1,0:T(8,128)S(1)} %reshape.141), channel_id=1, replica_groups=mesh['wide'=32,'tensor'=16] {'tensor'}, dimensions={0} | all-to-all | bytes 524288 | tf_op jit(solution)/shard_map/all_to_all | solution.py:92
  79.6 0.7 broadcast_in_dim.58
  80.2 3.4 %all-to-all-start.2 = ((bf16[16,16,256]{2,1,0:T(8,128)(2,1)}), bf16[16,16,256]{2,1,0:T(8,128)(2,1)S(1)}, u32[]{:S(2)}, u32[]{:S(2)}) async-start(bf16[16,16,256]{2,1,0:T(8,128)(2,1)} %broadcast_in_dim.58), calls=%async_computation.2 | async-start | bytes 262144 | tf_op jit(solution)/shard_map/all_to_all | solution.py:96
  83.7 0.0 all-gather.2.cloned.1.call-done
  83.7 5.7 %fusion.55 = f32[512,128]{1,0:T(8,128)S(1)} fusion(bf16[512,8192]{1,0:T(8,128)(2,1)} %all-gather.2.cloned.1.call-done, bf16[8192,128]{1,0:T(8,128)(2,1)S(1)} %copy-done), kind=kOutput, calls=%fused_computation.75 | convolution fusion | flops 1073741824 | bytes 10747904 | tf_op jit(solution)/shard_map/dot_general | solution.py:28
  89.5 0.6 slice.45
  90.8 1.4 %all-to-all-done.2 = bf16[16,16,256]{2,1,0:T(8,128)(2,1)S(1)} async-done(((bf16[16,16,256]{2,1,0:T(8,128)(2,1)}), bf16[16,16,256]{2,1,0:T(8,128)(2,1)S(1)}, u32[]{:S(2)}, u32[]{:S(2)}) %all-to-all-start.2) | async-done | bytes 131104 | tf_op jit(solution)/shard_map/all_to_all | solution.py:96
  92.1 0.2 add.55
  92.3 0.1 copy.15
  92.5 0.8 fusion.15
  93.2 0.1 reshape.142
  93.3 18.7 %all_to_all.21 = bf16[32,16,256]{2,1,0:T(8,128)(2,1)S(1)} all-to-all(bf16[32,16,256]{2,1,0:T(8,128)(2,1)S(1)} %reshape.142), channel_id=1, replica_groups=mesh['wide'=32,'tensor'=16] {'wide'}, dimensions={0} | all-to-all | bytes 524288 | tf_op jit(solution)/shard_map/all_to_all | solution.py:108
  112.0 0.1 reshape.143
  112.1 1.4 %fusion.19 = bf16[512,128]{1,0:T(8,128)(2,1)} fusion(f32[512,128]{1,0:T(8,128)S(1)} %fusion.55, bf16[1024,128]{1,0:T(8,128)(2,1)S(1)} %reshape.143, s32[512]{0:T(512)S(1)} %convert_add_fusion), kind=kOutput, calls=%fused_computation.16 | convolution fusion | flops 134873088 | bytes 657408 | tf_op jit(solution)/shard_map/dot_general | solution.py:112
  (20 shorter events, 0.2 us)
Async XLA Ops:
  6.5 77.2 %copy-start = (bf16[8192,128]{1,0:T(8,128)(2,1)S(1)}, bf16[8192,128]{1,0:T(8,128)(2,1)}, u32[]{:S(2)}) copy-start(bf16[8192,128]{1,0:T(8,128)(2,1)} %param.7) | copy-start | bytes 6291460
  6.5 3.6 %copy-start.1 = (bf16[512,512]{1,0:T(8,128)(2,1)S(1)}, bf16[512,512]{1,0:T(8,128)(2,1)}, u32[]{:S(2)}) copy-start(bf16[512,512]{1,0:T(8,128)(2,1)} %param.6) | copy-start | bytes 1572868
  6.5 77.2 %all-gather.2.cloned.1.call-start = ((), (), s32[]{:S(2)}) async-start(), calls=%async_computation.4 | async-start | bytes 8912896 | tf_op jit(solution)/shard_map/all_gather | solution.py:27
  12.1 41.1 %all-to-all-start = ((bf16[32,136,128]{2,1,0:T(8,128)(2,1)}), bf16[32,136,128]{2,1,0:T(8,128)(2,1)S(1)}, u32[]{:S(2)}, u32[]{:S(2)}) async-start(bf16[32,136,128]{2,1,0:T(8,128)(2,1)} %fusion.21), calls=%async_computation | async-start | bytes 2228224 | tf_op jit(solution)/shard_map/all_to_all | solution.py:70
  53.3 1.2 %copy-start.2 = (bf16[512,16,64]{0,2,1:T(8,128)(2,1)S(1)}, bf16[512,16,64]{0,2,1:T(8,128)(2,1)}, u32[]{:S(2)}) copy-start(bf16[512,16,64]{0,2,1:T(8,128)(2,1)} %param.8) | copy-start | bytes 3145732
  80.2 11.9 %all-to-all-start.2 = ((bf16[16,16,256]{2,1,0:T(8,128)(2,1)}), bf16[16,16,256]{2,1,0:T(8,128)(2,1)S(1)}, u32[]{:S(2)}, u32[]{:S(2)}) async-start(bf16[16,16,256]{2,1,0:T(8,128)(2,1)} %broadcast_in_dim.58), calls=%async_computation.2 | async-start | bytes 262144 | tf_op jit(solution)/shard_map/all_to_all | solution.py:96
  83.7 8.8 %copy-start.3 = (bf16[16,64,128]{2,1,0:T(8,128)(2,1)S(1)}, bf16[16,64,128]{2,1,0:T(8,128)(2,1)}, u32[]{:S(2)}) copy-start(bf16[16,64,128]{2,1,0:T(8,128)(2,1)} %param.9) | copy-start | bytes 786436
Sparse Core Ops, SparseCore 0:
  9.5 67.3 all-gather.1

commit v15 on v13

--- a/solution.py
+++ b/solution.py
@@ -87,7 +87,7 @@
     all_ranks = all_ranks.reshape(slot_count, present_adapters, rank_dimension)
     partial_value = jnp.sum(jnp.where(selected, all_ranks, 0.0), axis=1)
     block_rows = slot_count // tensor_count
-    dense_shape = (tensor_count, 8, block_rows * rank_dimension // 8)
+    dense_shape = (tensor_count, block_rows * rank_dimension // 128, 128)
     slot_blocks = partial_value.reshape(dense_shape)
     gathered_blocks = lax.all_to_all(slot_blocks, "tensor", split_axis=0, concat_axis=0, tiled=True)
     own_sum = jnp.sum(gathered_blocks, axis=0).astype(jnp.bfloat16)

time: 121 us -> 121 us (level)
  no operation moved by 1% of the time
where the time goes in v15:
time: 121 us; the launch traced here: 120 us
  blocking collectives  42 us (35%)
  waiting for transfers between devices  29.4 us (24%)
  starting transfers between devices  17.1 us (14%)
  between operations  14.3 us (12%)
  matrix products  11.9 us (10%)
  local copies, waits for them, and re-layouts  3.23 us (3%)
  other arithmetic  2.17 us (2%)
    all_to_all x1, waiting for transfers between devices, body(): lax.all_to_all(send_block, 'wide', split_axis=0, concat_axis=0, tiled=True)  27.3 us
    all_to_all x1, blocking collectives, body(): lax.all_to_all(slot_blocks, 'tensor', split_axis=0, concat_axis=0, tiled=...  23.4 us
    all_to_all x1, blocking collectives, body(): lax.all_to_all(adapter_correction, 'wide', split_axis=0, concat_axis=0, t...  18.7 us
    all_to_all x1, starting transfers between devices, body(): lax.all_to_all(send_block, 'wide', split_axis=0, concat_axis=0, tiled=True)  13.7 us
    dot_general x1, matrix products, body(): jnp.dot(gathered, key_value_weight, preferred_element_type=jnp.float32)  5.74 us
    all_to_all x1, starting transfers between devices, body(): lax.all_to_all(spread, 'tensor', split_axis=0, concat_axis=0, tiled=True)  3.41 us
  transfers between devices with their start and end apart: 3, of which 2 were waited for; matrix products, arithmetic and copies ran while one was open for 11% of the time, Pallas kernels for 0%

profile of v15, /device:TPU:1, one launch (start us, length us, event | category | flops | bytes accessed | tf_op | source)
XLA Modules:
  0.0 120.1 jit_solution(7140281131898327111)
XLA Ops:
  6.5 0.7 all-gather.2.cloned.1.call-update
  7.3 0.8 fusion.42
  8.0 1.1 fusion.35
  9.1 0.3 fusion.20
  9.4 0.6 fusion.4
  10.1 0.1 convert_element_type.96
  10.2 0.8 fusion.9
  10.9 1.2 fusion.21
  12.1 13.7 %all-to-all-start = ((bf16[32,136,128]{2,1,0:T(8,128)(2,1)}), bf16[32,136,128]{2,1,0:T(8,128)(2,1)S(1)}, u32[]{:S(2)}, u32[]{:S(2)}) async-start(bf16[32,136,128]{2,1,0:T(8,128)(2,1)} %fusion.21), calls=%async_computation | async-start | bytes 2228224 | tf_op jit(solution)/shard_map/all_to_all | solution.py:70
  25.8 27.3 %all-to-all-done = bf16[32,136,128]{2,1,0:T(8,128)(2,1)S(1)} async-done(((bf16[32,136,128]{2,1,0:T(8,128)(2,1)}), bf16[32,136,128]{2,1,0:T(8,128)(2,1)S(1)}, u32[]{:S(2)}, u32[]{:S(2)}) %all-to-all-start) | async-done | bytes 1114144 | tf_op jit(solution)/shard_map/all_to_all | solution.py:70
  53.2 0.1 fusion.40
  53.2 0.1 reshape.144
  53.3 0.1 broadcast_compare_fusion
  53.4 0.1 fusion.54
  53.5 1.0 copy-done.2
  54.5 1.3 %select_reduce_fusion = f32[1024,64]{0,1:T(8,128)S(1)} fusion(pred[1024,16]{0,1:T(8,128)(4,1)S(1)} %broadcast_compare_fusion, bf16[1024,128]{1,0:T(8,128)(2,1)S(1)} %bitcast.51, bf16[1024,128]{1,0:T(8,128)(2,1)S(1)} %bitcast.52, bf16[1024,128]{1,0:T(8,128)(2,1)S(1)} %bitcast.53, bf16[1024,128]{1,0:T(8,128)(2,1)S(1)} %bitcast.50, ...), kind=kOutput, calls=%fused_computation | convolution fusion | flops 1079967744 | bytes 2375680 | tf_op jit(solution)/shard_map/dot_general | solution.py:86
  55.8 0.2 copy.14
  56.0 0.1 reshape.141
  56.2 23.4 %all_to_all.20 = f32[16,32,128]{2,1,0:T(8,128)S(1)} all-to-all(f32[16,32,128]{2,1,0:T(8,128)S(1)} %reshape.141), channel_id=1, replica_groups=mesh['wide'=32,'tensor'=16] {'tensor'}, dimensions={0} | all-to-all | bytes 524288 | tf_op jit(solution)/shard_map/all_to_all | solution.py:92
  79.6 0.7 broadcast_in_dim.58
  80.2 3.4 %all-to-all-start.2 = ((bf16[16,16,256]{2,1,0:T(8,128)(2,1)}), bf16[16,16,256]{2,1,0:T(8,128)(2,1)S(1)}, u32[]{:S(2)}, u32[]{:S(2)}) async-start(bf16[16,16,256]{2,1,0:T(8,128)(2,1)} %broadcast_in_dim.58), calls=%async_computation.2 | async-start | bytes 262144 | tf_op jit(solution)/shard_map/all_to_all | solution.py:96
  83.7 0.0 copy-start.3
  83.7 0.0 all-gather.2.cloned.1.call-done
  83.7 0.0 copy-done
  83.7 5.7 %fusion.55 = f32[512,128]{1,0:T(8,128)S(1)} fusion(bf16[512,8192]{1,0:T(8,128)(2,1)} %all-gather.2.cloned.1.call-done, bf16[8192,128]{1,0:T(8,128)(2,1)S(1)} %copy-done), kind=kOutput, calls=%fused_computation.75 | convolution fusion | flops 1073741824 | bytes 10747904 | tf_op jit(solution)/shard_map/dot_general | solution.py:28
  89.5 0.6 slice.45
  90.8 1.4 %all-to-all-done.2 = bf16[16,16,256]{2,1,0:T(8,128)(2,1)S(1)} async-done(((bf16[16,16,256]{2,1,0:T(8,128)(2,1)}), bf16[16,16,256]{2,1,0:T(8,128)(2,1)S(1)}, u32[]{:S(2)}, u32[]{:S(2)}) %all-to-all-start.2) | async-done | bytes 131104 | tf_op jit(solution)/shard_map/all_to_all | solution.py:96
  92.1 0.2 add.55
  92.3 0.1 copy.15
  92.5 0.8 fusion.15
  93.2 18.7 %all_to_all.21 = bf16[32,32,128]{2,1,0:T(8,128)(2,1)S(1)} all-to-all(bf16[32,32,128]{2,1,0:T(8,128)(2,1)S(1)} %bitcast.49), channel_id=1, replica_groups=mesh['wide'=32,'tensor'=16] {'wide'}, dimensions={0} | all-to-all | bytes 524288 | tf_op jit(solution)/shard_map/all_to_all | solution.py:108
  111.9 1.4 %fusion.19 = bf16[512,128]{1,0:T(8,128)(2,1)} fusion(f32[512,128]{1,0:T(8,128)S(1)} %fusion.55, bf16[1024,128]{1,0:T(8,128)(2,1)S(1)} %bitcast.48, s32[512]{0:T(512)S(1)} %convert_add_fusion), kind=kOutput, calls=%fused_computation.16 | convolution fusion | flops 134873088 | bytes 657408 | tf_op jit(solution)/shard_map/dot_general | solution.py:112
  (18 shorter events, 0.2 us)
Async XLA Ops:
  6.5 77.2 %copy-start = (bf16[8192,128]{1,0:T(8,128)(2,1)S(1)}, bf16[8192,128]{1,0:T(8,128)(2,1)}, u32[]{:S(2)}) copy-start(bf16[8192,128]{1,0:T(8,128)(2,1)} %param.7) | copy-start | bytes 6291460
  6.5 3.6 %copy-start.1 = (bf16[512,512]{1,0:T(8,128)(2,1)S(1)}, bf16[512,512]{1,0:T(8,128)(2,1)}, u32[]{:S(2)}) copy-start(bf16[512,512]{1,0:T(8,128)(2,1)} %param.6) | copy-start | bytes 1572868
  6.5 77.2 %all-gather.2.cloned.1.call-start = ((), (), s32[]{:S(2)}) async-start(), calls=%async_computation.4 | async-start | bytes 8912896 | tf_op jit(solution)/shard_map/all_gather | solution.py:27
  12.1 41.1 %all-to-all-start = ((bf16[32,136,128]{2,1,0:T(8,128)(2,1)}), bf16[32,136,128]{2,1,0:T(8,128)(2,1)S(1)}, u32[]{:S(2)}, u32[]{:S(2)}) async-start(bf16[32,136,128]{2,1,0:T(8,128)(2,1)} %fusion.21), calls=%async_computation | async-start | bytes 2228224 | tf_op jit(solution)/shard_map/all_to_all | solution.py:70
  53.3 1.2 %copy-start.2 = (bf16[512,16,64]{0,2,1:T(8,128)(2,1)S(1)}, bf16[512,16,64]{0,2,1:T(8,128)(2,1)}, u32[]{:S(2)}) copy-start(bf16[512,16,64]{0,2,1:T(8,128)(2,1)} %param.8) | copy-start | bytes 3145732
  80.2 11.9 %all-to-all-start.2 = ((bf16[16,16,256]{2,1,0:T(8,128)(2,1)}), bf16[16,16,256]{2,1,0:T(8,128)(2,1)S(1)}, u32[]{:S(2)}, u32[]{:S(2)}) async-start(bf16[16,16,256]{2,1,0:T(8,128)(2,1)} %broadcast_in_dim.58), calls=%async_computation.2 | async-start | bytes 262144 | tf_op jit(solution)/shard_map/all_to_all | solution.py:96
  83.7 8.8 %copy-start.3 = (bf16[16,64,128]{2,1,0:T(8,128)(2,1)S(1)}, bf16[16,64,128]{2,1,0:T(8,128)(2,1)}, u32[]{:S(2)}) copy-start(bf16[16,64,128]{2,1,0:T(8,128)(2,1)} %param.9) | copy-start | bytes 786436
Sparse Core Ops, SparseCore 0:
  9.5 67.3 all-gather.1

commit v16 on v13

--- a/solution.py
+++ b/solution.py
@@ -48,9 +48,11 @@
     rank_in_owner = jnp.sum(earlier * owner_onehot, axis=1).astype(jnp.int32)
     destination = owner_index * capacity + rank_in_owner
 
-    placement = (
-        jnp.arange(slot_count, dtype=jnp.int32)[:, None] == destination[None, :]
-    ).astype(jnp.bfloat16)
+    placement = lax.optimization_barrier(
+        (jnp.arange(slot_count, dtype=jnp.int32)[:, None] == destination[None, :]).astype(
+            jnp.bfloat16
+        )
+    )
 
     lane_tiles = feature_portion // lane
     local_code = jnp.broadcast_to(

time: 121 us -> 126 us (1.041)
  local copies, waits for them, and re-layouts: 3.23 us -> 5.64 us
  other arithmetic: 2.17 us -> 4.2 us
  matrix products: 11.9 us -> 13.5 us
    all_to_all x1, blocking collectives: 23.4 us -> 21.7 us  [body(): lax.all_to_all(slot_blocks, 'tensor', split_axis=0, concat_axis=0, tiled=...]
    slice x1, local copies, waits for them, and re-layouts: 0.08 us -> 1.36 us  [body(): got_block[:, tile * capacity:(tile + 1) * capacity, :]]
  transfers between devices with their start and end apart: 3 -> 3, of which waited for: 2 -> 2; matrix products, arithmetic and copies ran while one was open for 11% -> 16% of each run, Pallas kernels for 0% -> 0%
where the time goes in v16:
time: 126 us; the launch traced here: 125 us
  blocking collectives  40.9 us (32%)
  waiting for transfers between devices  29.4 us (23%)
  starting transfers between devices  17.2 us (14%)
  between operations  14.2 us (11%)
  matrix products  13.5 us (11%)
  local copies, waits for them, and re-layouts  5.64 us (4%)
  other arithmetic  4.2 us (3%)
    all_to_all x1, waiting for transfers between devices, body(): lax.all_to_all(send_block, 'wide', split_axis=0, concat_axis=0, tiled=True)  27.3 us
    all_to_all x1, blocking collectives, body(): lax.all_to_all(slot_blocks, 'tensor', split_axis=0, concat_axis=0, tiled=...  21.7 us
    all_to_all x1, blocking collectives, body(): lax.all_to_all(adapter_correction, 'wide', split_axis=0, concat_axis=0, t...  19.2 us
    all_to_all x1, starting transfers between devices, body(): lax.all_to_all(send_block, 'wide', split_axis=0, concat_axis=0, tiled=True)  13.8 us
    dot_general x1, matrix products, body(): jnp.dot(gathered, key_value_weight, preferred_element_type=jnp.float32)  5.7 us
    all_to_all x1, starting transfers between devices, body(): lax.all_to_all(spread, 'tensor', split_axis=0, concat_axis=0, tiled=True)  3.41 us
  transfers between devices with their start and end apart: 3, of which 2 were waited for; matrix products, arithmetic and copies ran while one was open for 16% of the time, Pallas kernels for 0%

profile of v16, /device:TPU:1, one launch (start us, length us, event | category | flops | bytes accessed | tf_op | source)
XLA Modules:
  0.0 125.1 jit_solution(12547788311815755686)
XLA Ops:
  6.5 0.7 all-gather.2.cloned.1.call-update
  7.3 0.7 fusion.31
  8.0 1.1 fusion.23
  9.0 0.3 fusion.12
  9.3 0.4 fusion.3
  9.8 0.5 fusion.26
  10.4 0.1 convert_element_type.99
  10.5 1.7 %convolution_convert_fusion = bf16[32,32,4,128]{3,1,2,0:T(8,128)(2,1)S(1)} fusion(bf16[32,32,512,1]{2,1,3,0:T(8,128)(2,1)S(1)} %bitcast.48, bf16[512,512]{1,0:T(8,128)(2,1)} %param.6), kind=kOutput, calls=%fused_computation.8 | convolution fusion | flops 537395200 | bytes 2621440 | tf_op jit(solution)/shard_map/dcr,rjl->djcl/dot_general | solution.py:63
  12.2 1.1 fusion.13
  13.3 13.8 %all-to-all-start = ((bf16[32,136,128]{2,1,0:T(8,128)(2,1)}), bf16[32,136,128]{2,1,0:T(8,128)(2,1)}, u32[]{:S(2)}, u32[]{:S(2)}) async-start(bf16[32,136,128]{2,1,0:T(8,128)(2,1)} %fusion.13), calls=%async_computation | async-start | bytes 2228224 | tf_op jit(solution)/shard_map/all_to_all | solution.py:72
  27.1 27.3 %all-to-all-done = bf16[32,136,128]{2,1,0:T(8,128)(2,1)} async-done(((bf16[32,136,128]{2,1,0:T(8,128)(2,1)}), bf16[32,136,128]{2,1,0:T(8,128)(2,1)}, u32[]{:S(2)}, u32[]{:S(2)}) %all-to-all-start) | async-done | bytes 1114144 | tf_op jit(solution)/shard_map/all_to_all | solution.py:72
  54.5 0.9 fusion.29
  55.4 0.1 reshape.130
  55.5 0.1 broadcast_compare_fusion
  55.5 1.4 %fusion.43 = (bf16[32,32,128]{2,1,0:T(8,128)(2,1)S(1)}, bf16[32,32,128]{2,1,0:T(8,128)(2,1)S(1)}, bf16[32,32,128]{2,1,0:T(8,128)(2,1)S(1)}, bf16[32,32,128]{2,1,0:T(8,128)(2,1)S(1)}) fusion(bf16[32,136,128]{2,1,0:T(8,128)(2,1)} %all-to-all-done), kind=kLoop, calls=%fused_computation.66 | loop fusion | bytes 2097152 | tf_op jit(solution)/shard_map/slice | solution.py:75
  56.9 0.1 copy-done.3
  57.0 1.3 %select_reduce_fusion = f32[1024,64]{0,1:T(8,128)S(1)} fusion(pred[1024,16]{0,1:T(8,128)(4,1)S(1)} %broadcast_compare_fusion, bf16[1024,128]{1,0:T(8,128)(2,1)S(1)} %bitcast.53, bf16[1024,128]{1,0:T(8,128)(2,1)S(1)} %bitcast.54, bf16[1024,128]{1,0:T(8,128)(2,1)S(1)} %bitcast.55, bf16[1024,128]{1,0:T(8,128)(2,1)S(1)} %bitcast.52, ...), kind=kOutput, calls=%fused_computation | convolution fusion | flops 1079967744 | bytes 2375680 | tf_op jit(solution)/shard_map/dot_general | solution.py:88
  58.3 1.1 copy.14
  59.4 1.3 %reshape.127 = f32[16,8,512]{2,1,0:T(8,128)S(1)} reshape(f32[1024,64]{1,0:T(8,128)} %copy.14) | data formatting | bytes 524288 | tf_op jit(solution)/shard_map/reshape | solution.py:93
  60.6 21.7 %all_to_all.20 = f32[16,8,512]{2,1,0:T(8,128)} all-to-all(f32[16,8,512]{2,1,0:T(8,128)S(1)} %reshape.127), channel_id=1, replica_groups=mesh['wide'=32,'tensor'=16] {'tensor'}, dimensions={0} | all-to-all | bytes 524288 | tf_op jit(solution)/shard_map/all_to_all | solution.py:94
  82.4 1.0 reduce_sum.29
  83.3 0.7 broadcast_in_dim.58
  84.0 3.4 %all-to-all-start.2 = ((bf16[16,16,256]{2,1,0:T(8,128)(2,1)}), bf16[16,16,256]{2,1,0:T(8,128)(2,1)S(1)}, u32[]{:S(2)}, u32[]{:S(2)}) async-start(bf16[16,16,256]{2,1,0:T(8,128)(2,1)} %broadcast_in_dim.58), calls=%async_computation.2 | async-start | bytes 262144 | tf_op jit(solution)/shard_map/all_to_all | solution.py:98
  87.5 5.7 %fusion.44 = f32[512,128]{1,0:T(8,128)S(1)} fusion(bf16[512,8192]{1,0:T(8,128)(2,1)} %all-gather.2.cloned.1.call-done, bf16[8192,128]{1,0:T(8,128)(2,1)S(1)} %copy-done), kind=kOutput, calls=%fused_computation.67 | convolution fusion | flops 1073741824 | bytes 10747904 | tf_op jit(solution)/shard_map/dot_general | solution.py:28
  93.2 0.6 slice.45
  93.8 0.1 copy-done.1
  94.5 1.3 %all-to-all-done.2 = bf16[16,16,256]{2,1,0:T(8,128)(2,1)S(1)} async-done(((bf16[16,16,256]{2,1,0:T(8,128)(2,1)}), bf16[16,16,256]{2,1,0:T(8,128)(2,1)S(1)}, u32[]{:S(2)}, u32[]{:S(2)}) %all-to-all-start.2) | async-done | bytes 131104 | tf_op jit(solution)/shard_map/all_to_all | solution.py:98
  95.8 0.2 add.51
  96.0 0.1 copy.15
  96.1 1.8 %fusion.8 = bf16[1024,128]{1,0:T(8,128)(2,1)S(1)} fusion(bf16[16,64,128]{2,1,0:T(8,128)(2,1)} %param.9, pred[1024,16]{0,1:T(8,128)(4,1)S(1)} %broadcast_compare_fusion, bf16[1024,64]{0,1:T(8,128)(2,1)S(1)} %copy.15), kind=kOutput, calls=%fused_computation.10 | convolution fusion | flops 269615104 | bytes 671744 | tf_op jit(solution)/shard_map/dot_general | solution.py:106
  97.9 19.2 %all_to_all.21 = bf16[32,32,128]{2,1,0:T(8,128)(2,1)S(1)} all-to-all(bf16[32,32,128]{2,1,0:T(8,128)(2,1)S(1)} %bitcast.51), channel_id=1, replica_groups=mesh['wide'=32,'tensor'=16] {'wide'}, dimensions={0} | all-to-all | bytes 524288 | tf_op jit(solution)/shard_map/all_to_all | solution.py:110
  117.1 1.1 fusion.11
  (18 shorter events, 0.1 us)
Async XLA Ops:
  6.5 80.9 %copy-start = (bf16[8192,128]{1,0:T(8,128)(2,1)S(1)}, bf16[8192,128]{1,0:T(8,128)(2,1)}, u32[]{:S(2)}) copy-start(bf16[8192,128]{1,0:T(8,128)(2,1)} %param.7) | copy-start | bytes 6291460
  6.5 80.9 %all-gather.2.cloned.1.call-start = ((), (), s32[]{:S(2)}) async-start(), calls=%async_computation.4 | async-start | bytes 8912896 | tf_op jit(solution)/shard_map/all_gather | solution.py:27
  13.3 41.2 %all-to-all-start = ((bf16[32,136,128]{2,1,0:T(8,128)(2,1)}), bf16[32,136,128]{2,1,0:T(8,128)(2,1)}, u32[]{:S(2)}, u32[]{:S(2)}) async-start(bf16[32,136,128]{2,1,0:T(8,128)(2,1)} %fusion.13), calls=%async_computation | async-start | bytes 2228224 | tf_op jit(solution)/shard_map/all_to_all | solution.py:72
  55.4 1.6 %copy-start.3 = (bf16[512,16,64]{0,2,1:T(8,128)(2,1)S(1)}, bf16[512,16,64]{0,2,1:T(8,128)(2,1)}, u32[]{:S(2)}) copy-start(bf16[512,16,64]{0,2,1:T(8,128)(2,1)} %param.8) | copy-start | bytes 3145732
  84.0 11.8 %all-to-all-start.2 = ((bf16[16,16,256]{2,1,0:T(8,128)(2,1)}), bf16[16,16,256]{2,1,0:T(8,128)(2,1)S(1)}, u32[]{:S(2)}, u32[]{:S(2)}) async-start(bf16[16,16,256]{2,1,0:T(8,128)(2,1)} %broadcast_in_dim.58), calls=%async_computation.2 | async-start | bytes 262144 | tf_op jit(solution)/shard_map/all_to_all | solution.py:98
  93.2 0.7 copy-start.1
  96.1 21.0 %copy-start.2 = (f32[512,128]{1,0:T(8,128)S(1)}, f32[512,128]{1,0:T(8,128)}, u32[]{:S(2)}) copy-start(f32[512,128]{1,0:T(8,128)} %copy-done.1) | copy-start | bytes 786436
Sparse Core Ops, SparseCore 0:
  9.5 64.1 all-gather.1

commit v17 on v13

--- a/solution.py
+++ b/solution.py
@@ -53,17 +53,15 @@
     ).astype(jnp.bfloat16)
 
     lane_tiles = feature_portion // lane
-    local_code = jnp.broadcast_to(
-        (local_index + 1).astype(jnp.bfloat16)[:, None], (row_count, lane)
-    )
     placement_blocks = placement.reshape(wide_count, capacity, row_count)
     token_tiles = tokens.reshape(row_count, lane_tiles, lane)
     placed = jnp.einsum(
         "dcr,rjl->djcl", placement_blocks, token_tiles, preferred_element_type=jnp.float32
     ).astype(jnp.bfloat16)
     pieces = [placed.reshape(wide_count, lane_tiles * capacity, lane)]
-    placed_code = jnp.dot(placement, local_code, preferred_element_type=jnp.float32)
-    slot_code = placed_code[:, 0].astype(jnp.bfloat16).reshape(wide_count, 1, capacity)
+    slot_code = jnp.sum(
+        jnp.where(placement > 0, (local_index + 1)[None, :], 0), axis=1
+    ).astype(jnp.bfloat16).reshape(wide_count, 1, capacity)
     pieces.append(jnp.pad(slot_code, ((0, 0), (0, info_rows - 1), (0, lane - capacity))))
     send_block = jnp.concatenate(pieces, axis=1)
 

time: 121 us -> 121 us (level)
  transfers between devices with their start and end apart: 3 -> 3, of which waited for: 2 -> 2; matrix products, arithmetic and copies ran while one was open for 11% -> 12% of each run, Pallas kernels for 0% -> 0%
where the time goes in v17:
time: 121 us
  blocking collectives  42 us (35%)
  waiting for transfers between devices  29.4 us (24%)
  starting transfers between devices  17.1 us (14%)
  between operations  14.3 us (12%)
  matrix products  12.3 us (10%)
  local copies, waits for them, and re-layouts  3.22 us (3%)
  other arithmetic  2.51 us (2%)
    all_to_all x1, waiting for transfers between devices, body(): lax.all_to_all(send_block, 'wide', split_axis=0, concat_axis=0, tiled=True)  27.3 us
    all_to_all x1, blocking collectives, body(): lax.all_to_all(slot_blocks, 'tensor', split_axis=0, concat_axis=0, tiled=...  22.6 us
    all_to_all x1, blocking collectives, body(): lax.all_to_all(adapter_correction, 'wide', split_axis=0, concat_axis=0, t...  19.5 us
    all_to_all x1, starting transfers between devices, body(): lax.all_to_all(send_block, 'wide', split_axis=0, concat_axis=0, tiled=True)  13.7 us
    dot_general x1, matrix products, body(): jnp.dot(gathered, key_value_weight, preferred_element_type=jnp.float32)  5.74 us
    all_to_all x1, starting transfers between devices, body(): lax.all_to_all(spread, 'tensor', split_axis=0, concat_axis=0, tiled=True)  3.41 us
  transfers between devices with their start and end apart: 3, of which 2 were waited for; matrix products, arithmetic and copies ran while one was open for 12% of the time, Pallas kernels for 0%

profile of v17, /device:TPU:1, one launch (start us, length us, event | category | flops | bytes accessed | tf_op | source)
XLA Modules:
  0.0 120.9 jit_solution(5223123476182406349)
XLA Ops:
  6.5 0.0 copy-start
  6.5 0.7 all-gather.2.cloned.1.call-update
  7.3 0.7 fusion.39
  8.0 1.1 fusion.34
  9.0 0.3 fusion.20
  9.3 0.4 select_reduce_fusion.1
  9.8 0.1 convert_element_type.101
  9.9 1.8 %fusion.9 = bf16[32,32,4,128]{3,1,2,0:T(8,128)(2,1)S(1)} fusion(s32[512]{0:T(512)S(1)} %convert_add_fusion, s32[32,32]{1,0:T(8,128)S(1)} %multiply_add_fusion, bf16[512,512]{1,0:T(8,128)(2,1)} %param.6), kind=kOutput, calls=%fused_computation.13 | convolution fusion | flops 537919488 | bytes 1579008 | tf_op jit(solution)/shard_map/dcr,rjl->djcl/dot_general | solution.py:58
  11.7 1.2 fusion.21
  12.9 13.7 %all-to-all-start = ((bf16[32,136,128]{2,1,0:T(8,128)(2,1)}), bf16[32,136,128]{2,1,0:T(8,128)(2,1)S(1)}, u32[]{:S(2)}, u32[]{:S(2)}) async-start(bf16[32,136,128]{2,1,0:T(8,128)(2,1)} %fusion.21), calls=%async_computation | async-start | bytes 2228224 | tf_op jit(solution)/shard_map/all_to_all | solution.py:68
  26.6 27.3 %all-to-all-done = bf16[32,136,128]{2,1,0:T(8,128)(2,1)S(1)} async-done(((bf16[32,136,128]{2,1,0:T(8,128)(2,1)}), bf16[32,136,128]{2,1,0:T(8,128)(2,1)S(1)}, u32[]{:S(2)}, u32[]{:S(2)}) %all-to-all-start) | async-done | bytes 1114144 | tf_op jit(solution)/shard_map/all_to_all | solution.py:68
  53.9 0.1 fusion.38
  54.0 0.1 reshape.153
  54.1 0.1 broadcast_compare_fusion
  54.2 0.1 fusion.49
  54.3 1.1 copy-done.1
  55.3 1.3 %select_reduce_fusion = f32[1024,64]{0,1:T(8,128)S(1)} fusion(pred[1024,16]{0,1:T(8,128)(4,1)S(1)} %broadcast_compare_fusion, bf16[1024,128]{1,0:T(8,128)(2,1)S(1)} %bitcast.52, bf16[1024,128]{1,0:T(8,128)(2,1)S(1)} %bitcast.53, bf16[1024,128]{1,0:T(8,128)(2,1)S(1)} %bitcast.54, bf16[1024,128]{1,0:T(8,128)(2,1)S(1)} %bitcast.51, ...), kind=kOutput, calls=%fused_computation | convolution fusion | flops 1079967744 | bytes 2375680 | tf_op jit(solution)/shard_map/dot_general | solution.py:84
  56.6 0.2 copy.17
  56.8 0.1 reshape.150
  57.0 22.6 %all_to_all.20 = f32[16,8,512]{2,1,0:T(8,128)S(1)} all-to-all(f32[16,8,512]{2,1,0:T(8,128)S(1)} %reshape.150), channel_id=1, replica_groups=mesh['wide'=32,'tensor'=16] {'tensor'}, dimensions={0} | all-to-all | bytes 524288 | tf_op jit(solution)/shard_map/all_to_all | solution.py:90
  79.6 0.7 broadcast_in_dim.63
  80.2 3.4 %all-to-all-start.2 = ((bf16[16,16,256]{2,1,0:T(8,128)(2,1)}), bf16[16,16,256]{2,1,0:T(8,128)(2,1)S(1)}, u32[]{:S(2)}, u32[]{:S(2)}) async-start(bf16[16,16,256]{2,1,0:T(8,128)(2,1)} %broadcast_in_dim.63), calls=%async_computation.2 | async-start | bytes 262144 | tf_op jit(solution)/shard_map/all_to_all | solution.py:94
  83.7 0.0 copy-start.2
  83.7 0.0 all-gather.2.cloned.1.call-done
  83.7 5.7 %fusion.50 = f32[512,128]{1,0:T(8,128)S(1)} fusion(bf16[512,8192]{1,0:T(8,128)(2,1)} %all-gather.2.cloned.1.call-done, bf16[8192,128]{1,0:T(8,128)(2,1)S(1)} %copy-done), kind=kOutput, calls=%fused_computation.70 | convolution fusion | flops 1073741824 | bytes 10747904 | tf_op jit(solution)/shard_map/dot_general | solution.py:28
  89.5 0.6 slice.39
  90.8 1.4 %all-to-all-done.2 = bf16[16,16,256]{2,1,0:T(8,128)(2,1)S(1)} async-done(((bf16[16,16,256]{2,1,0:T(8,128)(2,1)}), bf16[16,16,256]{2,1,0:T(8,128)(2,1)S(1)}, u32[]{:S(2)}, u32[]{:S(2)}) %all-to-all-start.2) | async-done | bytes 131104 | tf_op jit(solution)/shard_map/all_to_all | solution.py:94
  92.1 0.2 add.62
  92.3 0.1 copy.18
  92.4 0.8 fusion.15
  93.2 19.5 %all_to_all.21 = bf16[32,32,128]{2,1,0:T(8,128)(2,1)S(1)} all-to-all(bf16[32,32,128]{2,1,0:T(8,128)(2,1)S(1)} %bitcast.50), channel_id=1, replica_groups=mesh['wide'=32,'tensor'=16] {'wide'}, dimensions={0} | all-to-all | bytes 524288 | tf_op jit(solution)/shard_map/all_to_all | solution.py:106
  112.7 1.4 %fusion.19 = bf16[512,128]{1,0:T(8,128)(2,1)} fusion(f32[512,128]{1,0:T(8,128)S(1)} %fusion.50, bf16[1024,128]{1,0:T(8,128)(2,1)S(1)} %bitcast.49, s32[512]{0:T(512)S(1)} %convert_add_fusion), kind=kOutput, calls=%fused_computation.17 | convolution fusion | flops 134873088 | bytes 657408 | tf_op jit(solution)/shard_map/dot_general | solution.py:110
  (15 shorter events, 0.1 us)
Async XLA Ops:
  6.5 77.2 %copy-start = (bf16[8192,128]{1,0:T(8,128)(2,1)S(1)}, bf16[8192,128]{1,0:T(8,128)(2,1)}, u32[]{:S(2)}) copy-start(bf16[8192,128]{1,0:T(8,128)(2,1)} %param.7) | copy-start | bytes 6291460
  6.5 77.2 %all-gather.2.cloned.1.call-start = ((), (), s32[]{:S(2)}) async-start(), calls=%async_computation.4 | async-start | bytes 8912896 | tf_op jit(solution)/shard_map/all_gather | solution.py:27
  12.9 41.1 %all-to-all-start = ((bf16[32,136,128]{2,1,0:T(8,128)(2,1)}), bf16[32,136,128]{2,1,0:T(8,128)(2,1)S(1)}, u32[]{:S(2)}, u32[]{:S(2)}) async-start(bf16[32,136,128]{2,1,0:T(8,128)(2,1)} %fusion.21), calls=%async_computation | async-start | bytes 2228224 | tf_op jit(solution)/shard_map/all_to_all | solution.py:68
  54.1 1.2 %copy-start.1 = (bf16[512,16,64]{0,2,1:T(8,128)(2,1)S(1)}, bf16[512,16,64]{0,2,1:T(8,128)(2,1)}, u32[]{:S(2)}) copy-start(bf16[512,16,64]{0,2,1:T(8,128)(2,1)} %param.8) | copy-start | bytes 3145732
  80.2 11.9 %all-to-all-start.2 = ((bf16[16,16,256]{2,1,0:T(8,128)(2,1)}), bf16[16,16,256]{2,1,0:T(8,128)(2,1)S(1)}, u32[]{:S(2)}, u32[]{:S(2)}) async-start(bf16[16,16,256]{2,1,0:T(8,128)(2,1)} %broadcast_in_dim.63), calls=%async_computation.2 | async-start | bytes 262144 | tf_op jit(solution)/shard_map/all_to_all | solution.py:94
  83.7 8.8 %copy-start.2 = (bf16[16,64,128]{2,1,0:T(8,128)(2,1)S(1)}, bf16[16,64,128]{2,1,0:T(8,128)(2,1)}, u32[]{:S(2)}) copy-start(bf16[16,64,128]{2,1,0:T(8,128)(2,1)} %param.9) | copy-start | bytes 786436
Sparse Core Ops, SparseCore 0:
  9.5 65.7 all-gather.1
